TPU v7x, 512 devices: a whole 4x4x16 slice. The times are simulated.
512 devices in a mesh: dp: 32 (over z, core), freq: 16 (over x, y).
Axes of the slice: x: 4, y: 4, z: 16, core: 2. Of those that a mesh axis runs over, the one named last changes fastest.
Arguments:
- output_grad: bfloat16 [1024, 384, 1024], P(('dp', 'freq')), may hold values from -6 to 6
- layer_input: bfloat16 [1024, 384, 1024], P(('dp', 'freq')), may hold values from -6 to 6
- counts: int32 [512], P(('dp', 'freq')), may hold values from 0 to 2, as said below
- bin_order: int32 [64], replicated, may hold values from 0 to 1023, as said below
- inverse_factor: bfloat16 [64, 2, 384, 384], P('freq'), may hold values from -0.10306207 to 0.70406207
Outputs:
- input_spectra_grad: bfloat16 [1024, 128, 384], P(('dp', 'freq'))
- tap_grad: float32 [9, 384, 384], P(None, 'dp', 'freq')
Inputs may be any that keep to these rules, and one draw needn't show every extreme that they name: `counts`: slots at or past a shard's count hold no image; some shard has all 2 slots live and some has none. `bin_order`: entries are distinct bins of the 32 x 32 grid; slot j belongs to freq index j // 4.
All inputs are finite; a program needn't handle non-finite values.
Results may differ from a plain program's by a relative error of at most 0.0071.
Values may be sent and summed in bfloat16 or wider, within the bound.
No kernel may reach another device: no remote copies, remote signals or barrier semaphores. Data moves between devices by JAX's collectives and lax.ppermute only.
A program may use at most 64 MiB of HBM per device.

v0:
```python
import math

import jax
import jax.numpy as jnp
from jax import lax
from jax.sharding import PartitionSpec as P

GRID = 32


def dft_table(bin_order, grid_side):
    pixel_index = jnp.arange(grid_side * grid_side, dtype=jnp.int32)
    row_pos = pixel_index // grid_side
    col_pos = pixel_index % grid_side
    freq_u = bin_order // grid_side
    freq_v = bin_order % grid_side
    phase_turns = (
        row_pos[:, None] * freq_u[None, :] + col_pos[:, None] * freq_v[None, :]
    ) % grid_side
    phase_angle = phase_turns.astype(jnp.float32) * (2.0 * math.pi / grid_side)
    both_parts = jnp.stack([jnp.cos(phase_angle), -jnp.sin(phase_angle)], axis=2) / grid_side
    return both_parts.reshape(grid_side * grid_side, -1).astype(jnp.bfloat16)


def tap_phases(bin_order, grid_side):
    offsets = jnp.arange(9, dtype=jnp.int32)
    shift_y = offsets // 3 - 1
    shift_x = offsets % 3 - 1
    freq_u = bin_order // grid_side
    freq_v = bin_order % grid_side
    phase_turns = (
        freq_u[:, None] * shift_y[None, :] + freq_v[:, None] * shift_x[None, :]
    ) % grid_side
    phase_angle = phase_turns.astype(jnp.float32) * (2.0 * math.pi / grid_side)
    return (jnp.cos(phase_angle), jnp.sin(phase_angle))


def left_product(factor_real, factor_imag, half_real, half_imag):
    full_real = -2.0 * (
        jnp.einsum("bkr,bkc->brc", factor_real, half_real, preferred_element_type=jnp.float32)
        + jnp.einsum("bkr,bkc->brc", factor_imag, half_imag, preferred_element_type=jnp.float32)
    )
    full_imag = -2.0 * (
        jnp.einsum("bkr,bkc->brc", factor_real, half_imag, preferred_element_type=jnp.float32)
        - jnp.einsum("bkr,bkc->brc", factor_imag, half_real, preferred_element_type=jnp.float32)
    )
    return (full_real, full_imag)


def local(output_grad, layer_input, counts, bin_order, inverse_factor):
    slot_count, channels, pixels = output_grad.shape
    freq_devices = lax.axis_size("freq")
    data_devices = lax.axis_size("dp")
    bins_local = inverse_factor.shape[0]
    total_bins = bin_order.shape[0]
    live_mask = (jnp.arange(slot_count, dtype=jnp.int32) < counts[0]).astype(jnp.bfloat16)
    bins_table = dft_table(bin_order, GRID)

    def spectrum(images):
        masked = images * live_mask[:, None, None]
        return jnp.einsum(
            "scp,pk->skc", masked, bins_table, preferred_element_type=jnp.float32
        ).astype(jnp.bfloat16)

    grad_spec = spectrum(output_grad)
    input_spec = spectrum(layer_input)
    grad_recv, input_recv = (
        lax.all_to_all(grad_spec, "freq", split_axis=1, concat_axis=0, tiled=True),
        lax.all_to_all(input_spec, "freq", split_axis=1, concat_axis=0, tiled=True),
    )
    image_rows = grad_recv.shape[0]
    grad_parts = grad_recv.reshape(image_rows, bins_local, 2, channels)
    input_parts = input_recv.reshape(image_rows, bins_local, 2, channels)
    grad_real = grad_parts[:, :, 0]
    grad_imag = grad_parts[:, :, 1]
    input_real = input_parts[:, :, 0]
    input_imag = input_parts[:, :, 1]
    factor_real = inverse_factor[:, 0]
    factor_imag = inverse_factor[:, 1]
    back_real = 2.0 * (
        jnp.einsum("ibr,brc->ibc", grad_real, factor_real, preferred_element_type=jnp.float32)
        + jnp.einsum("ibr,brc->ibc", grad_imag, factor_imag, preferred_element_type=jnp.float32)
    ) - grad_real.astype(jnp.float32)
    back_imag = 2.0 * (
        jnp.einsum("ibr,brc->ibc", grad_imag, factor_real, preferred_element_type=jnp.float32)
        - jnp.einsum("ibr,brc->ibc", grad_real, factor_imag, preferred_element_type=jnp.float32)
    ) - grad_imag.astype(jnp.float32)
    back_both = (
        jnp.stack([back_real, back_imag], axis=2)
        .astype(jnp.bfloat16)
        .reshape(image_rows, 2 * bins_local, channels)
    )
    returned = lax.all_to_all(back_both, "freq", split_axis=0, concat_axis=1, tiled=True)
    gram_scale = 1.0 / math.sqrt(data_devices * freq_devices * slot_count)
    gram_real = (
        jnp.einsum("ibr,ibc->brc", grad_real, input_real, preferred_element_type=jnp.float32)
        + jnp.einsum("ibr,ibc->brc", grad_imag, input_imag, preferred_element_type=jnp.float32)
    ) * gram_scale
    gram_imag = (
        jnp.einsum("ibr,ibc->brc", grad_imag, input_real, preferred_element_type=jnp.float32)
        - jnp.einsum("ibr,ibc->brc", grad_real, input_imag, preferred_element_type=jnp.float32)
    ) * gram_scale
    gram_local = jnp.stack([gram_real, gram_imag], axis=1)
    gram_matrix = lax.psum(gram_local, "dp").astype(jnp.bfloat16)
    summed_real = gram_matrix[:, 0]
    summed_imag = gram_matrix[:, 1]
    half_real = (
        jnp.einsum("brk,bck->brc", summed_real, factor_real, preferred_element_type=jnp.float32)
        + jnp.einsum("brk,bck->brc", summed_imag, factor_imag, preferred_element_type=jnp.float32)
    ).astype(jnp.bfloat16)
    half_imag = (
        jnp.einsum("brk,bck->brc", summed_imag, factor_real, preferred_element_type=jnp.float32)
        - jnp.einsum("brk,bck->brc", summed_real, factor_imag, preferred_element_type=jnp.float32)
    ).astype(jnp.bfloat16)
    row_share = channels // data_devices
    row_start = lax.axis_index("dp") * row_share
    full_real, full_imag = left_product(factor_real, factor_imag, half_real, half_imag)
    skew_real = full_real - jnp.swapaxes(full_real, 1, 2)
    skew_imag = full_imag + jnp.swapaxes(full_imag, 1, 2)
    skew_real = lax.dynamic_slice_in_dim(skew_real, row_start, row_share, 1)
    skew_imag = lax.dynamic_slice_in_dim(skew_imag, row_start, row_share, 1)
    local_bins = lax.dynamic_slice_in_dim(
        bin_order, lax.axis_index("freq") * bins_local, bins_local
    )
    cos_local, sin_local = tap_phases(local_bins, GRID)
    tap_partial = jnp.sum(
        cos_local[:, :, None, None] * skew_real[:, None]
        - sin_local[:, :, None, None] * skew_imag[:, None],
        axis=0,
    )
    tap_partial = tap_partial / math.sqrt(total_bins)
    tap_grad = lax.psum_scatter(tap_partial, "freq", scatter_dimension=2, tiled=True)
    return (returned, tap_grad)


def solution(mesh):
    return jax.shard_map(
        local,
        mesh=mesh,
        in_specs=(
            P(("dp", "freq"), None, None),
            P(("dp", "freq"), None, None),
            P(("dp", "freq")),
            P(),
            P("freq", None, None, None),
        ),
        out_specs=(P(("dp", "freq"), None, None), P(None, "dp", "freq")),
        check_vma=False,
    )
```

profile of v0, /device:TPU:1, one launch (start us, length us, event | category | flops | bytes accessed | tf_op | source)
XLA Modules:
  0.0 309.6 jit_solution(17051504270346240911)
XLA Ops:
  8.0 1.1 fusion.90
  11.8 7.6 %all-to-all-start = ((bf16[2,128,384]{2,0,1:T(2,128)(2,1)}), bf16[2,128,384]{2,0,1:T(2,128)(2,1)S(1)}, u32[]{:S(2)}, u32[]{:S(2)}) async-start(bf16[2,128,384]{2,0,1:T(2,128)(2,1)} %copy.110), calls=%async_computation | async-start | bytes 393216 | tf_op jit(solution)/shard_map/all_to_all | solution.py:68
  19.4 2.3 fusion.30
  22.8 3.5 %all-to-all-done = bf16[2,128,384]{2,0,1:T(2,128)(2,1)S(1)} async-done(((bf16[2,128,384]{2,0,1:T(2,128)(2,1)}), bf16[2,128,384]{2,0,1:T(2,128)(2,1)S(1)}, u32[]{:S(2)}, u32[]{:S(2)}) %all-to-all-start) | async-done | bytes 196640 | tf_op jit(solution)/shard_map/all_to_all | solution.py:68
  26.3 3.5 %all-to-all-start.2 = ((bf16[2,128,384]{2,0,1:T(2,128)(2,1)}), bf16[2,128,384]{2,0,1:T(2,128)(2,1)S(1)}, u32[]{:S(2)}, u32[]{:S(2)}) async-start(bf16[2,128,384]{2,0,1:T(2,128)(2,1)} %copy.119), calls=%async_computation.2 | async-start | bytes 393216 | tf_op jit(solution)/shard_map/all_to_all | solution.py:69
  30.3 1.0 fusion.8
  31.6 5.2 %all-to-all-done.2 = bf16[2,128,384]{2,0,1:T(2,128)(2,1)S(1)} async-done(((bf16[2,128,384]{2,0,1:T(2,128)(2,1)}), bf16[2,128,384]{2,0,1:T(2,128)(2,1)S(1)}, u32[]{:S(2)}, u32[]{:S(2)}) %all-to-all-start.2) | async-done | bytes 196640 | tf_op jit(solution)/shard_map/all_to_all | solution.py:69
  39.2 2.4 pad_maximum_fusion
  41.7 121.8 %all-reduce.5 = bf16[4,2,384,384]{3,2,0,1:T(8,128)(2,1)} all-reduce(f32[4,2,384,384]{3,2,0,1:T(8,128)} %pad_maximum_fusion), channel_id=1, replica_groups=mesh['dp'=32,'freq'=16] {'dp'}, use_global_device_ids=true, to_apply=%region_0.1 | all-reduce | flops 1179648 | bytes 7077888 | tf_op jit(solution)/shard_map/psum | solution.py:104
  163.5 2.4 fusion.14
  168.7 0.9 subtract_convert_fusion
  171.5 2.4 fusion.16
  173.9 1.0 convolution_subtract_fusion
  174.9 1.4 copy-done.2
  176.3 1.2 constant_dynamic-slice_fusion
  177.4 2.0 copy.143
  179.5 1.0 fusion.91
  181.1 4.0 %add_multiply_fusion = f32[4,384,384]{2,1,0:T(8,128)} fusion(f32[4,384,384]{2,1,0:T(8,128)} %fusion.16, bf16[4,384,384]{2,1,0:T(8,128)(2,1)S(1)} %subtract_convert_fusion, bf16[4,2,384,384]{3,2,1,0:T(8,128)(2,1)S(1)} %copy-done), kind=kOutput, calls=%fused_computation.1 | convolution fusion | flops 454164480 | bytes 7077888 | tf_op jit(solution)/shard_map/bkr,bkc->brc/dot_general | solution.py:41
  185.2 2.1 copy.125
  187.2 0.9 dynamic-slice_subtract_fusion
  190.3 3.5 %all-to-all-start.1 = ((bf16[32,8,384]{2,1,0:T(8,128)(2,1)}), bf16[32,8,384]{2,1,0:T(8,128)(2,1)S(1)}, u32[]{:S(2)}, u32[]{:S(2)}) async-start(bf16[32,8,384]{2,1,0:T(8,128)(2,1)} %copy.117), calls=%async_computation.1 | async-start | bytes 393216 | tf_op jit(solution)/shard_map/all_to_all | solution.py:93
  193.9 1.3 dynamic-slice
  195.8 104.6 %all-reduce.4.cloned.1.call-done = f32[9,12,384]{2,1,0:T(8,128)} async-done(((f32[9,12,384]{2,1,0:T(8,128)}), f32[9,12,384]{2,1,0:T(8,128)}) %all-reduce.4.cloned.1.call-update) | async-done | bytes 165904
  300.4 1.6 constant_dynamic-slice_fusion.1
  (57 shorter events, 15.2 us)
Async XLA Ops:
  7.2 3.0 copy-start.8
  10.9 11.7 %copy-start.7 = (s32[64]{0:T(128)S(1)}, s32[64]{0:T(128)}, u32[]{:S(2)}) copy-start(s32[64]{0:T(128)} %param.8) | copy-start | bytes 772
  11.8 14.5 %all-to-all-start = ((bf16[2,128,384]{2,0,1:T(2,128)(2,1)}), bf16[2,128,384]{2,0,1:T(2,128)(2,1)S(1)}, u32[]{:S(2)}, u32[]{:S(2)}) async-start(bf16[2,128,384]{2,0,1:T(2,128)(2,1)} %copy.110), calls=%async_computation | async-start | bytes 393216 | tf_op jit(solution)/shard_map/all_to_all | solution.py:68
  19.4 10.9 %copy-start = (bf16[4,2,384,384]{3,2,1,0:T(8,128)(2,1)S(1)}, bf16[4,2,384,384]{3,2,1,0:T(8,128)(2,1)}, u32[]{:S(2)}) copy-start(bf16[4,2,384,384]{3,2,1,0:T(8,128)(2,1)} %param.9) | copy-start | bytes 7077892
  26.3 10.4 %all-to-all-start.2 = ((bf16[2,128,384]{2,0,1:T(2,128)(2,1)}), bf16[2,128,384]{2,0,1:T(2,128)(2,1)S(1)}, u32[]{:S(2)}, u32[]{:S(2)}) async-start(bf16[2,128,384]{2,0,1:T(2,128)(2,1)} %copy.119), calls=%async_computation.2 | async-start | bytes 393216 | tf_op jit(solution)/shard_map/all_to_all | solution.py:69
  29.9 270.6 %all-reduce.4.cloned.1.call-start = ((), (), s32[]{:S(2)}) async-start(), calls=%async_computation.3 | async-start | bytes 442368
  163.5 2.4 copy-start.1
  165.8 0.9 copy-start.3
  174.9 1.4 copy-start.2
  185.1 3.1 copy-start.6
  185.2 4.4 %copy-start.4 = (bf16[32,4,1,384]{3,0,1,2:T(8,128)(2,1)S(1)}, bf16[32,4,1,384]{3,0,1,2:T(8,128)(2,1)}, u32[]{:S(2)}) copy-start(bf16[32,4,1,384]{3,0,1,2:T(8,128)(2,1)} %fusion.69) | copy-start | bytes 294916
  185.2 4.4 %copy-start.5 = (bf16[32,4,1,384]{3,0,1,2:T(8,128)(2,1)S(1)}, bf16[32,4,1,384]{3,0,1,2:T(8,128)(2,1)}, u32[]{:S(2)}) copy-start(bf16[32,4,1,384]{3,0,1,2:T(8,128)(2,1)} %fusion.66) | copy-start | bytes 294916
  190.3 111.7 %all-to-all-start.1 = ((bf16[32,8,384]{2,1,0:T(8,128)(2,1)}), bf16[32,8,384]{2,1,0:T(8,128)(2,1)S(1)}, u32[]{:S(2)}, u32[]{:S(2)}) async-start(bf16[32,8,384]{2,1,0:T(8,128)(2,1)} %copy.117), calls=%async_computation.1 | async-start | bytes 393216 | tf_op jit(solution)/shard_map/all_to_all | solution.py:93
Sparse Core Ops, SparseCore 0:
  189.6 110.7 all-reduce.3
where the time goes:
time: 311 us; the launch traced here: 310 us
  blocking collectives  122 us (39%)
  waiting for transfers between devices  113 us (36%)
  matrix products  21.7 us (7%)
  between operations  15.7 us (5%)
  local copies, waits for them, and re-layouts  14.7 us (5%)
  starting transfers between devices  14.7 us (5%)
  other arithmetic  7.82 us (3%)
    psum x1, blocking collectives, local(): gram_matrix = lax.psum(gram_local, 'dp').astype(jnp.bfloat16)  122 us
    unnamed x2, waiting for transfers between devices  105 us
    all_to_all x1, starting transfers between devices, local(): lax.all_to_all(grad_spec, 'freq', split_axis=1, concat_axis=0, tiled=True)  7.58 us
    unnamed x21, local copies, waits for them, and re-layouts  6.37 us
  transfers between devices with their start and end apart: 4, of which 3 were waited for; matrix products, arithmetic and copies ran while one was open for 3% of the time, Pallas kernels for 0%

commit v1 on v0

--- a/solution.py
+++ b/solution.py
@@ -129,7 +129,12 @@
         axis=0,
     )
     tap_partial = tap_partial / math.sqrt(total_bins)
-    tap_grad = lax.psum_scatter(tap_partial, "freq", scatter_dimension=2, tiled=True)
+    col_share = channels // freq_devices
+    tap_pieces = jnp.transpose(
+        tap_partial.reshape(tap_partial.shape[0], row_share, freq_devices, col_share), (2, 0, 1, 3)
+    )
+    tap_pieces = lax.all_to_all(tap_pieces, "freq", split_axis=0, concat_axis=0, tiled=True)
+    tap_grad = jnp.sum(tap_pieces, axis=0)
     return (returned, tap_grad)
 
 

time: 311 us -> 213 us (0.68)
  the two profiles are of different devices: /device:TPU:1 before, /device:TPU:2 now
where the time goes in v1:
time: 213 us; the launch traced here: 212 us
  blocking collectives  120 us (56%)
  starting transfers between devices  24.9 us (12%)
  matrix products  22.1 us (10%)
  local copies, waits for them, and re-layouts  18.1 us (8%)
  waiting for transfers between devices  15.3 us (7%)
  other arithmetic  9.87 us (5%)
    psum x1, blocking collectives, local(): gram_matrix = lax.psum(gram_local, 'dp').astype(jnp.bfloat16)  120 us
    all_to_all x1, starting transfers between devices, local(): lax.all_to_all(grad_spec, 'freq', split_axis=1, concat_axis=0, tiled=True)  9.24 us
    unnamed x17, local copies, waits for them, and re-layouts  5.28 us
    all_to_all x1, starting transfers between devices, local(): lax.all_to_all(tap_pieces, 'freq', split_axis=0, concat_axis=0, tiled=True)  5.25 us
    all_to_all x1, starting transfers between devices, local(): lax.all_to_all(input_spec, 'freq', split_axis=1, concat_axis=0, tiled=True)  5.22 us
    all_to_all x1, starting transfers between devices, local(): lax.all_to_all(back_both, 'freq', split_axis=0, concat_axis=1, tiled=True)  5.17 us
    all_to_all x1, waiting for transfers between devices, local(): lax.all_to_all(input_spec, 'freq', split_axis=1, concat_axis=0, tiled=True)  4.91 us
  transfers between devices with their start and end apart: 4, of which 4 were waited for; matrix products, arithmetic and copies ran while one was open for 5% of the time, Pallas kernels for 0%

profile of v1, /device:TPU:2, one launch (start us, length us, event | category | flops | bytes accessed | tf_op | source)
XLA Modules:
  0.0 212.1 jit_solution(3314384072957820823)
XLA Ops:
  1.4 1.1 fusion.90
  5.3 9.2 %all-to-all-start = ((bf16[2,128,384]{2,0,1:T(2,128)(2,1)}), bf16[2,128,384]{2,0,1:T(2,128)(2,1)S(1)}, u32[]{:S(2)}, u32[]{:S(2)}) async-start(bf16[2,128,384]{2,0,1:T(2,128)(2,1)} %copy.132), calls=%async_computation | async-start | bytes 393216 | tf_op jit(solution)/shard_map/all_to_all | solution.py:68
  14.6 2.3 %fusion.30 = bf16[2,128,384]{2,1,0:T(8,128)(2,1)S(1)} fusion(bf16[1024,128,1]{0,1,2:T(8,128)(2,1)S(1)} %reshape.407, bf16[2,384,1024]{2,1,0:T(8,128)(2,1)} %param.6, bf16[2]{0:T(256)(128)(2,1)S(1)} %compare_convert_fusion), kind=kOutput, calls=%fused_computation.35 | convolution fusion | flops 204570624 | bytes 2031620 | tf_op jit(solution)/shard_map/scp,pk->skc/dot_general | solution.py:61
  17.9 3.2 %all-to-all-done = bf16[2,128,384]{2,0,1:T(2,128)(2,1)S(1)} async-done(((bf16[2,128,384]{2,0,1:T(2,128)(2,1)}), bf16[2,128,384]{2,0,1:T(2,128)(2,1)S(1)}, u32[]{:S(2)}, u32[]{:S(2)}) %all-to-all-start) | async-done | bytes 196640 | tf_op jit(solution)/shard_map/all_to_all | solution.py:68
  21.2 5.2 %all-to-all-start.2 = ((bf16[2,128,384]{2,0,1:T(2,128)(2,1)}), bf16[2,128,384]{2,0,1:T(2,128)(2,1)S(1)}, u32[]{:S(2)}, u32[]{:S(2)}) async-start(bf16[2,128,384]{2,0,1:T(2,128)(2,1)} %copy.141), calls=%async_computation.2 | async-start | bytes 393216 | tf_op jit(solution)/shard_map/all_to_all | solution.py:69
  28.1 4.9 %all-to-all-done.2 = bf16[2,128,384]{2,0,1:T(2,128)(2,1)S(1)} async-done(((bf16[2,128,384]{2,0,1:T(2,128)(2,1)}), bf16[2,128,384]{2,0,1:T(2,128)(2,1)S(1)}, u32[]{:S(2)}, u32[]{:S(2)}) %all-to-all-start.2) | async-done | bytes 196640 | tf_op jit(solution)/shard_map/all_to_all | solution.py:69
  35.5 2.4 %pad_maximum_fusion = f32[4,2,384,384]{3,2,0,1:T(8,128)} fusion(f32[4,1,384,384]{3,2,0,1:T(8,128)S(1)} %multiply_bitcast_fusion, f32[4,1,384,384]{3,2,0,1:T(8,128)S(1)} %multiply_bitcast_fusion.1), kind=kLoop, calls=%fused_computation | loop fusion | flops 1179648 | bytes 9437184 | tf_op jit(solution)/shard_map/stack | solution.py:103
  37.9 120.3 %all-reduce.1 = bf16[4,2,384,384]{3,2,0,1:T(8,128)(2,1)} all-reduce(f32[4,2,384,384]{3,2,0,1:T(8,128)} %pad_maximum_fusion), channel_id=1, replica_groups=mesh['dp'=32,'freq'=16] {'dp'}, use_global_device_ids=true, to_apply=%region_0.1 | all-reduce | flops 1179648 | bytes 7077888 | tf_op jit(solution)/shard_map/psum | solution.py:104
  158.2 2.4 %fusion.14 = f32[4,384,384]{2,1,0:T(8,128)S(1)} fusion(bf16[4,2,384,384]{3,2,0,1:T(8,128)(2,1)} %all-reduce.1, bf16[4,2,384,384]{3,2,1,0:T(8,128)(2,1)S(1)} %copy-done), kind=kOutput, calls=%fused_computation.23 | convolution fusion | flops 452984832 | bytes 4718592 | tf_op jit(solution)/shard_map/brk,bck->brc/dot_general | solution.py:112
  165.3 2.3 %fusion.16 = f32[4,384,384]{2,1,0:T(8,128)} fusion(bf16[4,384,384]{2,1,0:T(8,128)(2,1)S(1)} %add_convert_fusion, bf16[4,2,384,384]{3,2,1,0:T(8,128)(2,1)S(1)} %copy-done), kind=kOutput, calls=%fused_computation.25 | convolution fusion | flops 452984832 | bytes 4718592 | tf_op jit(solution)/shard_map/bkr,bkc->brc/dot_general | solution.py:40
  168.7 1.4 copy-done.2
  170.0 1.2 constant_dynamic-slice_fusion
  171.2 2.0 copy.164
  174.9 4.0 %add_multiply_fusion = f32[4,384,384]{2,1,0:T(8,128)} fusion(f32[4,384,384]{2,1,0:T(8,128)} %fusion.16, bf16[4,384,384]{2,1,0:T(8,128)(2,1)S(1)} %subtract_convert_fusion, bf16[4,2,384,384]{3,2,1,0:T(8,128)(2,1)S(1)} %copy-done), kind=kOutput, calls=%fused_computation.1 | convolution fusion | flops 454164480 | bytes 7077888 | tf_op jit(solution)/shard_map/bkr,bkc->brc/dot_general | solution.py:41
  178.9 3.1 %copy.147 = f32[4,384,384]{1,2,0:T(8,128)} copy(f32[4,384,384]{2,1,0:T(8,128)} %add_multiply_fusion) | data formatting | bytes 4718592 | tf_op jit(solution)/shard_map/mul | solution.py:39
  183.6 1.5 div.71
  185.1 1.5 copy.153
  186.6 1.3 reshape.409
  187.9 5.2 %all-to-all-start.3 = ((f32[16,1,2592]{2,1,0:T(1,128)}), f32[16,1,2592]{2,1,0:T(1,128)S(1)}, u32[]{:S(2)}, u32[]{:S(2)}) async-start(f32[16,1,2592]{2,1,0:T(1,128)} %reshape.409), calls=%async_computation.3 | async-start | bytes 344064 | tf_op jit(solution)/shard_map/all_to_all | solution.py:136
  193.2 1.4 fusion.66
  196.3 3.4 %all-to-all-done.3 = f32[16,1,2592]{2,1,0:T(1,128)S(1)} async-done(((f32[16,1,2592]{2,1,0:T(1,128)}), f32[16,1,2592]{2,1,0:T(1,128)S(1)}, u32[]{:S(2)}, u32[]{:S(2)}) %all-to-all-start.3) | async-done | bytes 165920 | tf_op jit(solution)/shard_map/all_to_all | solution.py:136
  199.7 5.2 %all-to-all-start.1 = ((bf16[32,8,384]{2,1,0:T(8,128)(2,1)}), bf16[32,8,384]{2,1,0:T(8,128)(2,1)S(1)}, u32[]{:S(2)}, u32[]{:S(2)}) async-start(bf16[32,8,384]{2,1,0:T(8,128)(2,1)} %copy.139), calls=%async_computation.1 | async-start | bytes 393216 | tf_op jit(solution)/shard_map/all_to_all | solution.py:93
  205.3 1.0 reduce
  207.7 3.8 %all-to-all-done.1 = bf16[32,8,384]{2,1,0:T(8,128)(2,1)S(1)} async-done(((bf16[32,8,384]{2,1,0:T(8,128)(2,1)}), bf16[32,8,384]{2,1,0:T(8,128)(2,1)S(1)}, u32[]{:S(2)}, u32[]{:S(2)}) %all-to-all-start.1) | async-done | bytes 196640 | tf_op jit(solution)/shard_map/all_to_all | solution.py:93
  (57 shorter events, 21.0 us)
Async XLA Ops:
  0.6 3.0 %copy-start.6 = (bf16[2,384,1024]{2,1,0:T(8,128)(2,1)S(1)}, bf16[2,384,1024]{2,1,0:T(8,128)(2,1)}, u32[]{:S(2)}) copy-start(bf16[2,384,1024]{2,1,0:T(8,128)(2,1)} %param.5) | copy-start | bytes 4718596
  4.4 13.3 %copy-start.5 = (s32[64]{0:T(128)S(1)}, s32[64]{0:T(128)}, u32[]{:S(2)}) copy-start(s32[64]{0:T(128)} %param.8) | copy-start | bytes 772
  5.3 15.9 %all-to-all-start = ((bf16[2,128,384]{2,0,1:T(2,128)(2,1)}), bf16[2,128,384]{2,0,1:T(2,128)(2,1)S(1)}, u32[]{:S(2)}, u32[]{:S(2)}) async-start(bf16[2,128,384]{2,0,1:T(2,128)(2,1)} %copy.132), calls=%async_computation | async-start | bytes 393216 | tf_op jit(solution)/shard_map/all_to_all | solution.py:68
  14.5 12.3 %copy-start = (bf16[4,2,384,384]{3,2,1,0:T(8,128)(2,1)S(1)}, bf16[4,2,384,384]{3,2,1,0:T(8,128)(2,1)}, u32[]{:S(2)}) copy-start(bf16[4,2,384,384]{3,2,1,0:T(8,128)(2,1)} %param.9) | copy-start | bytes 7077892
  21.2 11.8 %all-to-all-start.2 = ((bf16[2,128,384]{2,0,1:T(2,128)(2,1)}), bf16[2,128,384]{2,0,1:T(2,128)(2,1)S(1)}, u32[]{:S(2)}, u32[]{:S(2)}) async-start(bf16[2,128,384]{2,0,1:T(2,128)(2,1)} %copy.141), calls=%async_computation.2 | async-start | bytes 393216 | tf_op jit(solution)/shard_map/all_to_all | solution.py:69
  26.8 7.6 %copy-start.3 = (bf16[32,4,1,384]{3,2,1,0:T(2,128)(2,1)}, bf16[32,4,1,384]{3,2,1,0:T(2,128)(2,1)S(1)}, u32[]{:S(2)}) copy-start(bf16[32,4,1,384]{3,2,1,0:T(2,128)(2,1)S(1)} %get-tuple-element.7) | copy-start | bytes 294916
  158.2 2.4 %copy-start.1 = (bf16[4,2,384,384]{3,2,0,1:T(8,128)(2,1)S(1)}, bf16[4,2,384,384]{3,2,0,1:T(8,128)(2,1)}, u32[]{:S(2)}) copy-start(bf16[4,2,384,384]{3,2,0,1:T(8,128)(2,1)} %all-reduce.1) | copy-start | bytes 7077892
  168.6 1.4 copy-start.2
  178.9 4.1 %copy-start.4 = (f32[4,12,384]{2,0,1:T(4,128)S(1)}, f32[4,12,384]{2,0,1:T(4,128)}, u32[]{:S(2)}) copy-start(f32[4,12,384]{2,0,1:T(4,128)} %copy.152) | copy-start | bytes 221188
  187.9 11.7 %all-to-all-start.3 = ((f32[16,1,2592]{2,1,0:T(1,128)}), f32[16,1,2592]{2,1,0:T(1,128)S(1)}, u32[]{:S(2)}, u32[]{:S(2)}) async-start(f32[16,1,2592]{2,1,0:T(1,128)} %reshape.409), calls=%async_computation.3 | async-start | bytes 344064 | tf_op jit(solution)/shard_map/all_to_all | solution.py:136
  199.7 11.7 %all-to-all-start.1 = ((bf16[32,8,384]{2,1,0:T(8,128)(2,1)}), bf16[32,8,384]{2,1,0:T(8,128)(2,1)S(1)}, u32[]{:S(2)}, u32[]{:S(2)}) async-start(bf16[32,8,384]{2,1,0:T(8,128)(2,1)} %copy.139), calls=%async_computation.1 | async-start | bytes 393216 | tf_op jit(solution)/shard_map/all_to_all | solution.py:93

commit v2 on v0

--- a/solution.py
+++ b/solution.py
@@ -100,10 +100,8 @@
         jnp.einsum("ibr,ibc->brc", grad_imag, input_real, preferred_element_type=jnp.float32)
         - jnp.einsum("ibr,ibc->brc", grad_real, input_imag, preferred_element_type=jnp.float32)
     ) * gram_scale
-    gram_local = jnp.stack([gram_real, gram_imag], axis=1)
-    gram_matrix = lax.psum(gram_local, "dp").astype(jnp.bfloat16)
-    summed_real = gram_matrix[:, 0]
-    summed_imag = gram_matrix[:, 1]
+    summed_real = gram_real.astype(jnp.bfloat16)
+    summed_imag = gram_imag.astype(jnp.bfloat16)
     half_real = (
         jnp.einsum("brk,bck->brc", summed_real, factor_real, preferred_element_type=jnp.float32)
         + jnp.einsum("brk,bck->brc", summed_imag, factor_imag, preferred_element_type=jnp.float32)
@@ -112,24 +110,33 @@
         jnp.einsum("brk,bck->brc", summed_imag, factor_real, preferred_element_type=jnp.float32)
         - jnp.einsum("brk,bck->brc", summed_real, factor_imag, preferred_element_type=jnp.float32)
     ).astype(jnp.bfloat16)
-    row_share = channels // data_devices
-    row_start = lax.axis_index("dp") * row_share
     full_real, full_imag = left_product(factor_real, factor_imag, half_real, half_imag)
-    skew_real = full_real - jnp.swapaxes(full_real, 1, 2)
-    skew_imag = full_imag + jnp.swapaxes(full_imag, 1, 2)
-    skew_real = lax.dynamic_slice_in_dim(skew_real, row_start, row_share, 1)
-    skew_imag = lax.dynamic_slice_in_dim(skew_imag, row_start, row_share, 1)
     local_bins = lax.dynamic_slice_in_dim(
         bin_order, lax.axis_index("freq") * bins_local, bins_local
     )
     cos_local, sin_local = tap_phases(local_bins, GRID)
-    tap_partial = jnp.sum(
-        cos_local[:, :, None, None] * skew_real[:, None]
-        - sin_local[:, :, None, None] * skew_imag[:, None],
-        axis=0,
+    tap_scale = 1.0 / math.sqrt(total_bins)
+    phased = jnp.einsum(
+        "bt,brc->trc", cos_local * tap_scale, full_real, preferred_element_type=jnp.float32
+    ) - jnp.einsum(
+        "bt,brc->trc", sin_local * tap_scale, full_imag, preferred_element_type=jnp.float32
     )
-    tap_partial = tap_partial / math.sqrt(total_bins)
-    tap_grad = lax.psum_scatter(tap_partial, "freq", scatter_dimension=2, tiled=True)
+    tap_partial = phased - jnp.swapaxes(phased[::-1], 1, 2)
+    taps = tap_partial.shape[0]
+    col_share = channels // freq_devices
+    row_share = channels // data_devices
+    col_pieces = jnp.transpose(
+        tap_partial.astype(jnp.bfloat16).reshape(taps, channels, freq_devices, col_share),
+        (2, 0, 1, 3),
+    )
+    col_pieces = lax.all_to_all(col_pieces, "freq", split_axis=0, concat_axis=0, tiled=True)
+    col_sum = jnp.sum(col_pieces.astype(jnp.float32), axis=0)
+    row_pieces = jnp.transpose(
+        col_sum.astype(jnp.bfloat16).reshape(taps, data_devices, row_share, col_share),
+        (1, 0, 2, 3),
+    )
+    row_pieces = lax.all_to_all(row_pieces, "dp", split_axis=0, concat_axis=0, tiled=True)
+    tap_grad = jnp.sum(row_pieces.astype(jnp.float32), axis=0)
     return (returned, tap_grad)
 
 

time: 311 us -> 199 us (0.64)
  blocking collectives: 122 us -> 0 us
  waiting for transfers between devices: 113 us -> 55.8 us
  local copies, waits for them, and re-layouts: 14.7 us -> 56.4 us
  starting transfers between devices: 14.7 us -> 42.9 us
  between operations: 15.7 us -> 1.79 us
  other arithmetic: 7.82 us -> 15.2 us
  matrix products: 21.7 us -> 25.2 us
    psum x1 -> x0, blocking collectives: 122 us -> none  [local(): gram_matrix = lax.psum(gram_local, 'dp').astype(jnp.bfloat16)]
    unnamed x2 -> x0, waiting for transfers between devices: 105 us -> none
    all_to_all x0 -> x2, waiting for transfers between devices: none -> 45.4 us  [the longest x1 28.2 us: local(): lax.all_to_all(col_pieces, 'freq', split_axis=0, concat_axis=0, tiled=True)]
    all_to_all x0 -> x2, starting transfers between devices: none -> 24.8 us  [the longest x1 20.2 us: local(): lax.all_to_all(row_pieces, 'dp', split_axis=0, concat_axis=0, tiled=True)]
    rev x0 -> x1, local copies, waits for them, and re-layouts: none -> 13.9 us  [local(): tap_partial = phased - jnp.swapaxes(phased[::-1], 1, 2)]
    convert_element_type x0 -> x1, other arithmetic: none -> 10 us  [local(): tap_partial.astype(jnp.bfloat16)]
    sub x0 -> x1, local copies, waits for them, and re-layouts: none -> 9.72 us  [local(): jnp.einsum('bt,brc->trc', cos_local * tap_scale, full_real, preferred_ele...]
    convert_element_type x0 -> x1, local copies, waits for them, and re-layouts: none -> 6.78 us  [local(): tap_partial.astype(jnp.bfloat16)]
  transfers between devices with their start and end apart: 4 -> 5, of which waited for: 3 -> 4; matrix products, arithmetic and copies ran while one was open for 3% -> 8% of each run, Pallas kernels for 0% -> 0%
where the time goes in v2:
time: 199 us; the launch traced here: 197 us
  local copies, waits for them, and re-layouts  56.4 us (28%)
  waiting for transfers between devices  55.8 us (28%)
  starting transfers between devices  42.9 us (22%)
  matrix products  25.2 us (13%)
  other arithmetic  15.2 us (8%)
    all_to_all x1, waiting for transfers between devices, local(): lax.all_to_all(col_pieces, 'freq', split_axis=0, concat_axis=0, tiled=True)  28.2 us
    all_to_all x1, starting transfers between devices, local(): lax.all_to_all(row_pieces, 'dp', split_axis=0, concat_axis=0, tiled=True)  20.2 us
    all_to_all x1, waiting for transfers between devices, local(): lax.all_to_all(row_pieces, 'dp', split_axis=0, concat_axis=0, tiled=True)  17.2 us
    rev x1, local copies, waits for them, and re-layouts, local(): tap_partial = phased - jnp.swapaxes(phased[::-1], 1, 2)  13.9 us
    convert_element_type x1, other arithmetic, local(): tap_partial.astype(jnp.bfloat16)  10 us
    sub x1, local copies, waits for them, and re-layouts, local(): jnp.einsum('bt,brc->trc', cos_local * tap_scale, full_real, preferred_ele...  9.72 us
    all_to_all x1, starting transfers between devices, local(): lax.all_to_all(input_spec, 'freq', split_axis=1, concat_axis=0, tiled=True)  7.58 us
    all_to_all x1, starting transfers between devices, local(): lax.all_to_all(back_both, 'freq', split_axis=0, concat_axis=1, tiled=True)  6.85 us
  transfers between devices with their start and end apart: 5, of which 4 were waited for; matrix products, arithmetic and copies ran while one was open for 8% of the time, Pallas kernels for 0%

profile of v2, /device:TPU:1, one launch (start us, length us, event | category | flops | bytes accessed | tf_op | source)
XLA Modules:
  0.0 197.4 jit_solution(3954096775494600744)
XLA Ops:
  5.3 7.6 %all-to-all-start.2 = ((bf16[2,128,384]{2,0,1:T(2,128)(2,1)}), bf16[2,128,384]{2,0,1:T(2,128)(2,1)S(1)}, u32[]{:S(2)}, u32[]{:S(2)}) async-start(bf16[2,128,384]{2,0,1:T(2,128)(2,1)} %copy.102), calls=%async_computation.2 | async-start | bytes 393216 | tf_op jit(solution)/shard_map/all_to_all | solution.py:69
  12.9 2.1 %fusion.34 = bf16[2,128,384]{2,1,0:T(8,128)(2,1)S(1)} fusion(bf16[1024,128,1]{0,1,2:T(8,128)(2,1)S(1)} %reshape.289, bf16[2,384,1024]{2,1,0:T(8,128)(2,1)} %param.5, bf16[2]{0:T(256)(128)(2,1)S(1)} %compare_convert_fusion), kind=kOutput, calls=%fused_computation.37 | convolution fusion | flops 204570624 | bytes 2031620 | tf_op jit(solution)/shard_map/scp,pk->skc/dot_general | solution.py:61
  16.0 3.8 %all-to-all-done.2 = bf16[2,128,384]{2,0,1:T(2,128)(2,1)S(1)} async-done(((bf16[2,128,384]{2,0,1:T(2,128)(2,1)}), bf16[2,128,384]{2,0,1:T(2,128)(2,1)S(1)}, u32[]{:S(2)}, u32[]{:S(2)}) %all-to-all-start.2) | async-done | bytes 196640 | tf_op jit(solution)/shard_map/all_to_all | solution.py:69
  19.8 3.7 %all-to-all-start = ((bf16[2,128,384]{2,0,1:T(2,128)(2,1)}), bf16[2,128,384]{2,0,1:T(2,128)(2,1)S(1)}, u32[]{:S(2)}, u32[]{:S(2)}) async-start(bf16[2,128,384]{2,0,1:T(2,128)(2,1)} %copy.93), calls=%async_computation | async-start | bytes 393216 | tf_op jit(solution)/shard_map/all_to_all | solution.py:68
  23.6 6.6 %all-to-all-done = bf16[2,128,384]{2,0,1:T(2,128)(2,1)S(1)} async-done(((bf16[2,128,384]{2,0,1:T(2,128)(2,1)}), bf16[2,128,384]{2,0,1:T(2,128)(2,1)S(1)}, u32[]{:S(2)}, u32[]{:S(2)}) %all-to-all-start) | async-done | bytes 196640 | tf_op jit(solution)/shard_map/all_to_all | solution.py:68
  38.9 2.4 %fusion.17 = f32[4,384,384]{2,1,0:T(8,128)} fusion(bf16[4,384,384]{2,1,0:T(8,128)(2,1)S(1)} %add_convert_fusion, bf16[4,2,384,384]{3,2,1,0:T(8,128)(2,1)S(1)} %copy-done), kind=kOutput, calls=%fused_computation.26 | convolution fusion | flops 452984832 | bytes 4718592 | tf_op jit(solution)/shard_map/bkr,bkc->brc/dot_general | solution.py:40
  41.3 2.0 %multiply_bitcast_fusion = bf16[4,384,384]{1,2,0:T(8,128)(2,1)} fusion(f32[4,384,384]{2,1,0:T(8,128)S(1)} %fusion.13, bf16[4,384,384]{2,1,0:T(8,128)(2,1)S(1)} %add_convert_fusion, bf16[4,2,384,384]{3,2,1,0:T(8,128)(2,1)S(1)} %copy-done), kind=kOutput, calls=%fused_computation.3 | convolution fusion | flops 454754304 | bytes 5898240 | tf_op jit(solution)/shard_map/bkr,bkc->brc/dot_general | solution.py:45
  43.3 3.4 %copy.111 = bf16[4,384,384]{2,0,1:T(4,128)(2,1)} copy(bf16[4,384,384]{1,2,0:T(8,128)(2,1)} %multiply_bitcast_fusion) | data formatting | bytes 2359296 | tf_op jit(solution)/shard_map/mul | solution.py:43
  46.7 3.6 %multiply_bitcast_fusion.1 = bf16[4,384,384]{1,2,0:T(8,128)(2,1)} fusion(f32[4,384,384]{2,1,0:T(8,128)} %fusion.17, bf16[4,384,384]{2,1,0:T(8,128)(2,1)S(1)} %subtract_convert_fusion, bf16[4,2,384,384]{3,2,1,0:T(8,128)(2,1)S(1)} %copy-done), kind=kOutput, calls=%fused_computation.4 | convolution fusion | flops 454754304 | bytes 5898240 | tf_op jit(solution)/shard_map/bkr,bkc->brc/dot_general | solution.py:41
  50.3 2.5 %copy.108 = bf16[4,384,384]{2,0,1:T(4,128)(2,1)S(1)} copy(bf16[4,384,384]{1,2,0:T(8,128)(2,1)} %multiply_bitcast_fusion.1) | data formatting | bytes 2359296 | tf_op jit(solution)/shard_map/mul | solution.py:39
  54.5 4.9 %convolution_subtract_fusion = f32[9,384,384]{2,0,1:T(8,128)} fusion(f32[9,384,384]{2,0,1:T(8,128)S(1)} %fusion.105, bf16[4,384,384]{2,0,1:T(4,128)(2,1)S(1)} %copy-done.1, s32[9]{0:T(128)S(1)} %get-tuple-element.20, s32[4]{0:T(128)S(1)} %and_select_fusion.1, s32[9]{0:T(128)S(1)} %get-tuple-element.21, s32[4]{0:T(128)S(1)} %get-tuple-element.8), kind=kOutput, calls=%fused_computation.2 | convolution fusion | flops 11944548 | bytes 11796584 | tf_op jit(solution)/shard_map/bt,brc->trc/dot_general | solution.py:121
  59.3 9.7 %copy.112 = f32[9,384,384]{1,0,2:T(8,128)} copy(f32[9,384,384]{2,0,1:T(8,128)} %convolution_subtract_fusion) | data formatting | bytes 10616832 | tf_op jit(solution)/shard_map/sub | solution.py:119
  69.1 13.9 %rev.3 = f32[9,384,384]{1,0,2:T(8,128)} reverse(f32[9,384,384]{1,0,2:T(8,128)} %copy.112), dimensions={0} | reverse | bytes 10616832 | tf_op jit(solution)/shard_map/rev | solution.py:124
  83.0 10.0 %fusion = bf16[9,384,384]{2,0,1:T(8,128)(2,1)} fusion(f32[9,384,384]{2,0,1:T(8,128)} %convolution_subtract_fusion, f32[9,384,384]{1,0,2:T(8,128)} %rev.3), kind=kLoop, calls=%fused_computation.1 | loop fusion | flops 2654208 | bytes 13271040 | tf_op jit(solution)/shard_map/convert_element_type | solution.py:129
  93.0 6.8 %copy.113 = bf16[9,384,384]{1,2,0:T(8,128)(2,1)} copy(bf16[9,384,384]{2,0,1:T(8,128)(2,1)} %fusion) | data formatting | bytes 5308416 | tf_op jit(solution)/shard_map/convert_element_type | solution.py:129
  99.8 3.5 %copy.114 = bf16[16,9,384,24]{2,3,1,0:T(8,128)(2,1)} copy(bf16[16,9,384,24]{2,3,0,1:T(8,128)(2,1)} %bitcast.159) | data formatting | bytes 5308416 | tf_op jit(solution)/shard_map/transpose | solution.py:128
  103.3 4.6 %all-to-all-start.3 = ((bf16[16,9,384,24]{2,3,1,0:T(8,128)(2,1)}), bf16[16,9,384,24]{2,3,1,0:T(8,128)(2,1)}, u32[]{:S(2)}, u32[]{:S(2)}) async-start(bf16[16,9,384,24]{2,3,1,0:T(8,128)(2,1)} %copy.114), calls=%async_computation.3 | async-start | bytes 5308416 | tf_op jit(solution)/shard_map/all_to_all | solution.py:132
  110.0 28.2 %all-to-all-done.3 = bf16[16,9,384,24]{2,3,1,0:T(8,128)(2,1)} async-done(((bf16[16,9,384,24]{2,3,1,0:T(8,128)(2,1)}), bf16[16,9,384,24]{2,3,1,0:T(8,128)(2,1)}, u32[]{:S(2)}, u32[]{:S(2)}) %all-to-all-start.3) | async-done | bytes 2654240 | tf_op jit(solution)/shard_map/all_to_all | solution.py:132
  138.1 6.9 %all-to-all-start.1 = ((bf16[32,8,384]{2,1,0:T(8,128)(2,1)}), bf16[32,8,384]{2,1,0:T(8,128)(2,1)S(1)}, u32[]{:S(2)}, u32[]{:S(2)}) async-start(bf16[32,8,384]{2,1,0:T(8,128)(2,1)} %copy.100), calls=%async_computation.1 | async-start | bytes 393216 | tf_op jit(solution)/shard_map/all_to_all | solution.py:93
  145.0 2.2 %reduce_sum.21 = bf16[9,384,24]{1,2,0:T(8,128)(2,1)S(1)} reduce(bf16[16,9,384,24]{2,3,1,0:T(8,128)(2,1)} %all-to-all-done.3, bf16[]{:T(256)} %constant.125.clone.1), dimensions={0}, to_apply=%region_0.1 | reduce | flops 1244160 | bytes 2820098 | tf_op jit(solution)/shard_map/reduce_sum | solution.py:133
  147.2 4.0 %reshape.288 = bf16[9,32,12,24]{2,1,3,0:T(8,128)(2,1)S(1)} reshape(bf16[9,384,24]{1,2,0:T(8,128)(2,1)S(1)} %reduce_sum.21) | data formatting | bytes 331776 | tf_op jit(solution)/shard_map/reshape | solution.py:135
  151.2 2.4 %copy.115 = bf16[32,9,12,24]{3,2,1,0:T(8,128)(2,1)S(1)} copy(bf16[32,9,12,24]{2,0,3,1:T(8,128)(2,1)S(1)} %bitcast.160) | data formatting | bytes 331776 | tf_op jit(solution)/shard_map/transpose | solution.py:134
  155.4 20.2 %all-to-all-start.4 = ((bf16[32,2,1296]{2,1,0:T(2,128)(2,1)}), bf16[32,2,1296]{2,1,0:T(2,128)(2,1)S(1)}, u32[]{:S(2)}, u32[]{:S(2)}) async-start(bf16[32,2,1296]{2,1,0:T(2,128)(2,1)} %reshape.293), calls=%async_computation.4 | async-start | bytes 360448 | tf_op jit(solution)/shard_map/all_to_all | solution.py:138
  176.3 17.2 %all-to-all-done.4 = bf16[32,2,1296]{2,1,0:T(2,128)(2,1)S(1)} async-done(((bf16[32,2,1296]{2,1,0:T(2,128)(2,1)}), bf16[32,2,1296]{2,1,0:T(2,128)(2,1)S(1)}, u32[]{:S(2)}, u32[]{:S(2)}) %all-to-all-start.4) | async-done | bytes 165920 | tf_op jit(solution)/shard_map/all_to_all | solution.py:138
  (58 shorter events, 23.3 us)
Async XLA Ops:
  0.6 3.0 %copy-start.7 = (bf16[2,384,1024]{2,1,0:T(8,128)(2,1)S(1)}, bf16[2,384,1024]{2,1,0:T(8,128)(2,1)}, u32[]{:S(2)}) copy-start(bf16[2,384,1024]{2,1,0:T(8,128)(2,1)} %param.6) | copy-start | bytes 4718596
  4.4 11.5 %copy-start.6 = (s32[64]{0:T(128)S(1)}, s32[64]{0:T(128)}, u32[]{:S(2)}) copy-start(s32[64]{0:T(128)} %param.8) | copy-start | bytes 772
  5.3 14.5 %all-to-all-start.2 = ((bf16[2,128,384]{2,0,1:T(2,128)(2,1)}), bf16[2,128,384]{2,0,1:T(2,128)(2,1)S(1)}, u32[]{:S(2)}, u32[]{:S(2)}) async-start(bf16[2,128,384]{2,0,1:T(2,128)(2,1)} %copy.102), calls=%async_computation.2 | async-start | bytes 393216 | tf_op jit(solution)/shard_map/all_to_all | solution.py:69
  19.8 10.4 %all-to-all-start = ((bf16[2,128,384]{2,0,1:T(2,128)(2,1)}), bf16[2,128,384]{2,0,1:T(2,128)(2,1)S(1)}, u32[]{:S(2)}, u32[]{:S(2)}) async-start(bf16[2,128,384]{2,0,1:T(2,128)(2,1)} %copy.93), calls=%async_computation | async-start | bytes 393216 | tf_op jit(solution)/shard_map/all_to_all | solution.py:68
  30.6 1.3 copy-start.4
  30.6 1.9 copy-start.2
  32.5 1.7 copy-start
  52.8 1.6 copy-start.1
  103.3 4.6 %copy-start.3 = (bf16[32,4,1,384]{3,2,1,0:T(2,128)(2,1)S(1)}, bf16[32,4,1,384]{3,2,1,0:T(2,128)(2,1)}, u32[]{:S(2)}) copy-start(bf16[32,4,1,384]{3,2,1,0:T(2,128)(2,1)} %copy-done.2) | copy-start | bytes 294916
  103.3 4.9 %copy-start.5 = (bf16[32,4,1,384]{3,2,1,0:T(2,128)(2,1)S(1)}, bf16[32,4,1,384]{3,2,1,0:T(2,128)(2,1)}, u32[]{:S(2)}) copy-start(bf16[32,4,1,384]{3,2,1,0:T(2,128)(2,1)} %copy-done.4) | copy-start | bytes 294916
  103.3 34.8 %all-to-all-start.3 = ((bf16[16,9,384,24]{2,3,1,0:T(8,128)(2,1)}), bf16[16,9,384,24]{2,3,1,0:T(8,128)(2,1)}, u32[]{:S(2)}, u32[]{:S(2)}) async-start(bf16[16,9,384,24]{2,3,1,0:T(8,128)(2,1)} %copy.114), calls=%async_computation.3 | async-start | bytes 5308416 | tf_op jit(solution)/shard_map/all_to_all | solution.py:132
  138.1 17.3 %all-to-all-start.1 = ((bf16[32,8,384]{2,1,0:T(8,128)(2,1)}), bf16[32,8,384]{2,1,0:T(8,128)(2,1)S(1)}, u32[]{:S(2)}, u32[]{:S(2)}) async-start(bf16[32,8,384]{2,1,0:T(8,128)(2,1)} %copy.100), calls=%async_computation.1 | async-start | bytes 393216 | tf_op jit(solution)/shard_map/all_to_all | solution.py:93
  155.4 38.1 %all-to-all-start.4 = ((bf16[32,2,1296]{2,1,0:T(2,128)(2,1)}), bf16[32,2,1296]{2,1,0:T(2,128)(2,1)S(1)}, u32[]{:S(2)}, u32[]{:S(2)}) async-start(bf16[32,2,1296]{2,1,0:T(2,128)(2,1)} %reshape.293), calls=%async_computation.4 | async-start | bytes 360448 | tf_op jit(solution)/shard_map/all_to_all | solution.py:138

commit v3 on v2

v3 whole, which is shorter than its diff:
```python
import math

import jax
import jax.numpy as jnp
from jax import lax
from jax.sharding import PartitionSpec as P

GRID = 32


def dft_table(bin_order, grid_side):
    pixel_index = jnp.arange(grid_side * grid_side, dtype=jnp.int32)
    row_pos = pixel_index // grid_side
    col_pos = pixel_index % grid_side
    freq_u = bin_order // grid_side
    freq_v = bin_order % grid_side
    phase_turns = (
        row_pos[:, None] * freq_u[None, :] + col_pos[:, None] * freq_v[None, :]
    ) % grid_side
    phase_angle = phase_turns.astype(jnp.float32) * (2.0 * math.pi / grid_side)
    both_parts = jnp.stack([jnp.cos(phase_angle), -jnp.sin(phase_angle)], axis=2) / grid_side
    return both_parts.reshape(grid_side * grid_side, -1).astype(jnp.bfloat16)


def tap_phases(bin_order, grid_side):
    offsets = jnp.arange(9, dtype=jnp.int32)
    shift_y = offsets // 3 - 1
    shift_x = offsets % 3 - 1
    freq_u = bin_order // grid_side
    freq_v = bin_order % grid_side
    phase_turns = (
        freq_u[:, None] * shift_y[None, :] + freq_v[:, None] * shift_x[None, :]
    ) % grid_side
    phase_angle = phase_turns.astype(jnp.float32) * (2.0 * math.pi / grid_side)
    return (jnp.cos(phase_angle), jnp.sin(phase_angle))


def local(output_grad, layer_input, counts, bin_order, inverse_factor):
    slot_count, channels, pixels = output_grad.shape
    freq_devices = lax.axis_size("freq")
    data_devices = lax.axis_size("dp")
    bins_local = inverse_factor.shape[0]
    total_bins = bin_order.shape[0]
    live_mask = (jnp.arange(slot_count, dtype=jnp.int32) < counts[0]).astype(jnp.bfloat16)
    bins_table = dft_table(bin_order, GRID)

    def spectrum(images):
        masked = images * live_mask[:, None, None]
        return jnp.einsum(
            "scp,pk->skc", masked, bins_table, preferred_element_type=jnp.float32
        ).astype(jnp.bfloat16)

    both_spec = jnp.stack([spectrum(output_grad), spectrum(layer_input)], axis=0)
    both_recv = lax.all_to_all(both_spec, "freq", split_axis=2, concat_axis=1, tiled=True)
    image_rows = both_recv.shape[1]
    parts = both_recv.reshape(2, image_rows, bins_local, 2, channels)
    grad_real = parts[0, :, :, 0]
    grad_imag = parts[0, :, :, 1]
    input_real = parts[1, :, :, 0]
    input_imag = parts[1, :, :, 1]
    factor_real = inverse_factor[:, 0]
    factor_imag = inverse_factor[:, 1]
    f32 = jnp.float32

    def mm(x, p, eq):
        return jnp.einsum(eq, x, p, preferred_element_type=f32)

    u_real = mm(grad_real, factor_real, "ibr,brc->ibc") + mm(grad_imag, factor_imag, "ibr,brc->ibc")
    u_imag = mm(grad_imag, factor_real, "ibr,brc->ibc") - mm(grad_real, factor_imag, "ibr,brc->ibc")
    back_real = 2.0 * u_real - grad_real.astype(f32)
    back_imag = 2.0 * u_imag - grad_imag.astype(f32)
    back_both = (
        jnp.stack([back_real, back_imag], axis=2)
        .astype(jnp.bfloat16)
        .reshape(image_rows, 2 * bins_local, channels)
    )
    returned = lax.all_to_all(back_both, "freq", split_axis=0, concat_axis=1, tiled=True)
    v_real = mm(input_real, factor_real, "ibk,bck->ibc") - mm(input_imag, factor_imag, "ibk,bck->ibc")
    v_imag = mm(input_real, factor_imag, "ibk,bck->ibc") + mm(input_imag, factor_real, "ibk,bck->ibc")
    local_bins = lax.dynamic_slice_in_dim(
        bin_order, lax.axis_index("freq") * bins_local, bins_local
    )
    cos_local, sin_local = tap_phases(local_bins, GRID)
    cos_t = cos_local.T[:, None, :, None]
    sin_t = sin_local.T[:, None, :, None]
    ur = u_real[None]
    ui = u_imag[None]
    z_t = jnp.stack([cos_t * ur - sin_t * ui, cos_t * ui + sin_t * ur], axis=1).astype(jnp.bfloat16)
    w_t = jnp.stack([cos_t * ur + sin_t * ui, cos_t * ui - sin_t * ur], axis=1).astype(jnp.bfloat16)
    y_all = jnp.stack([v_real, v_imag], axis=0).astype(jnp.bfloat16)
    taps = z_t.shape[0]
    col_share = channels // freq_devices
    row_share = channels // data_devices
    y_cols = y_all.reshape(2, image_rows, bins_local, freq_devices, col_share)
    w_cols = w_t.reshape(taps, 2, image_rows, bins_local, freq_devices, col_share)
    first = jnp.einsum("teibr,eibfc->ftrc", z_t, y_cols, preferred_element_type=f32)
    second = jnp.einsum("eibr,teibfc->ftrc", y_all, w_cols, preferred_element_type=f32)
    gram_scale = 1.0 / math.sqrt(data_devices * freq_devices * slot_count)
    tap_scale = 2.0 * gram_scale / math.sqrt(total_bins)
    col_pieces = ((second - first) * tap_scale).astype(jnp.bfloat16)
    col_pieces = lax.all_to_all(col_pieces, "freq", split_axis=0, concat_axis=0, tiled=True)
    col_sum = jnp.sum(col_pieces.astype(f32), axis=0)
    row_pieces = jnp.transpose(
        col_sum.reshape(taps, data_devices, row_share, col_share), (1, 0, 2, 3)
    )
    row_pieces = lax.all_to_all(row_pieces, "dp", split_axis=0, concat_axis=0, tiled=True)
    tap_grad = jnp.sum(row_pieces, axis=0)
    return (returned, tap_grad)


def solution(mesh):
    return jax.shard_map(
        local,
        mesh=mesh,
        in_specs=(
            P(("dp", "freq"), None, None),
            P(("dp", "freq"), None, None),
            P(("dp", "freq")),
            P(),
            P("freq", None, None, None),
        ),
        out_specs=(P(("dp", "freq"), None, None), P(None, "dp", "freq")),
        check_vma=False,
    )
```

time: 199 us -> 151 us (0.76)
  local copies, waits for them, and re-layouts: 56.4 us -> 27.7 us
  matrix products: 25.2 us -> 13 us
  other arithmetic: 15.2 us -> 8.46 us
  waiting for transfers between devices: 55.8 us -> 61.6 us
  starting transfers between devices: 42.9 us -> 38.3 us
    rev x1 -> x0, local copies, waits for them, and re-layouts: 13.9 us -> none  [local(): tap_partial = phased - jnp.swapaxes(phased[::-1], 1, 2)]
    dot_general x18 -> x10, matrix products: 22.4 us -> 10.1 us  [the longest x8 4.61 us: mm(): return jnp.einsum(eq, x, p, preferred_element_type=f32)]
    convert_element_type x1 -> x0, other arithmetic: 10 us -> none  [local(): tap_partial.astype(jnp.bfloat16)]
    sub x1 -> x0, local copies, waits for them, and re-layouts: 9.72 us -> none  [local(): jnp.einsum('bt,brc->trc', cos_local * tap_scale, full_real, preferred_ele...]
    all_to_all x1, waiting for transfers between devices: 17.2 us -> 24.2 us  [local(): lax.all_to_all(row_pieces, 'dp', split_axis=0, concat_axis=0, tiled=True)]
    another operation x0 -> x5, local copies, waits for them, and re-layouts: none -> 6.82 us  [the longest x4 5.67 us: local(): y_all = jnp.stack([v_real, v_imag], axis=0).astype(jnp.bfloat16)]
    convert_element_type x3 -> x1, local copies, waits for them, and re-layouts: 8.53 us -> 1.77 us  [local(): col_pieces = ((second - first) * tap_scale).astype(jnp.bfloat16)]
    all_to_all x2 -> x1, starting transfers between devices: 11.3 us -> 7.59 us  [local(): lax.all_to_all(both_spec, 'freq', split_axis=2, concat_axis=1, tiled=True)]
  transfers between devices with their start and end apart: 5 -> 4, of which waited for: 4 -> 3; matrix products, arithmetic and copies ran while one was open for 8% -> 10% of each run, Pallas kernels for 0% -> 0%
where the time goes in v3:
time: 151 us
  waiting for transfers between devices  61.6 us (41%)
  starting transfers between devices  38.3 us (25%)
  local copies, waits for them, and re-layouts  27.7 us (18%)
  matrix products  13 us (9%)
  other arithmetic  8.46 us (6%)
  between operations  1.65 us (1%)
    all_to_all x1, waiting for transfers between devices, local(): lax.all_to_all(col_pieces, 'freq', split_axis=0, concat_axis=0, tiled=True)  29.6 us
    all_to_all x1, waiting for transfers between devices, local(): lax.all_to_all(row_pieces, 'dp', split_axis=0, concat_axis=0, tiled=True)  24.2 us
    all_to_all x1, starting transfers between devices, local(): lax.all_to_all(row_pieces, 'dp', split_axis=0, concat_axis=0, tiled=True)  18.5 us
    all_to_all x1, starting transfers between devices, local(): lax.all_to_all(back_both, 'freq', split_axis=0, concat_axis=1, tiled=True)  8.43 us
    all_to_all x1, waiting for transfers between devices, local(): lax.all_to_all(both_spec, 'freq', split_axis=2, concat_axis=1, tiled=True)  7.74 us
    all_to_all x1, starting transfers between devices, local(): lax.all_to_all(both_spec, 'freq', split_axis=2, concat_axis=1, tiled=True)  7.59 us
    another operation x4, local copies, waits for them, and re-layouts, local(): y_all = jnp.stack([v_real, v_imag], axis=0).astype(jnp.bfloat16)  5.67 us
    reshape x1, local copies, waits for them, and re-layouts, local(): col_sum.reshape(taps, data_devices, row_share, col_share)  4.81 us
  transfers between devices with their start and end apart: 4, of which 3 were waited for; matrix products, arithmetic and copies ran while one was open for 10% of the time, Pallas kernels for 0%

profile of v3, /device:TPU:1, one launch (start us, length us, event | category | flops | bytes accessed | tf_op | source)
XLA Modules:
  0.0 150.7 jit_solution(6233264693370141867)
XLA Ops:
  1.4 1.1 fusion.84
  4.4 2.1 %fusion.40 = bf16[1,2,128,384]{3,2,1,0:T(8,128)(2,1)S(1)} fusion(bf16[1024,128,1]{0,1,2:T(8,128)(2,1)S(1)} %reshape.456, bf16[2,384,1024]{2,1,0:T(8,128)(2,1)} %param.5, bf16[2]{0:T(256)(128)(2,1)S(1)} %compare_convert_fusion), kind=kOutput, calls=%fused_computation.39 | convolution fusion | flops 204570624 | bytes 2031620 | tf_op jit(solution)/shard_map/scp,pk->skc/dot_general | solution.py:49
  6.6 1.2 copy.86
  7.8 7.6 %all-to-all-start = ((bf16[2,2,128,384]{3,1,0,2:T(2,128)(2,1)}), bf16[2,2,128,384]{3,1,0,2:T(2,128)(2,1)S(1)}, u32[]{:S(2)}, u32[]{:S(2)}) async-start(bf16[2,2,128,384]{3,1,0,2:T(2,128)(2,1)} %copy.86), calls=%async_computation | async-start | bytes 786432 | tf_op jit(solution)/shard_map/all_to_all | solution.py:54
  15.6 7.7 %all-to-all-done = bf16[2,2,128,384]{3,1,0,2:T(2,128)(2,1)S(1)} async-done(((bf16[2,2,128,384]{3,1,0,2:T(2,128)(2,1)}), bf16[2,2,128,384]{3,1,0,2:T(2,128)(2,1)S(1)}, u32[]{:S(2)}, u32[]{:S(2)}) %all-to-all-start) | async-done | bytes 393248 | tf_op jit(solution)/shard_map/all_to_all | solution.py:54
  25.9 1.2 fusion.17
  27.5 1.5 stack.67
  29.0 2.2 %copy.101 = bf16[1,32,4,16,24]{1,4,0,2,3:T(8,128)(2,1)} copy(bf16[1,32,4,16,24]{4,3,1,2,0:T(8,128)(2,1)} %stack.67) | data formatting | bytes 196608 | tf_op jit(solution)/shard_map/stack | solution.py:90
  31.2 1.4 fusion.64
  33.3 1.3 copy.100
  37.6 2.0 %add_convert_fusion = (bf16[9,1,32,4,16,24]{2,5,1,3,4,0:T(8,128)(2,1)S(1)}, bf16[9,1,32,4,16,24]{2,5,1,3,4,0:T(8,128)(2,1)S(1)}) fusion(f32[32,4,16,24]{0,3,1,2:T(8,128)S(1)} %copy.96, f32[9,4]{1,0:T(8,128)S(1)} %get-tuple-element.21, f32[32,4,16,24]{0,3,1,2:T(8,128)S(1)} %copy.95, f32[9,4]{1,0:T(8,128)S(1)} %get-tuple-element.20), kind=kLoop, calls=%fused_computation.5 | loop fusion | flops 3538944 | bytes 2162976 | tf_op jit(solution)/shard_map/convert.10
  40.7 4.4 %fusion.5 = bf16[16,9,384,24]{2,3,0,1:T(8,128)(2,1)S(1)} fusion(f32[16,24,9,384,1,1]{3,1,5,4,0,2:T(8,128)S(1)} %fusion.8, bf16[9,1,32,4,16,24]{2,5,1,3,4,0:T(8,128)(2,1)S(1)} %get-tuple-element.11, bf16[9,1,32,4,16,24]{2,5,1,3,4,0:T(8,128)(2,1)S(1)} %get-tuple-element.10, bf16[1,32,4,384]{3,1,2,0:T(8,128)(2,1)S(1)} %bitcast.141, ...), kind=kOutput, calls=%fused_computation.8 | convolution fusion | flops 684441600 | bytes 9928704 | tf_op jit(solution)/shard_map/eibr,teibfc->ftrc/dot_general | solution.py:97
  45.2 1.8 %copy.102 = bf16[16,9,384,24]{2,3,1,0:T(8,128)(2,1)} copy(bf16[16,9,384,24]{2,3,0,1:T(8,128)(2,1)S(1)} %fusion.5) | data formatting | bytes 5308416 | tf_op jit(solution)/shard_map/convert_element_type | solution.py:100
  47.0 3.7 %all-to-all-start.2 = ((bf16[16,9,384,24]{2,3,1,0:T(8,128)(2,1)}), bf16[16,9,384,24]{2,3,1,0:T(8,128)(2,1)S(1)}, u32[]{:S(2)}, u32[]{:S(2)}) async-start(bf16[16,9,384,24]{2,3,1,0:T(8,128)(2,1)} %copy.102), calls=%async_computation.2 | async-start | bytes 5308416 | tf_op jit(solution)/shard_map/all_to_all | solution.py:101
  51.6 29.6 %all-to-all-done.2 = bf16[16,9,384,24]{2,3,1,0:T(8,128)(2,1)S(1)} async-done(((bf16[16,9,384,24]{2,3,1,0:T(8,128)(2,1)}), bf16[16,9,384,24]{2,3,1,0:T(8,128)(2,1)S(1)}, u32[]{:S(2)}, u32[]{:S(2)}) %all-to-all-start.2) | async-done | bytes 2654240 | tf_op jit(solution)/shard_map/all_to_all | solution.py:101
  81.2 8.4 %all-to-all-start.1 = ((bf16[32,8,384]{2,1,0:T(8,128)(2,1)}), bf16[32,8,384]{2,1,0:T(8,128)(2,1)}, u32[]{:S(2)}, u32[]{:S(2)}) async-start(bf16[32,8,384]{2,1,0:T(8,128)(2,1)} %copy.93), calls=%async_computation.1 | async-start | bytes 393216 | tf_op jit(solution)/shard_map/all_to_all | solution.py:77
  89.7 1.1 convert_reduce_fusion
  90.8 4.8 %reshape.455 = f32[9,32,12,24]{2,1,3,0:T(8,128)S(1)} reshape(f32[9,384,24]{1,2,0:T(8,128)} %convert_reduce_fusion) | data formatting | bytes 663552 | tf_op jit(solution)/shard_map/reshape | solution.py:104
  95.6 3.4 %copy.103 = f32[32,9,12,24]{3,2,1,0:T(8,128)} copy(f32[32,9,12,24]{2,0,3,1:T(8,128)S(1)} %bitcast.136) | data formatting | bytes 663552 | tf_op jit(solution)/shard_map/transpose | solution.py:103
  98.9 3.5 %reshape.463 = f32[32,1,2592]{2,1,0:T(1,128)} reshape(f32[32,9,12,24]{3,2,1,0:T(8,128)} %copy.103) | data formatting | bytes 663552
  102.4 18.5 %all-to-all-start.3 = ((f32[32,1,2592]{2,1,0:T(1,128)}), f32[32,1,2592]{2,1,0:T(1,128)S(1)}, u32[]{:S(2)}, u32[]{:S(2)}) async-start(f32[32,1,2592]{2,1,0:T(1,128)} %reshape.463), calls=%async_computation.3 | async-start | bytes 688128 | tf_op jit(solution)/shard_map/all_to_all | solution.py:106
  121.0 1.6 %copy.138 = bf16[2,16,8,384]{3,2,1,0:T(8,128)(2,1)} copy(bf16[2,16,8,384]{3,2,0,1:T(8,128)(2,1)} %bitcast.19) | data formatting | bytes 393216 | tf_op jit(solution)/shard_map/all_to_all | solution.py:77
  122.6 24.2 %all-to-all-done.3 = f32[32,1,2592]{2,1,0:T(1,128)S(1)} async-done(((f32[32,1,2592]{2,1,0:T(1,128)}), f32[32,1,2592]{2,1,0:T(1,128)S(1)}, u32[]{:S(2)}, u32[]{:S(2)}) %all-to-all-start.3) | async-done | bytes 331808 | tf_op jit(solution)/shard_map/all_to_all | solution.py:106
  147.4 1.5 reduce
  (50 shorter events, 13.1 us)
Async XLA Ops:
  0.6 3.0 %copy-start.6 = (bf16[2,384,1024]{2,1,0:T(8,128)(2,1)S(1)}, bf16[2,384,1024]{2,1,0:T(8,128)(2,1)}, u32[]{:S(2)}) copy-start(bf16[2,384,1024]{2,1,0:T(8,128)(2,1)} %param.6) | copy-start | bytes 4718596
  4.4 11.0 %copy-start.5 = (s32[64]{0:T(128)S(1)}, s32[64]{0:T(128)}, u32[]{:S(2)}) copy-start(s32[64]{0:T(128)} %param.8) | copy-start | bytes 772
  6.6 17.7 %copy-start = (bf16[4,2,384,384]{3,2,1,0:T(8,128)(2,1)S(1)}, bf16[4,2,384,384]{3,2,1,0:T(8,128)(2,1)}, u32[]{:S(2)}) copy-start(bf16[4,2,384,384]{3,2,1,0:T(8,128)(2,1)} %param.9) | copy-start | bytes 7077892
  7.8 15.6 %all-to-all-start = ((bf16[2,2,128,384]{3,1,0,2:T(2,128)(2,1)}), bf16[2,2,128,384]{3,1,0,2:T(2,128)(2,1)S(1)}, u32[]{:S(2)}, u32[]{:S(2)}) async-start(bf16[2,2,128,384]{3,1,0,2:T(2,128)(2,1)} %copy.86), calls=%async_computation | async-start | bytes 786432 | tf_op jit(solution)/shard_map/all_to_all | solution.py:54
  32.6 3.1 %copy-start.3 = (bf16[4,32,384]{2,1,0:T(8,128)(2,1)}, bf16[4,32,384]{2,1,0:T(8,128)(2,1)S(1)}, u32[]{:S(2)}) copy-start(bf16[4,32,384]{2,1,0:T(8,128)(2,1)S(1)} %fusion.64) | copy-start | bytes 294916
  37.6 2.0 %copy-start.1 = (bf16[1,32,4,16,24]{1,4,0,2,3:T(8,128)(2,1)S(1)}, bf16[1,32,4,16,24]{1,4,0,2,3:T(8,128)(2,1)}, u32[]{:S(2)}) copy-start(bf16[1,32,4,16,24]{1,4,0,2,3:T(8,128)(2,1)} %copy.101) | copy-start | bytes 294916
  37.6 2.0 %copy-start.2 = (bf16[1,32,4,16,24]{1,4,0,2,3:T(8,128)(2,1)S(1)}, bf16[1,32,4,16,24]{1,4,0,2,3:T(8,128)(2,1)}, u32[]{:S(2)}) copy-start(bf16[1,32,4,16,24]{1,4,0,2,3:T(8,128)(2,1)} %copy.100) | copy-start | bytes 294916
  39.7 1.1 copy-start.4
  47.0 34.3 %all-to-all-start.2 = ((bf16[16,9,384,24]{2,3,1,0:T(8,128)(2,1)}), bf16[16,9,384,24]{2,3,1,0:T(8,128)(2,1)S(1)}, u32[]{:S(2)}, u32[]{:S(2)}) async-start(bf16[16,9,384,24]{2,3,1,0:T(8,128)(2,1)} %copy.102), calls=%async_computation.2 | async-start | bytes 5308416 | tf_op jit(solution)/shard_map/all_to_all | solution.py:101
  81.2 21.2 %all-to-all-start.1 = ((bf16[32,8,384]{2,1,0:T(8,128)(2,1)}), bf16[32,8,384]{2,1,0:T(8,128)(2,1)}, u32[]{:S(2)}, u32[]{:S(2)}) async-start(bf16[32,8,384]{2,1,0:T(8,128)(2,1)} %copy.93), calls=%async_computation.1 | async-start | bytes 393216 | tf_op jit(solution)/shard_map/all_to_all | solution.py:77
  102.4 44.4 %all-to-all-start.3 = ((f32[32,1,2592]{2,1,0:T(1,128)}), f32[32,1,2592]{2,1,0:T(1,128)S(1)}, u32[]{:S(2)}, u32[]{:S(2)}) async-start(f32[32,1,2592]{2,1,0:T(1,128)} %reshape.463), calls=%async_computation.3 | async-start | bytes 688128 | tf_op jit(solution)/shard_map/all_to_all | solution.py:106

commit v4 on v3

--- a/solution.py
+++ b/solution.py
@@ -3,7 +3,7 @@
 import jax
 import jax.numpy as jnp
 from jax import lax
-from jax.sharding import PartitionSpec as P
+from jax.sharding import Mesh, PartitionSpec as P
 
 GRID = 32
 
@@ -38,7 +38,6 @@
 def local(output_grad, layer_input, counts, bin_order, inverse_factor):
     slot_count, channels, pixels = output_grad.shape
     freq_devices = lax.axis_size("freq")
-    data_devices = lax.axis_size("dp")
     bins_local = inverse_factor.shape[0]
     total_bins = bin_order.shape[0]
     live_mask = (jnp.arange(slot_count, dtype=jnp.int32) < counts[0]).astype(jnp.bfloat16)
@@ -89,36 +88,53 @@
     w_t = jnp.stack([cos_t * ur + sin_t * ui, cos_t * ui - sin_t * ur], axis=1).astype(jnp.bfloat16)
     y_all = jnp.stack([v_real, v_imag], axis=0).astype(jnp.bfloat16)
     taps = z_t.shape[0]
+    z_devices = lax.axis_size("z")
+    core_devices = lax.axis_size("c")
     col_share = channels // freq_devices
-    row_share = channels // data_devices
+    row_share = channels // (z_devices * core_devices)
+    def core_major(x):
+        lead = x.shape[:-1]
+        x = x.reshape(lead + (z_devices, core_devices, row_share))
+        x = jnp.swapaxes(x, -3, -2)
+        return x.reshape(lead + (core_devices, z_devices * row_share))
+
+    z_rows = core_major(z_t)
+    y_rows = core_major(y_all)
     y_cols = y_all.reshape(2, image_rows, bins_local, freq_devices, col_share)
     w_cols = w_t.reshape(taps, 2, image_rows, bins_local, freq_devices, col_share)
-    first = jnp.einsum("teibr,eibfc->ftrc", z_t, y_cols, preferred_element_type=f32)
-    second = jnp.einsum("eibr,teibfc->ftrc", y_all, w_cols, preferred_element_type=f32)
-    gram_scale = 1.0 / math.sqrt(data_devices * freq_devices * slot_count)
+    first = jnp.einsum("teibCr,eibfk->Cftrk", z_rows, y_cols, preferred_element_type=f32)
+    second = jnp.einsum("eibCr,teibfk->Cftrk", y_rows, w_cols, preferred_element_type=f32)
+    gram_scale = 1.0 / math.sqrt(z_devices * core_devices * freq_devices * slot_count)
     tap_scale = 2.0 * gram_scale / math.sqrt(total_bins)
-    col_pieces = ((second - first) * tap_scale).astype(jnp.bfloat16)
+    chip_pieces = (second - first) * tap_scale
+    chip_pieces = lax.all_to_all(chip_pieces, "c", split_axis=0, concat_axis=0, tiled=True)
+    col_pieces = jnp.sum(chip_pieces, axis=0).astype(jnp.bfloat16)
     col_pieces = lax.all_to_all(col_pieces, "freq", split_axis=0, concat_axis=0, tiled=True)
-    col_sum = jnp.sum(col_pieces.astype(f32), axis=0)
+    row_pieces = jnp.sum(col_pieces.astype(f32), axis=0)
     row_pieces = jnp.transpose(
-        col_sum.reshape(taps, data_devices, row_share, col_share), (1, 0, 2, 3)
+        row_pieces.reshape(taps, z_devices, row_share, col_share), (1, 0, 2, 3)
     )
-    row_pieces = lax.all_to_all(row_pieces, "dp", split_axis=0, concat_axis=0, tiled=True)
+    row_pieces = lax.all_to_all(row_pieces, "z", split_axis=0, concat_axis=0, tiled=True)
     tap_grad = jnp.sum(row_pieces, axis=0)
     return (returned, tap_grad)
 
 
 def solution(mesh):
+    cores = 2
+    chips = Mesh(
+        mesh.devices.reshape(mesh.shape["dp"] // cores, cores, mesh.shape["freq"]),
+        ("z", "c", "freq"),
+    )
     return jax.shard_map(
         local,
-        mesh=mesh,
+        mesh=chips,
         in_specs=(
-            P(("dp", "freq"), None, None),
-            P(("dp", "freq"), None, None),
-            P(("dp", "freq")),
+            P(("z", "c", "freq"), None, None),
+            P(("z", "c", "freq"), None, None),
+            P(("z", "c", "freq")),
             P(),
             P("freq", None, None, None),
         ),
-        out_specs=(P(("dp", "freq"), None, None), P(None, "dp", "freq")),
+        out_specs=(P(("z", "c", "freq"), None, None), P(None, ("z", "c"), "freq")),
         check_vma=False,
     )

time: 151 us -> 188 us (1.25); the launches traced: 151 us -> 185 us
  other arithmetic: 8.46 us -> 33 us
  waiting for transfers between devices: 61.6 us -> 46.4 us
  blocking collectives: 0 us -> 14.2 us
  matrix products: 13 us -> 26.2 us
  starting transfers between devices: 38.3 us -> 28.9 us
  local copies, waits for them, and re-layouts: 27.7 us -> 34 us
    another operation x2 -> x3, other arithmetic: 2.74 us -> 21.9 us  [the longest x1 11.9 us: local(): jnp.stack([cos_t * ur - sin_t * ui, cos_t * ui + sin_t * ur], axis=1)]
    all_to_all x0 -> x1, blocking collectives: none -> 14.2 us  [local(): lax.all_to_all(chip_pieces, 'c', split_axis=0, concat_axis=0, tiled=True)]
    all_to_all x1, waiting for transfers between devices: 24.2 us -> 11.5 us  [local(): lax.all_to_all(row_pieces, 'z', split_axis=0, concat_axis=0, tiled=True)]
    dot_general x8, matrix products: 4.61 us -> 10.5 us  [mm(): return jnp.einsum(eq, x, p, preferred_element_type=f32)]
    dot_general x2, matrix products: 5.51 us -> 11.3 us  [the longest x1 6.44 us: local(): jnp.einsum('eibCr,teibfk->Cftrk', y_rows, w_cols, preferred_element_type=...]
    all_to_all x1, waiting for transfers between devices: 29.6 us -> 23.9 us  [local(): lax.all_to_all(col_pieces, 'freq', split_axis=0, concat_axis=0, tiled=True)]
    all_to_all x1, starting transfers between devices: 18.5 us -> 13.9 us  [local(): lax.all_to_all(row_pieces, 'z', split_axis=0, concat_axis=0, tiled=True)]
    all_to_all x1, starting transfers between devices: 8.43 us -> 3.78 us  [local(): lax.all_to_all(back_both, 'freq', split_axis=0, concat_axis=1, tiled=True)]
  transfers between devices with their start and end apart: 4 -> 4, of which waited for: 3 -> 4; matrix products, arithmetic and copies ran while one was open for 10% -> 4% of each run, Pallas kernels for 0% -> 0%
where the time goes in v4:
time: 188 us; the launch traced here: 185 us
  waiting for transfers between devices  46.4 us (25%)
  local copies, waits for them, and re-layouts  34 us (18%)
  other arithmetic  33 us (18%)
  starting transfers between devices  28.9 us (15%)
  matrix products  26.2 us (14%)
  blocking collectives  14.2 us (8%)
    all_to_all x1, waiting for transfers between devices, local(): lax.all_to_all(col_pieces, 'freq', split_axis=0, concat_axis=0, tiled=True)  23.9 us
    all_to_all x1, blocking collectives, local(): lax.all_to_all(chip_pieces, 'c', split_axis=0, concat_axis=0, tiled=True)  14.2 us
    all_to_all x1, starting transfers between devices, local(): lax.all_to_all(row_pieces, 'z', split_axis=0, concat_axis=0, tiled=True)  13.9 us
    another operation x1, other arithmetic, local(): jnp.stack([cos_t * ur - sin_t * ui, cos_t * ui + sin_t * ur], axis=1)  11.9 us
    all_to_all x1, waiting for transfers between devices, local(): lax.all_to_all(row_pieces, 'z', split_axis=0, concat_axis=0, tiled=True)  11.5 us
    dot_general x8, matrix products, mm(): return jnp.einsum(eq, x, p, preferred_element_type=f32)  10.5 us
    another operation x2, other arithmetic  10.1 us
    all_to_all x1, waiting for transfers between devices, local(): lax.all_to_all(both_spec, 'freq', split_axis=2, concat_axis=1, tiled=True)  7.74 us
  transfers between devices with their start and end apart: 4, of which 4 were waited for; matrix products, arithmetic and copies ran while one was open for 4% of the time, Pallas kernels for 0%

profile of v4, /device:TPU:1, one launch (start us, length us, event | category | flops | bytes accessed | tf_op | source)
XLA Modules:
  0.0 184.5 jit_solution(6487495534679786608)
XLA Ops:
  3.5 2.1 %fusion.32 = bf16[1,2,128,384]{3,2,1,0:T(8,128)(2,1)S(1)} fusion(bf16[1024,128,1]{0,1,2:T(8,128)(2,1)S(1)} %reshape.470, bf16[2,384,1024]{2,1,0:T(8,128)(2,1)} %param.6, bf16[2]{0:T(256)(128)(2,1)S(1)} %compare_convert_fusion), kind=kOutput, calls=%fused_computation.36 | convolution fusion | flops 204570624 | bytes 2031620 | tf_op jit(solution)/shard_map/scp,pk->skc/dot_general | solution.py:48
  5.7 2.3 %fusion.35 = bf16[1,2,128,384]{3,2,1,0:T(8,128)(2,1)S(1)} fusion(bf16[1024,128,1]{0,1,2:T(8,128)(2,1)S(1)} %reshape.470, bf16[2,384,1024]{2,1,0:T(8,128)(2,1)} %param.5, bf16[2]{0:T(256)(128)(2,1)S(1)} %compare_convert_fusion), kind=kOutput, calls=%fused_computation.37 | convolution fusion | flops 204570624 | bytes 2031620 | tf_op jit(solution)/shard_map/scp,pk->skc/dot_general | solution.py:48
  9.2 7.6 %all-to-all-start = ((bf16[2,2,128,384]{3,1,0,2:T(2,128)(2,1)}), bf16[2,2,128,384]{3,1,0,2:T(2,128)(2,1)S(1)}, u32[]{:S(2)}, u32[]{:S(2)}) async-start(bf16[2,2,128,384]{3,1,0,2:T(2,128)(2,1)} %copy.124), calls=%async_computation | async-start | bytes 786432 | tf_op jit(solution)/shard_map/all_to_all | solution.py:53
  17.0 7.7 %all-to-all-done = bf16[2,2,128,384]{3,1,0,2:T(2,128)(2,1)S(1)} async-done(((bf16[2,2,128,384]{3,1,0,2:T(2,128)(2,1)}), bf16[2,2,128,384]{3,1,0,2:T(2,128)(2,1)S(1)}, u32[]{:S(2)}, u32[]{:S(2)}) %all-to-all-start) | async-done | bytes 393248 | tf_op jit(solution)/shard_map/all_to_all | solution.py:53
  29.3 2.1 %copy.145 = f32[32,4,384]{0,1,2:T(4,128)} copy(f32[32,4,384]{2,0,1:T(8,128)} %fusion.47) | data formatting | bytes 393216 | tf_op jit(solution)/shard_map/sub | solution.py:68
  33.0 2.0 %fusion.41 = f32[32,4,384]{2,0,1:T(8,128)} fusion(f32[4,32,384]{2,1,0:T(8,128)} %fusion.16, bf16[4,2,384,384]{3,2,1,0:T(8,128)(2,1)S(1)} %copy-done, bf16[1,32,4,1,384]{4,0,3,2,1:T(2,128)(2,1)} %copy-done.7), kind=kOutput, calls=%fused_computation.39 | convolution fusion | flops 37797888 | bytes 1671168 | tf_op jit(solution)/shard_map/ibr,brc->ibc/dot_general | solution.py:65
  35.0 2.1 %copy.143 = f32[32,4,384]{0,1,2:T(4,128)} copy(f32[32,4,384]{2,0,1:T(8,128)} %fusion.41) | data formatting | bytes 393216 | tf_op jit(solution)/shard_map/add | solution.py:67
  37.0 2.6 %mul.332 = f32[32,4,16,24]{3,2,0,1:T(8,128)} reshape(f32[32,4,384]{2,0,1:T(8,128)} %fusion.41) | data formatting | bytes 393216 | tf_op jit(solution)/shard_map/mul | solution.py:88
  41.0 2.1 %fusion.12 = f32[4,32,384]{2,1,0:T(8,128)} fusion(bf16[4,2,384,384]{3,2,1,0:T(8,128)(2,1)S(1)} %copy-done, bf16[1,32,4,1,384]{4,0,3,2,1:T(2,128)(2,1)} %get-tuple-element.14), kind=kOutput, calls=%fused_computation.20 | convolution fusion | flops 37748736 | bytes 1474560 | tf_op jit(solution)/shard_map/ibk,bck->ibc/dot_general | solution.py:65
  50.9 2.5 %copy.146 = f32[32,4,16,2,12]{0,3,4,2,1:T(2,128)} copy(f32[32,4,16,2,12]{0,1,4,3,2:T(4,128)} %bitcast.153) | data formatting | bytes 393216 | tf_op jit(solution)/shard_map/mul | solution.py:88
  56.0 2.2 %copy.141 = bf16[1,32,4,16,24]{1,4,0,2,3:T(8,128)(2,1)} copy(bf16[1,32,4,16,24]{4,3,1,2,0:T(8,128)(2,1)} %stack.62) | data formatting | bytes 196608 | tf_op jit(solution)/shard_map/stack | solution.py:89
  61.7 7.8 %subtract_convert_fusion = (bf16[9,1,32,4,16,2,12]{2,5,6,4,3,1,0:T(2,128)(2,1)S(1)}, bf16[9,1,32,4,16,2,12]{2,5,6,4,3,1,0:T(2,128)(2,1)S(1)}) fusion(f32[32,4,16,2,12]{0,3,4,2,1:T(2,128)S(1)} %copy-done.2, f32[9,4]{1,0:T(8,128)S(1)} %get-tuple-element.21, f32[32,4,16,2,12]{0,3,4,2,1:T(2,128)S(1)} %copy-done.3, f32[9,4]{1,0:T(8,128)S(1)} %get-tuple-element.20), kind=kLoop, calls=%fused_computation.10 | loop fusion | flops 3538944 | bytes 2162976 | tf_op jit(solution)/shard_map/convert
  69.5 11.9 %pad_maximum_fusion = bf16[9,2,32,4,16,2,12]{2,5,6,4,3,1,0:T(2,128)(2,1)S(1)} fusion(bf16[9,1,32,4,16,2,12]{2,5,6,4,3,1,0:T(2,128)(2,1)S(1)} %get-tuple-element.13, bf16[9,1,32,4,16,2,12]{2,5,6,4,3,1,0:T(2,128)(2,1)S(1)} %get-tuple-element.12), kind=kLoop, calls=%fused_computation.4 | loop fusion | flops 884736 | bytes 3538944 | tf_op jit(solution)/shard_map/stack | solution.py:87
  81.5 2.2 %add_convert_fusion.1 = (bf16[9,1,32,4,16,24]{2,5,1,3,4,0:T(8,128)(2,1)S(1)}, bf16[9,1,32,4,16,24]{2,5,1,3,4,0:T(8,128)(2,1)S(1)}) fusion(f32[32,4,16,24]{0,3,1,2:T(8,128)S(1)} %copy.134, f32[9,4]{1,0:T(8,128)S(1)} %get-tuple-element.21, f32[32,4,16,24]{0,3,1,2:T(8,128)S(1)} %copy.133, f32[9,4]{1,0:T(8,128)S(1)} %get-tuple-element.20), kind=kLoop, calls=%fused_computation.12 | loop fusion | flops 3538944 | bytes 2162976 | tf_op jit(solution)/shard_map/convert.10
  83.7 4.8 %fusion.4 = f32[16,24,9,2,192,1,1]{4,1,6,5,3,0,2:T(8,128)} fusion(bf16[9,2,32,4,2,192,1]{2,4,5,3,1,0,6:T(2,128)(2,1)S(1)} %bitcast.150, bf16[1,32,4,16,24]{1,4,0,2,3:T(8,128)(2,1)S(1)} %copy-done.11, bf16[1,32,4,16,24]{1,4,0,2,3:T(8,128)(2,1)S(1)} %copy-done.12), kind=kOutput, calls=%fused_computation.7 | convolution fusion | flops 679870464 | bytes 7274496 | tf_op jit(solution)/shard_map/teibCr,eibfk->Cftrk/dot_general | solution.py:105
  88.5 6.4 %fusion.3 = f32[2,16,9,192,24]{3,4,0,1,2:T(8,128)S(1)} fusion(f32[16,24,9,2,192,1,1]{4,1,6,5,3,0,2:T(8,128)} %fusion.4, bf16[9,1,32,4,16,24]{2,5,1,3,4,0:T(8,128)(2,1)S(1)} %get-tuple-element.11, bf16[9,1,32,4,16,24]{2,5,1,3,4,0:T(8,128)(2,1)S(1)} %get-tuple-element.10, bf16[2,32,4,2,192,1,1]{1,3,4,2,0,6,5:T(2,128)(2,1)S(1)} %bitcast.158), kind=kOutput, calls=%fused_computation.6 | convolution fusion | flops 685670400 | bytes 12582912 | tf_op jit(solution)/shard_map/eibCr,teibfk->Cftrk/dot_general | solution.py:106
  95.7 14.2 %all_to_all.48 = f32[2,16,9,192,24]{3,4,1,2,0:T(8,128)} all-to-all(f32[2,16,9,192,24]{3,4,1,2,0:T(8,128)S(1)} %copy.148), channel_id=1, replica_groups=mesh['z'=16,'c'=2,'freq'=16] {'c'}, dimensions={0} | all-to-all | bytes 10616832 | tf_op jit(solution)/shard_map/all_to_all | solution.py:110
  109.9 4.0 %reduce_sum.27 = bf16[16,9,192,24]{2,3,0,1:T(8,128)(2,1)S(1)} reduce(f32[2,16,9,192,24]{3,4,1,2,0:T(8,128)} %all_to_all.48, f32[]{:T(128)} %constant.121.clone.1), dimensions={0}, to_apply=%region_0.1 | reduce | flops 663552 | bytes 6635524 | tf_op jit(solution)/shard_map/reduce_sum | solution.py:111
  115.4 3.7 %all-to-all-start.3 = ((bf16[16,9,192,24]{2,3,1,0:T(8,128)(2,1)}), bf16[16,9,192,24]{2,3,1,0:T(8,128)(2,1)S(1)}, u32[]{:S(2)}, u32[]{:S(2)}) async-start(bf16[16,9,192,24]{2,3,1,0:T(8,128)(2,1)} %copy.150), calls=%async_computation.3 | async-start | bytes 3538944 | tf_op jit(solution)/shard_map/all_to_all | solution.py:112
  120.9 23.9 %all-to-all-done.3 = bf16[16,9,192,24]{2,3,1,0:T(8,128)(2,1)S(1)} async-done(((bf16[16,9,192,24]{2,3,1,0:T(8,128)(2,1)}), bf16[16,9,192,24]{2,3,1,0:T(8,128)(2,1)S(1)}, u32[]{:S(2)}, u32[]{:S(2)}) %all-to-all-start.3) | async-done | bytes 1327136 | tf_op jit(solution)/shard_map/all_to_all | solution.py:112
  144.8 3.8 %all-to-all-start.1 = ((bf16[32,8,384]{2,1,0:T(8,128)(2,1)}), bf16[32,8,384]{2,1,0:T(8,128)(2,1)S(1)}, u32[]{:S(2)}, u32[]{:S(2)}) async-start(bf16[32,8,384]{2,1,0:T(8,128)(2,1)} %copy.131), calls=%async_computation.1 | async-start | bytes 393216 | tf_op jit(solution)/shard_map/all_to_all | solution.py:76
  152.4 3.2 %all-to-all-done.1 = bf16[32,8,384]{2,1,0:T(8,128)(2,1)S(1)} async-done(((bf16[32,8,384]{2,1,0:T(8,128)(2,1)}), bf16[32,8,384]{2,1,0:T(8,128)(2,1)S(1)}, u32[]{:S(2)}, u32[]{:S(2)}) %all-to-all-start.1) | async-done | bytes 196640 | tf_op jit(solution)/shard_map/all_to_all | solution.py:76
  155.6 13.9 %all-to-all-start.4 = ((f32[16,1,2592]{2,1,0:T(1,128)}), f32[16,1,2592]{2,1,0:T(1,128)S(1)}, u32[]{:S(2)}, u32[]{:S(2)}) async-start(f32[16,1,2592]{2,1,0:T(1,128)} %reshape.478), calls=%async_computation.4 | async-start | bytes 344064 | tf_op jit(solution)/shard_map/all_to_all | solution.py:117
  170.2 11.5 %all-to-all-done.4 = f32[16,1,2592]{2,1,0:T(1,128)S(1)} async-done(((f32[16,1,2592]{2,1,0:T(1,128)}), f32[16,1,2592]{2,1,0:T(1,128)S(1)}, u32[]{:S(2)}, u32[]{:S(2)}) %all-to-all-start.4) | async-done | bytes 165920 | tf_op jit(solution)/shard_map/all_to_all | solution.py:117
  (76 shorter events, 36.0 us)
Async XLA Ops:
  3.5 13.3 %copy-start.13 = (s32[64]{0:T(128)S(1)}, s32[64]{0:T(128)}, u32[]{:S(2)}) copy-start(s32[64]{0:T(128)} %param.8) | copy-start | bytes 772
  5.7 21.4 %copy-start = (bf16[4,2,384,384]{3,2,1,0:T(8,128)(2,1)S(1)}, bf16[4,2,384,384]{3,2,1,0:T(8,128)(2,1)}, u32[]{:S(2)}) copy-start(bf16[4,2,384,384]{3,2,1,0:T(8,128)(2,1)} %param.9) | copy-start | bytes 7077892
  9.2 15.6 %all-to-all-start = ((bf16[2,2,128,384]{3,1,0,2:T(2,128)(2,1)}), bf16[2,2,128,384]{3,1,0,2:T(2,128)(2,1)S(1)}, u32[]{:S(2)}, u32[]{:S(2)}) async-start(bf16[2,2,128,384]{3,1,0,2:T(2,128)(2,1)} %copy.124), calls=%async_computation | async-start | bytes 786432 | tf_op jit(solution)/shard_map/all_to_all | solution.py:53
  26.4 0.7 copy-start.7
  26.4 1.9 %copy-start.9 = (bf16[1,32,4,1,384]{4,0,3,2,1:T(2,128)(2,1)}, bf16[1,32,4,1,384]{4,0,3,2,1:T(2,128)(2,1)S(1)}, u32[]{:S(2)}) copy-start(bf16[1,32,4,1,384]{4,0,3,2,1:T(2,128)(2,1)S(1)} %get-tuple-element.16) | copy-start | bytes 294916
  48.4 5.0 %copy-start.4 = (f32[32,4,384]{0,1,2:T(4,128)S(1)}, f32[32,4,384]{0,1,2:T(4,128)}, u32[]{:S(2)}) copy-start(f32[32,4,384]{0,1,2:T(4,128)} %copy.143) | copy-start | bytes 589828
  48.4 6.3 %copy-start.6 = (bf16[1,32,4,16,24]{4,3,1,2,0:T(8,128)(2,1)S(1)}, bf16[1,32,4,16,24]{4,3,1,2,0:T(8,128)(2,1)}, u32[]{:S(2)}) copy-start(bf16[1,32,4,16,24]{4,3,1,2,0:T(8,128)(2,1)} %stack.63) | copy-start | bytes 294916
  50.9 7.8 %copy-start.1 = (f32[32,4,16,24]{3,2,0,1:T(8,128)S(1)}, f32[32,4,16,24]{3,2,0,1:T(8,128)}, u32[]{:S(2)}) copy-start(f32[32,4,16,24]{3,2,0,1:T(8,128)} %mul.332) | copy-start | bytes 589828
  58.7 3.0 %copy-start.2 = (f32[32,4,16,2,12]{0,3,4,2,1:T(2,128)S(1)}, f32[32,4,16,2,12]{0,3,4,2,1:T(2,128)}, u32[]{:S(2)}) copy-start(f32[32,4,16,2,12]{0,3,4,2,1:T(2,128)} %copy.146) | copy-start | bytes 589828
  59.2 2.5 %copy-start.3 = (f32[32,4,16,2,12]{0,3,4,2,1:T(2,128)S(1)}, f32[32,4,16,2,12]{0,3,4,2,1:T(2,128)}, u32[]{:S(2)}) copy-start(f32[32,4,16,2,12]{0,3,4,2,1:T(2,128)} %copy.144) | copy-start | bytes 589828
  81.4 2.3 %copy-start.11 = (bf16[1,32,4,16,24]{1,4,0,2,3:T(8,128)(2,1)S(1)}, bf16[1,32,4,16,24]{1,4,0,2,3:T(8,128)(2,1)}, u32[]{:S(2)}) copy-start(bf16[1,32,4,16,24]{1,4,0,2,3:T(8,128)(2,1)} %copy.142) | copy-start | bytes 294916
  81.4 2.3 %copy-start.12 = (bf16[1,32,4,16,24]{1,4,0,2,3:T(8,128)(2,1)S(1)}, bf16[1,32,4,16,24]{1,4,0,2,3:T(8,128)(2,1)}, u32[]{:S(2)}) copy-start(bf16[1,32,4,16,24]{1,4,0,2,3:T(8,128)(2,1)} %copy.141) | copy-start | bytes 294916
  114.0 5.1 %copy-start.10 = (bf16[1,32,4,1,384]{4,0,3,2,1:T(2,128)(2,1)S(1)}, bf16[1,32,4,1,384]{4,0,3,2,1:T(2,128)(2,1)}, u32[]{:S(2)}) copy-start(bf16[1,32,4,1,384]{4,0,3,2,1:T(2,128)(2,1)} %copy-done.9) | copy-start | bytes 294916
  114.0 6.1 %copy-start.5 = (f32[32,4,384]{2,0,1:T(8,128)S(1)}, f32[32,4,384]{2,0,1:T(8,128)}, u32[]{:S(2)}) copy-start(f32[32,4,384]{2,0,1:T(8,128)} %fusion.41) | copy-start | bytes 589828
  114.0 6.1 %copy-start.8 = (bf16[1,32,4,1,384]{4,0,3,2,1:T(2,128)(2,1)S(1)}, bf16[1,32,4,1,384]{4,0,3,2,1:T(2,128)(2,1)}, u32[]{:S(2)}) copy-start(bf16[1,32,4,1,384]{4,0,3,2,1:T(2,128)(2,1)} %copy-done.7) | copy-start | bytes 294916
  115.4 29.5 %all-to-all-start.3 = ((bf16[16,9,192,24]{2,3,1,0:T(8,128)(2,1)}), bf16[16,9,192,24]{2,3,1,0:T(8,128)(2,1)S(1)}, u32[]{:S(2)}, u32[]{:S(2)}) async-start(bf16[16,9,192,24]{2,3,1,0:T(8,128)(2,1)} %copy.150), calls=%async_computation.3 | async-start | bytes 3538944 | tf_op jit(solution)/shard_map/all_to_all | solution.py:112
  144.8 10.8 %all-to-all-start.1 = ((bf16[32,8,384]{2,1,0:T(8,128)(2,1)}), bf16[32,8,384]{2,1,0:T(8,128)(2,1)S(1)}, u32[]{:S(2)}, u32[]{:S(2)}) async-start(bf16[32,8,384]{2,1,0:T(8,128)(2,1)} %copy.131), calls=%async_computation.1 | async-start | bytes 393216 | tf_op jit(solution)/shard_map/all_to_all | solution.py:76
  155.6 26.1 %all-to-all-start.4 = ((f32[16,1,2592]{2,1,0:T(1,128)}), f32[16,1,2592]{2,1,0:T(1,128)S(1)}, u32[]{:S(2)}, u32[]{:S(2)}) async-start(f32[16,1,2592]{2,1,0:T(1,128)} %reshape.478), calls=%async_computation.4 | async-start | bytes 344064 | tf_op jit(solution)/shard_map/all_to_all | solution.py:117

commit v5 on v3

--- a/solution.py
+++ b/solution.py
@@ -100,11 +100,18 @@
     col_pieces = ((second - first) * tap_scale).astype(jnp.bfloat16)
     col_pieces = lax.all_to_all(col_pieces, "freq", split_axis=0, concat_axis=0, tiled=True)
     col_sum = jnp.sum(col_pieces.astype(f32), axis=0)
-    row_pieces = jnp.transpose(
-        col_sum.reshape(taps, data_devices, row_share, col_share), (1, 0, 2, 3)
-    )
-    row_pieces = lax.all_to_all(row_pieces, "dp", split_axis=0, concat_axis=0, tiled=True)
-    tap_grad = jnp.sum(row_pieces, axis=0)
+    dp_index = lax.axis_index("dp")
+    blocks = col_sum.reshape(taps, data_devices, row_share, col_share)
+    step = 1
+    while step < data_devices:
+        blocks = blocks.reshape(taps, -1, 2, row_share, col_share)
+        high = (dp_index // step) % 2 == 1
+        keep = jnp.where(high, blocks[:, :, 1], blocks[:, :, 0])
+        send = jnp.where(high, blocks[:, :, 0], blocks[:, :, 1])
+        pairs = [(i, i ^ step) for i in range(data_devices)]
+        blocks = keep + lax.ppermute(send, "dp", pairs)
+        step *= 2
+    tap_grad = blocks.reshape(taps, row_share, col_share)
     return (returned, tap_grad)
 
 

time: 151 us -> 175 us (1.16)
  starting transfers between devices: 38.3 us -> 55.2 us
  waiting for transfers between devices: 61.6 us -> 64.9 us
  local copies, waits for them, and re-layouts: 27.7 us -> 30.1 us
    ppermute x0 -> x5, starting transfers between devices: none -> 39.7 us  [local(): blocks = keep + lax.ppermute(send, 'dp', pairs)]
    ppermute x0 -> x5, waiting for transfers between devices: none -> 26.9 us  [local(): blocks = keep + lax.ppermute(send, 'dp', pairs)]
    all_to_all x1 -> x0, waiting for transfers between devices: 24.2 us -> none  [local(): lax.all_to_all(row_pieces, 'dp', split_axis=0, concat_axis=0, tiled=True)]
    all_to_all x1 -> x0, starting transfers between devices: 18.5 us -> none  [local(): lax.all_to_all(row_pieces, 'dp', split_axis=0, concat_axis=0, tiled=True)]
    another operation x0 -> x1, local copies, waits for them, and re-layouts: none -> 6.03 us  [local(): blocks = blocks.reshape(taps, -1, 2, row_share, col_share)]
    slice x0 -> x1, local copies, waits for them, and re-layouts: none -> 5.23 us  [local(): keep = jnp.where(high, blocks[:, :, 1], blocks[:, :, 0])]
    reshape x1 -> x0, local copies, waits for them, and re-layouts: 4.81 us -> none  [local(): col_sum.reshape(taps, data_devices, row_share, col_share)]
    all_to_all x1, starting transfers between devices: 8.43 us -> 3.92 us  [local(): lax.all_to_all(back_both, 'freq', split_axis=0, concat_axis=1, tiled=True)]
  transfers between devices with their start and end apart: 4 -> 8, of which waited for: 3 -> 7; matrix products, arithmetic and copies ran while one was open for 10% -> 1% of each run, Pallas kernels for 0% -> 0%
where the time goes in v5:
time: 175 us; the launch traced here: 174 us
  waiting for transfers between devices  64.9 us (37%)
  starting transfers between devices  55.2 us (32%)
  local copies, waits for them, and re-layouts  30.1 us (17%)
  matrix products  13.6 us (8%)
  other arithmetic  8.51 us (5%)
  between operations  2.03 us (1%)
    ppermute x5, starting transfers between devices, local(): blocks = keep + lax.ppermute(send, 'dp', pairs)  39.7 us
    all_to_all x1, waiting for transfers between devices, local(): lax.all_to_all(col_pieces, 'freq', split_axis=0, concat_axis=0, tiled=True)  30.3 us
    ppermute x5, waiting for transfers between devices, local(): blocks = keep + lax.ppermute(send, 'dp', pairs)  26.9 us
    all_to_all x1, waiting for transfers between devices, local(): lax.all_to_all(both_spec, 'freq', split_axis=2, concat_axis=1, tiled=True)  7.74 us
    all_to_all x1, starting transfers between devices, local(): lax.all_to_all(both_spec, 'freq', split_axis=2, concat_axis=1, tiled=True)  7.59 us
    unnamed x41, local copies, waits for them, and re-layouts  6.24 us
    another operation x1, local copies, waits for them, and re-layouts, local(): blocks = blocks.reshape(taps, -1, 2, row_share, col_share)  6.03 us
    dot_general x8, matrix products, mm(): return jnp.einsum(eq, x, p, preferred_element_type=f32)  5.26 us
  transfers between devices with their start and end apart: 8, of which 7 were waited for; matrix products, arithmetic and copies ran while one was open for 1% of the time, Pallas kernels for 0%

profile of v5, /device:TPU:1, one launch (start us, length us, event | category | flops | bytes accessed | tf_op | source)
XLA Modules:
  0.0 174.4 jit_solution(13077841316834949004)
XLA Ops:
  4.4 2.1 %fusion.40 = bf16[1,2,128,384]{3,2,1,0:T(8,128)(2,1)S(1)} fusion(bf16[1024,128,1]{0,1,2:T(8,128)(2,1)S(1)} %reshape.532, bf16[2,384,1024]{2,1,0:T(8,128)(2,1)} %param.5, bf16[2]{0:T(256)(128)(2,1)S(1)} %compare_convert_fusion), kind=kOutput, calls=%fused_computation.39 | convolution fusion | flops 204570624 | bytes 2031620 | tf_op jit(solution)/shard_map/scp,pk->skc/dot_general | solution.py:49
  7.8 7.6 %all-to-all-start = ((bf16[2,2,128,384]{3,1,0,2:T(2,128)(2,1)}), bf16[2,2,128,384]{3,1,0,2:T(2,128)(2,1)S(1)}, u32[]{:S(2)}, u32[]{:S(2)}) async-start(bf16[2,2,128,384]{3,1,0,2:T(2,128)(2,1)} %copy.168), calls=%async_computation | async-start | bytes 786432 | tf_op jit(solution)/shard_map/all_to_all | solution.py:54
  15.6 7.7 %all-to-all-done = bf16[2,2,128,384]{3,1,0,2:T(2,128)(2,1)S(1)} async-done(((bf16[2,2,128,384]{3,1,0,2:T(2,128)(2,1)}), bf16[2,2,128,384]{3,1,0,2:T(2,128)(2,1)S(1)}, u32[]{:S(2)}, u32[]{:S(2)}) %all-to-all-start) | async-done | bytes 393248 | tf_op jit(solution)/shard_map/all_to_all | solution.py:54
  28.3 1.6 stack.67
  31.2 1.4 fusion.64
  37.6 2.0 %add_convert_fusion = (bf16[9,1,32,4,16,24]{2,5,1,3,4,0:T(8,128)(2,1)S(1)}, bf16[9,1,32,4,16,24]{2,5,1,3,4,0:T(8,128)(2,1)S(1)}) fusion(f32[32,4,16,24]{0,3,1,2:T(8,128)S(1)} %copy.178, f32[9,4]{1,0:T(8,128)S(1)} %get-tuple-element.26, f32[32,4,16,24]{0,3,1,2:T(8,128)S(1)} %copy.177, f32[9,4]{1,0:T(8,128)S(1)} %get-tuple-element.25), kind=kLoop, calls=%fused_computation.5 | loop fusion | flops 3538944 | bytes 2162976 | tf_op jit(solution)/shard_map/convert.10
  40.7 4.4 %fusion.5 = bf16[16,9,384,24]{2,3,0,1:T(8,128)(2,1)S(1)} fusion(f32[16,24,9,384,1,1]{3,1,5,4,0,2:T(8,128)S(1)} %fusion.8, bf16[9,1,32,4,16,24]{2,5,1,3,4,0:T(8,128)(2,1)S(1)} %get-tuple-element.7, bf16[9,1,32,4,16,24]{2,5,1,3,4,0:T(8,128)(2,1)S(1)} %get-tuple-element.6, bf16[1,32,4,384]{3,1,2,0:T(8,128)(2,1)S(1)} %bitcast.201, ...), kind=kOutput, calls=%fused_computation.8 | convolution fusion | flops 684441600 | bytes 9928704 | tf_op jit(solution)/shard_map/eibr,teibfc->ftrc/dot_general | solution.py:97
  45.2 1.8 %copy.184 = bf16[16,9,384,24]{2,3,1,0:T(8,128)(2,1)} copy(bf16[16,9,384,24]{2,3,0,1:T(8,128)(2,1)S(1)} %fusion.5) | data formatting | bytes 5308416 | tf_op jit(solution)/shard_map/convert_element_type | solution.py:100
  46.9 4.0 %all-to-all-start.2 = ((bf16[16,9,384,24]{2,3,1,0:T(8,128)(2,1)}), bf16[16,9,384,24]{2,3,1,0:T(8,128)(2,1)S(1)}, u32[]{:S(2)}, u32[]{:S(2)}) async-start(bf16[16,9,384,24]{2,3,1,0:T(8,128)(2,1)} %copy.184), calls=%async_computation.2 | async-start | bytes 5308416 | tf_op jit(solution)/shard_map/all_to_all | solution.py:101
  50.9 30.3 %all-to-all-done.2 = bf16[16,9,384,24]{2,3,1,0:T(8,128)(2,1)S(1)} async-done(((bf16[16,9,384,24]{2,3,1,0:T(8,128)(2,1)}), bf16[16,9,384,24]{2,3,1,0:T(8,128)(2,1)S(1)}, u32[]{:S(2)}, u32[]{:S(2)}) %all-to-all-start.2) | async-done | bytes 2654240 | tf_op jit(solution)/shard_map/all_to_all | solution.py:101
  82.3 6.0 %reshape_reshape.3 = f32[9,16,2,12,24]{3,2,1,4,0:T(2,128)S(1)} reshape(f32[9,384,24]{1,2,0:T(8,128)} %convert_reduce_fusion) | data formatting | bytes 663552 | tf_op jit(solution)/shard_map/reshape;reshape | solution.py:107
  88.4 5.2 %fusion.107 = (f32[9,16,1,12,24]{3,2,1,4,0:T(1,128)}, f32[9,16,1,12,24]{3,2,1,4,0:T(1,128)}) fusion(f32[9,16,2,12,24]{3,2,1,4,0:T(2,128)S(1)} %reshape_reshape.3), kind=kLoop, calls=%fused_computation.138 | loop fusion | bytes 663552 | tf_op jit(solution)/shard_map/slice | solution.py:109
  93.6 3.9 %copy.217 = f32[9,16,1,12,24]{4,1,3,0,2:T(8,128)S(1)} copy(f32[9,16,1,12,24]{3,2,1,4,0:T(1,128)} %get-tuple-element.5) | data formatting | bytes 331776
  97.5 1.5 copy.216
  99.2 8.7 %collective-permute-start = (f32[9,16,12,24]{3,1,2,0:T(8,128)S(1)}, f32[9,16,12,24]{3,1,2,0:T(8,128)S(1)}, u32[]{:S(2)}, u32[]{:S(2)}) collective-permute-start(f32[9,16,12,24]{3,1,2,0:T(8,128)S(1)} %select_bitcast_fusion), channel_id=1, source_target_pairs={{0,16},{16,0},{32,48},{48,32},{64,80},{80,64},{96,112},{112,96},{1... | collective-permute-start | bytes 497672 | tf_op jit(solution)/shard_map/ppermute | solution.py:112
  108.0 1.9 %collective-permute-done = f32[9,16,12,24]{3,1,2,0:T(8,128)S(1)} collective-permute-done((f32[9,16,12,24]{3,1,2,0:T(8,128)S(1)}, f32[9,16,12,24]{3,1,2,0:T(8,128)S(1)}, u32[]{:S(2)}, u32[]{:S(2)}) %collective-permute-start) | collective-permute-done | bytes 165920 | tf_op jit(solution)/shard_map/ppermute | solution.py:112
  111.2 4.0 %collective-permute-start.1 = (f32[9,8,12,24]{3,1,2,0:T(8,128)S(1)}, f32[9,8,12,24]{3,1,2,0:T(8,128)S(1)}, u32[]{:S(2)}, u32[]{:S(2)}) collective-permute-start(f32[9,8,12,24]{3,1,2,0:T(8,128)S(1)} %bitcast.197), channel_id=1, source_target_pairs={{0,32},{16,48},{32,0},{48,16},{64,96},{80,112},{96,64},{112,80},{1... | collective-permute-start | bytes 248840 | tf_op jit(solution)/shard_map/ppermute | solution.py:112
  115.2 10.2 %collective-permute-done.1 = f32[9,8,12,24]{3,1,2,0:T(8,128)S(1)} collective-permute-done((f32[9,8,12,24]{3,1,2,0:T(8,128)S(1)}, f32[9,8,12,24]{3,1,2,0:T(8,128)S(1)}, u32[]{:S(2)}, u32[]{:S(2)}) %collective-permute-start.1) | collective-permute-done | bytes 82976 | tf_op jit(solution)/shard_map/ppermute | solution.py:112
  125.9 4.8 %collective-permute-start.2 = (f32[9,4,12,24]{3,1,2,0:T(4,128)S(1)}, f32[9,4,12,24]{3,1,2,0:T(4,128)S(1)}, u32[]{:S(2)}, u32[]{:S(2)}) collective-permute-start(f32[9,4,12,24]{3,1,2,0:T(4,128)S(1)} %bitcast.204), channel_id=1, source_target_pairs={{0,64},{16,80},{32,96},{48,112},{64,0},{80,16},{96,32},{112,48},{1... | collective-permute-start | bytes 124424 | tf_op jit(solution)/shard_map/ppermute | solution.py:112
  130.7 9.6 %collective-permute-done.2 = f32[9,4,12,24]{3,1,2,0:T(4,128)S(1)} collective-permute-done((f32[9,4,12,24]{3,1,2,0:T(4,128)S(1)}, f32[9,4,12,24]{3,1,2,0:T(4,128)S(1)}, u32[]{:S(2)}, u32[]{:S(2)}) %collective-permute-start.2) | collective-permute-done | bytes 41504 | tf_op jit(solution)/shard_map/ppermute | solution.py:112
  140.6 8.8 %collective-permute-start.3 = (f32[9,2,12,24]{3,1,2,0:T(2,128)S(1)}, f32[9,2,12,24]{3,1,2,0:T(2,128)S(1)}, u32[]{:S(2)}, u32[]{:S(2)}) collective-permute-start(f32[9,2,12,24]{3,1,2,0:T(2,128)S(1)} %bitcast.206), channel_id=1, source_target_pairs={{0,128},{16,144},{32,160},{48,176},{64,192},{80,208},{96,224},{112... | collective-permute-start | bytes 62216 | tf_op jit(solution)/shard_map/ppermute | solution.py:112
  150.2 3.9 %all-to-all-start.1 = ((bf16[32,8,384]{2,1,0:T(8,128)(2,1)}), bf16[32,8,384]{2,1,0:T(8,128)(2,1)S(1)}, u32[]{:S(2)}, u32[]{:S(2)}) async-start(bf16[32,8,384]{2,1,0:T(8,128)(2,1)} %copy.175), calls=%async_computation.1 | async-start | bytes 393216 | tf_op jit(solution)/shard_map/all_to_all | solution.py:77
  154.1 4.4 %collective-permute-done.3 = f32[9,2,12,24]{3,1,2,0:T(2,128)S(1)} collective-permute-done((f32[9,2,12,24]{3,1,2,0:T(2,128)S(1)}, f32[9,2,12,24]{3,1,2,0:T(2,128)S(1)}, u32[]{:S(2)}, u32[]{:S(2)}) %collective-permute-start.3) | collective-permute-done | bytes 20768 | tf_op jit(solution)/shard_map/ppermute | solution.py:112
  158.7 13.4 %collective-permute-start.4 = (f32[9,1,12,24]{3,1,2,0:T(1,128)S(1)}, f32[9,1,12,24]{3,1,2,0:T(1,128)S(1)}, u32[]{:S(2)}, u32[]{:S(2)}) collective-permute-start(f32[9,1,12,24]{3,1,2,0:T(1,128)S(1)} %fusion.90), channel_id=1, source_target_pairs={{0,256},{16,272},{32,288},{48,304},{64,320},{80,336},{96,352},{112... | collective-permute-start | bytes 31112 | tf_op jit(solution)/shard_map/ppermute | solution.py:112
  (90 shorter events, 23.1 us)
Async XLA Ops:
  0.6 3.0 %copy-start.18 = (bf16[2,384,1024]{2,1,0:T(8,128)(2,1)S(1)}, bf16[2,384,1024]{2,1,0:T(8,128)(2,1)}, u32[]{:S(2)}) copy-start(bf16[2,384,1024]{2,1,0:T(8,128)(2,1)} %param.6) | copy-start | bytes 4718596
  4.4 11.0 %copy-start.17 = (s32[64]{0:T(128)S(1)}, s32[64]{0:T(128)}, u32[]{:S(2)}) copy-start(s32[64]{0:T(128)} %param.8) | copy-start | bytes 772
  6.6 17.7 %copy-start = (bf16[4,2,384,384]{3,2,1,0:T(8,128)(2,1)S(1)}, bf16[4,2,384,384]{3,2,1,0:T(8,128)(2,1)}, u32[]{:S(2)}) copy-start(bf16[4,2,384,384]{3,2,1,0:T(8,128)(2,1)} %param.9) | copy-start | bytes 7077892
  7.8 15.6 %all-to-all-start = ((bf16[2,2,128,384]{3,1,0,2:T(2,128)(2,1)}), bf16[2,2,128,384]{3,1,0,2:T(2,128)(2,1)S(1)}, u32[]{:S(2)}, u32[]{:S(2)}) async-start(bf16[2,2,128,384]{3,1,0,2:T(2,128)(2,1)} %copy.168), calls=%async_computation | async-start | bytes 786432 | tf_op jit(solution)/shard_map/all_to_all | solution.py:54
  24.3 1.3 copy-start.6
  24.3 1.3 copy-start.10
  25.2 11.6 %copy-start.4 = (f32[32,4,384]{2,0,1:T(8,128)}, f32[32,4,384]{2,0,1:T(8,128)S(1)}, u32[]{:S(2)}) copy-start(f32[32,4,384]{2,0,1:T(8,128)S(1)} %fusion.52) | copy-start | bytes 589828
  25.5 11.3 %copy-start.2 = (f32[32,4,384]{2,0,1:T(8,128)}, f32[32,4,384]{2,0,1:T(8,128)S(1)}, u32[]{:S(2)}) copy-start(f32[32,4,384]{2,0,1:T(8,128)S(1)} %fusion.46) | copy-start | bytes 589828
  26.0 5.2 %copy-start.11 = (bf16[1,32,4,1,384]{4,0,3,2,1:T(2,128)(2,1)S(1)}, bf16[1,32,4,1,384]{4,0,3,2,1:T(2,128)(2,1)}, u32[]{:S(2)}) copy-start(bf16[1,32,4,1,384]{4,0,3,2,1:T(2,128)(2,1)} %copy-done.10) | copy-start | bytes 294916
  32.5 3.1 %copy-start.15 = (bf16[4,32,384]{2,1,0:T(8,128)(2,1)}, bf16[4,32,384]{2,1,0:T(8,128)(2,1)S(1)}, u32[]{:S(2)}) copy-start(bf16[4,32,384]{2,1,0:T(8,128)(2,1)S(1)} %fusion.64) | copy-start | bytes 294916
  37.5 2.0 %copy-start.12 = (bf16[1,32,4,16,24]{1,4,0,2,3:T(8,128)(2,1)S(1)}, bf16[1,32,4,16,24]{1,4,0,2,3:T(8,128)(2,1)}, u32[]{:S(2)}) copy-start(bf16[1,32,4,16,24]{1,4,0,2,3:T(8,128)(2,1)} %copy.183) | copy-start | bytes 294916
  37.5 2.0 %copy-start.13 = (bf16[1,32,4,16,24]{1,4,0,2,3:T(8,128)(2,1)S(1)}, bf16[1,32,4,16,24]{1,4,0,2,3:T(8,128)(2,1)}, u32[]{:S(2)}) copy-start(bf16[1,32,4,16,24]{1,4,0,2,3:T(8,128)(2,1)} %copy.182) | copy-start | bytes 294916
  46.9 34.3 %all-to-all-start.2 = ((bf16[16,9,384,24]{2,3,1,0:T(8,128)(2,1)}), bf16[16,9,384,24]{2,3,1,0:T(8,128)(2,1)S(1)}, u32[]{:S(2)}, u32[]{:S(2)}) async-start(bf16[16,9,384,24]{2,3,1,0:T(8,128)(2,1)} %copy.184), calls=%async_computation.2 | async-start | bytes 5308416 | tf_op jit(solution)/shard_map/all_to_all | solution.py:101
  93.6 4.0 %copy-start.1 = (f32[9,16,1,12,24]{3,2,1,4,0:T(1,128)S(1)}, f32[9,16,1,12,24]{3,2,1,4,0:T(1,128)}, u32[]{:S(2)}) copy-start(f32[9,16,1,12,24]{3,2,1,4,0:T(1,128)} %get-tuple-element.4) | copy-start | bytes 497668
  99.2 10.8 %collective-permute-start = (f32[9,16,12,24]{3,1,2,0:T(8,128)S(1)}, f32[9,16,12,24]{3,1,2,0:T(8,128)S(1)}, u32[]{:S(2)}, u32[]{:S(2)}) collective-permute-start(f32[9,16,12,24]{3,1,2,0:T(8,128)S(1)} %select_bitcast_fusion), channel_id=1, source_target_pairs={{0,16},{16,0},{32,48},{48,32},{64,80},{80,64},{96,112},{112,96},{1... | collective-permute-start | bytes 497672 | tf_op jit(solution)/shard_map/ppermute | solution.py:112
  108.0 7.2 %copy-start.5 = (f32[32,4,384]{2,0,1:T(8,128)S(1)}, f32[32,4,384]{2,0,1:T(8,128)}, u32[]{:S(2)}) copy-start(f32[32,4,384]{2,0,1:T(8,128)} %copy-done.4) | copy-start | bytes 589828
  108.0 7.2 %copy-start.9 = (bf16[1,32,4,1,384]{4,0,3,2,1:T(2,128)(2,1)S(1)}, bf16[1,32,4,1,384]{4,0,3,2,1:T(2,128)(2,1)}, u32[]{:S(2)}) copy-start(bf16[1,32,4,1,384]{4,0,3,2,1:T(2,128)(2,1)} %copy-done.8) | copy-start | bytes 294916
  110.1 20.6 %copy-start.3 = (f32[32,4,384]{2,0,1:T(8,128)S(1)}, f32[32,4,384]{2,0,1:T(8,128)}, u32[]{:S(2)}) copy-start(f32[32,4,384]{2,0,1:T(8,128)} %copy-done.2) | copy-start | bytes 589828
  110.1 20.6 %copy-start.7 = (bf16[1,32,4,1,384]{4,0,3,2,1:T(2,128)(2,1)S(1)}, bf16[1,32,4,1,384]{4,0,3,2,1:T(2,128)(2,1)}, u32[]{:S(2)}) copy-start(bf16[1,32,4,1,384]{4,0,3,2,1:T(2,128)(2,1)} %copy-done.6) | copy-start | bytes 294916
  111.2 14.2 %collective-permute-start.1 = (f32[9,8,12,24]{3,1,2,0:T(8,128)S(1)}, f32[9,8,12,24]{3,1,2,0:T(8,128)S(1)}, u32[]{:S(2)}, u32[]{:S(2)}) collective-permute-start(f32[9,8,12,24]{3,1,2,0:T(8,128)S(1)} %bitcast.197), channel_id=1, source_target_pairs={{0,32},{16,48},{32,0},{48,16},{64,96},{80,112},{96,64},{112,80},{1... | collective-permute-start | bytes 248840 | tf_op jit(solution)/shard_map/ppermute | solution.py:112
  125.9 14.4 %collective-permute-start.2 = (f32[9,4,12,24]{3,1,2,0:T(4,128)S(1)}, f32[9,4,12,24]{3,1,2,0:T(4,128)S(1)}, u32[]{:S(2)}, u32[]{:S(2)}) collective-permute-start(f32[9,4,12,24]{3,1,2,0:T(4,128)S(1)} %bitcast.204), channel_id=1, source_target_pairs={{0,64},{16,80},{32,96},{48,112},{64,0},{80,16},{96,32},{112,48},{1... | collective-permute-start | bytes 124424 | tf_op jit(solution)/shard_map/ppermute | solution.py:112
  140.6 17.9 %collective-permute-start.3 = (f32[9,2,12,24]{3,1,2,0:T(2,128)S(1)}, f32[9,2,12,24]{3,1,2,0:T(2,128)S(1)}, u32[]{:S(2)}, u32[]{:S(2)}) collective-permute-start(f32[9,2,12,24]{3,1,2,0:T(2,128)S(1)} %bitcast.206), channel_id=1, source_target_pairs={{0,128},{16,144},{32,160},{48,176},{64,192},{80,208},{96,224},{112... | collective-permute-start | bytes 62216 | tf_op jit(solution)/shard_map/ppermute | solution.py:112
  150.2 21.9 %all-to-all-start.1 = ((bf16[32,8,384]{2,1,0:T(8,128)(2,1)}), bf16[32,8,384]{2,1,0:T(8,128)(2,1)S(1)}, u32[]{:S(2)}, u32[]{:S(2)}) async-start(bf16[32,8,384]{2,1,0:T(8,128)(2,1)} %copy.175), calls=%async_computation.1 | async-start | bytes 393216 | tf_op jit(solution)/shard_map/all_to_all | solution.py:77
  158.7 14.9 %collective-permute-start.4 = (f32[9,1,12,24]{3,1,2,0:T(1,128)S(1)}, f32[9,1,12,24]{3,1,2,0:T(1,128)S(1)}, u32[]{:S(2)}, u32[]{:S(2)}) collective-permute-start(f32[9,1,12,24]{3,1,2,0:T(1,128)S(1)} %fusion.90), channel_id=1, source_target_pairs={{0,256},{16,272},{32,288},{48,304},{64,320},{80,336},{96,352},{112... | collective-permute-start | bytes 31112 | tf_op jit(solution)/shard_map/ppermute | solution.py:112
  (3 other events, 2.9 us)

commit v6 on v3

--- a/solution.py
+++ b/solution.py
@@ -3,7 +3,7 @@
 import jax
 import jax.numpy as jnp
 from jax import lax
-from jax.sharding import PartitionSpec as P
+from jax.sharding import Mesh, PartitionSpec as P
 
 GRID = 32
 
@@ -38,7 +38,7 @@
 def local(output_grad, layer_input, counts, bin_order, inverse_factor):
     slot_count, channels, pixels = output_grad.shape
     freq_devices = lax.axis_size("freq")
-    data_devices = lax.axis_size("dp")
+    data_devices = lax.axis_size("z") * lax.axis_size("c")
     bins_local = inverse_factor.shape[0]
     total_bins = bin_order.shape[0]
     live_mask = (jnp.arange(slot_count, dtype=jnp.int32) < counts[0]).astype(jnp.bfloat16)
@@ -100,25 +100,34 @@
     col_pieces = ((second - first) * tap_scale).astype(jnp.bfloat16)
     col_pieces = lax.all_to_all(col_pieces, "freq", split_axis=0, concat_axis=0, tiled=True)
     col_sum = jnp.sum(col_pieces.astype(f32), axis=0)
+    z_devices = lax.axis_size("z")
+    core_devices = lax.axis_size("c")
     row_pieces = jnp.transpose(
-        col_sum.reshape(taps, data_devices, row_share, col_share), (1, 0, 2, 3)
+        col_sum.reshape(taps, z_devices, core_devices, row_share, col_share), (2, 1, 0, 3, 4)
     )
-    row_pieces = lax.all_to_all(row_pieces, "dp", split_axis=0, concat_axis=0, tiled=True)
+    row_pieces = lax.all_to_all(row_pieces, "c", split_axis=0, concat_axis=0, tiled=True)
+    row_pieces = jnp.sum(row_pieces, axis=0)
+    row_pieces = lax.all_to_all(row_pieces, "z", split_axis=0, concat_axis=0, tiled=True)
     tap_grad = jnp.sum(row_pieces, axis=0)
     return (returned, tap_grad)
 
 
 def solution(mesh):
+    cores = 2
+    chips = Mesh(
+        mesh.devices.reshape(mesh.shape["dp"] // cores, cores, mesh.shape["freq"]),
+        ("z", "c", "freq"),
+    )
     return jax.shard_map(
         local,
-        mesh=mesh,
+        mesh=chips,
         in_specs=(
-            P(("dp", "freq"), None, None),
-            P(("dp", "freq"), None, None),
-            P(("dp", "freq")),
+            P(("z", "c", "freq"), None, None),
+            P(("z", "c", "freq"), None, None),
+            P(("z", "c", "freq")),
             P(),
             P("freq", None, None, None),
         ),
-        out_specs=(P(("dp", "freq"), None, None), P(None, "dp", "freq")),
+        out_specs=(P(("z", "c", "freq"), None, None), P(None, ("z", "c"), "freq")),
         check_vma=False,
     )

time: 151 us -> 150 us (level)
  the two profiles are of different devices: /device:TPU:1 before, /device:TPU:32 now
where the time goes in v6:
time: 150 us; the launch traced here: 149 us
  waiting for transfers between devices  60.2 us (40%)
  starting transfers between devices  30.4 us (20%)
  local copies, waits for them, and re-layouts  30 us (20%)
  matrix products  13 us (9%)
  other arithmetic  9.8 us (7%)
  blocking collectives  4 us (3%)
  between operations  1.68 us (1%)
    all_to_all x1, waiting for transfers between devices, local(): lax.all_to_all(col_pieces, 'freq', split_axis=0, concat_axis=0, tiled=True)  34 us
    all_to_all x1, starting transfers between devices, local(): lax.all_to_all(row_pieces, 'z', split_axis=0, concat_axis=0, tiled=True)  15.2 us
    all_to_all x1, waiting for transfers between devices, local(): lax.all_to_all(row_pieces, 'z', split_axis=0, concat_axis=0, tiled=True)  13.8 us
    all_to_all x1, waiting for transfers between devices, local(): lax.all_to_all(both_spec, 'freq', split_axis=2, concat_axis=1, tiled=True)  9.56 us
    all_to_all x1, starting transfers between devices, local(): lax.all_to_all(both_spec, 'freq', split_axis=2, concat_axis=1, tiled=True)  7.04 us
    reshape x1, local copies, waits for them, and re-layouts, local(): col_sum.reshape(taps, z_devices, core_devices, row_share, col_share)  6.03 us
    unnamed x18, local copies, waits for them, and re-layouts  5.72 us
    another operation x4, local copies, waits for them, and re-layouts, local(): y_all = jnp.stack([v_real, v_imag], axis=0).astype(jnp.bfloat16)  5.67 us
  transfers between devices with their start and end apart: 4, of which 4 were waited for; matrix products, arithmetic and copies ran while one was open for 5% of the time, Pallas kernels for 0%

profile of v6, /device:TPU:32, one launch (start us, length us, event | category | flops | bytes accessed | tf_op | source)
XLA Modules:
  0.0 149.0 jit_solution(16743570371700284100)
XLA Ops:
  4.4 2.1 %fusion.40 = bf16[1,2,128,384]{3,2,1,0:T(8,128)(2,1)S(1)} fusion(bf16[1024,128,1]{0,1,2:T(8,128)(2,1)S(1)} %reshape.456, bf16[2,384,1024]{2,1,0:T(8,128)(2,1)} %param.5, bf16[2]{0:T(256)(128)(2,1)S(1)} %compare_convert_fusion), kind=kOutput, calls=%fused_computation.39 | convolution fusion | flops 204570624 | bytes 2031620 | tf_op jit(solution)/shard_map/scp,pk->skc/dot_general | solution.py:49
  7.8 7.0 %all-to-all-start = ((bf16[2,2,128,384]{3,1,0,2:T(2,128)(2,1)}), bf16[2,2,128,384]{3,1,0,2:T(2,128)(2,1)S(1)}, u32[]{:S(2)}, u32[]{:S(2)}) async-start(bf16[2,2,128,384]{3,1,0,2:T(2,128)(2,1)} %copy.109), calls=%async_computation | async-start | bytes 786432 | tf_op jit(solution)/shard_map/all_to_all | solution.py:54
  15.1 9.6 %all-to-all-done = bf16[2,2,128,384]{3,1,0,2:T(2,128)(2,1)S(1)} async-done(((bf16[2,2,128,384]{3,1,0,2:T(2,128)(2,1)}), bf16[2,2,128,384]{3,1,0,2:T(2,128)(2,1)S(1)}, u32[]{:S(2)}, u32[]{:S(2)}) %all-to-all-start) | async-done | bytes 393248 | tf_op jit(solution)/shard_map/all_to_all | solution.py:54
  27.1 1.2 fusion.17
  28.8 1.5 %stack.67 = bf16[1,32,4,16,24]{4,3,1,2,0:T(8,128)(2,1)} reshape(bf16[32,4,384]{2,0,1:T(8,128)(2,1)S(1)} %bitcast.145) | data formatting | bytes 196608 | tf_op jit(solution)/shard_map/stack | solution.py:90
  30.3 2.2 %copy.124 = bf16[1,32,4,16,24]{1,4,0,2,3:T(8,128)(2,1)} copy(bf16[1,32,4,16,24]{4,3,1,2,0:T(8,128)(2,1)} %stack.67) | data formatting | bytes 196608 | tf_op jit(solution)/shard_map/stack | solution.py:90
  32.5 1.4 fusion.64
  34.6 1.3 copy.123
  38.9 2.0 %add_convert_fusion = (bf16[9,1,32,4,16,24]{2,5,1,3,4,0:T(8,128)(2,1)S(1)}, bf16[9,1,32,4,16,24]{2,5,1,3,4,0:T(8,128)(2,1)S(1)}) fusion(f32[32,4,16,24]{0,3,1,2:T(8,128)S(1)} %copy.119, f32[9,4]{1,0:T(8,128)S(1)} %get-tuple-element.21, f32[32,4,16,24]{0,3,1,2:T(8,128)S(1)} %copy.118, f32[9,4]{1,0:T(8,128)S(1)} %get-tuple-element.20), kind=kLoop, calls=%fused_computation.5 | loop fusion | flops 3538944 | bytes 2162976 | tf_op jit(solution)/shard_map/convert.10
  42.0 4.4 %fusion.5 = bf16[16,9,384,24]{2,3,0,1:T(8,128)(2,1)S(1)} fusion(f32[16,24,9,384,1,1]{3,1,5,4,0,2:T(8,128)S(1)} %fusion.8, bf16[9,1,32,4,16,24]{2,5,1,3,4,0:T(8,128)(2,1)S(1)} %get-tuple-element.11, bf16[9,1,32,4,16,24]{2,5,1,3,4,0:T(8,128)(2,1)S(1)} %get-tuple-element.10, bf16[1,32,4,384]{3,1,2,0:T(8,128)(2,1)S(1)} %bitcast.146, ...), kind=kOutput, calls=%fused_computation.8 | convolution fusion | flops 684441600 | bytes 9928704 | tf_op jit(solution)/shard_map/eibr,teibfc->ftrc/dot_general | solution.py:97
  46.4 1.8 %copy.125 = bf16[16,9,384,24]{2,3,1,0:T(8,128)(2,1)} copy(bf16[16,9,384,24]{2,3,0,1:T(8,128)(2,1)S(1)} %fusion.5) | data formatting | bytes 5308416 | tf_op jit(solution)/shard_map/convert_element_type | solution.py:100
  48.2 4.0 %all-to-all-start.2 = ((bf16[16,9,384,24]{2,3,1,0:T(8,128)(2,1)}), bf16[16,9,384,24]{2,3,1,0:T(8,128)(2,1)S(1)}, u32[]{:S(2)}, u32[]{:S(2)}) async-start(bf16[16,9,384,24]{2,3,1,0:T(8,128)(2,1)} %copy.125), calls=%async_computation.2 | async-start | bytes 5308416 | tf_op jit(solution)/shard_map/all_to_all | solution.py:101
  53.1 34.0 %all-to-all-done.2 = bf16[16,9,384,24]{2,3,1,0:T(8,128)(2,1)S(1)} async-done(((bf16[16,9,384,24]{2,3,1,0:T(8,128)(2,1)}), bf16[16,9,384,24]{2,3,1,0:T(8,128)(2,1)S(1)}, u32[]{:S(2)}, u32[]{:S(2)}) %all-to-all-start.2) | async-done | bytes 2654240 | tf_op jit(solution)/shard_map/all_to_all | solution.py:101
  88.2 6.0 %reshape.455 = f32[9,16,2,12,24]{3,2,1,4,0:T(2,128)S(1)} reshape(f32[9,384,24]{1,2,0:T(8,128)} %convert_reduce_fusion) | data formatting | bytes 663552 | tf_op jit(solution)/shard_map/reshape | solution.py:106
  94.2 3.9 %copy.126 = f32[2,16,9,12,24]{4,1,3,2,0:T(8,128)} copy(f32[2,16,9,12,24]{3,0,1,4,2:T(2,128)S(1)} %bitcast.139) | data formatting | bytes 663552 | tf_op jit(solution)/shard_map/transpose | solution.py:105
  98.1 2.5 %reshape.463 = f32[2,1,41472]{2,1,0:T(1,128)S(1)} reshape(f32[2,9,12,16,24]{4,3,2,1,0:T(8,128)} %bitcast.140) | data formatting | bytes 663552
  100.6 4.0 %all_to_all.48 = f32[2,1,41472]{2,1,0:T(1,128)S(1)} all-to-all(f32[2,1,41472]{2,1,0:T(1,128)S(1)} %reshape.463), channel_id=1, replica_groups=mesh['z'=16,'c'=2,'freq'=16] {'c'}, dimensions={0} | all-to-all | bytes 663552 | tf_op jit(solution)/shard_map/all_to_all | solution.py:108
  104.6 4.2 %all-to-all-start.1 = ((bf16[32,8,384]{2,1,0:T(8,128)(2,1)}), bf16[32,8,384]{2,1,0:T(8,128)(2,1)S(1)}, u32[]{:S(2)}, u32[]{:S(2)}) async-start(bf16[32,8,384]{2,1,0:T(8,128)(2,1)} %copy.116), calls=%async_computation.1 | async-start | bytes 393216 | tf_op jit(solution)/shard_map/all_to_all | solution.py:77
  109.3 1.7 %reduce = f32[2,41472]{1,0:T(2,128)S(1)} reduce(f32[2,1,41472]{2,1,0:T(1,128)S(1)} %all_to_all.48, f32[]{:T(128)} %broadcast.636), dimensions={1}, to_apply=%all_to_all.41.reduce_sub_computation | reduce | bytes 663556 | tf_op jit(solution)/shard_map/all_to_all | solution.py:108
  111.0 1.3 reshape.464
  112.8 1.3 reshape.465
  114.2 2.9 %all-to-all-done.1 = bf16[32,8,384]{2,1,0:T(8,128)(2,1)S(1)} async-done(((bf16[32,8,384]{2,1,0:T(8,128)(2,1)}), bf16[32,8,384]{2,1,0:T(8,128)(2,1)S(1)}, u32[]{:S(2)}, u32[]{:S(2)}) %all-to-all-start.1) | async-done | bytes 196640 | tf_op jit(solution)/shard_map/all_to_all | solution.py:77
  117.0 15.2 %all-to-all-start.4 = ((f32[16,1,2592]{2,1,0:T(1,128)}), f32[16,1,2592]{2,1,0:T(1,128)S(1)}, u32[]{:S(2)}, u32[]{:S(2)}) async-start(f32[16,1,2592]{2,1,0:T(1,128)} %reshape.465), calls=%async_computation.4 | async-start | bytes 344064 | tf_op jit(solution)/shard_map/all_to_all | solution.py:110
  132.9 13.8 %all-to-all-done.4 = f32[16,1,2592]{2,1,0:T(1,128)S(1)} async-done(((f32[16,1,2592]{2,1,0:T(1,128)}), f32[16,1,2592]{2,1,0:T(1,128)S(1)}, u32[]{:S(2)}, u32[]{:S(2)}) %all-to-all-start.4) | async-done | bytes 165920 | tf_op jit(solution)/shard_map/all_to_all | solution.py:110
  (56 shorter events, 18.1 us)
Async XLA Ops:
  0.6 3.0 %copy-start.6 = (bf16[2,384,1024]{2,1,0:T(8,128)(2,1)S(1)}, bf16[2,384,1024]{2,1,0:T(8,128)(2,1)}, u32[]{:S(2)}) copy-start(bf16[2,384,1024]{2,1,0:T(8,128)(2,1)} %param.6) | copy-start | bytes 4718596
  4.4 10.4 %copy-start.5 = (s32[64]{0:T(128)S(1)}, s32[64]{0:T(128)}, u32[]{:S(2)}) copy-start(s32[64]{0:T(128)} %param.8) | copy-start | bytes 772
  6.6 18.9 %copy-start = (bf16[4,2,384,384]{3,2,1,0:T(8,128)(2,1)S(1)}, bf16[4,2,384,384]{3,2,1,0:T(8,128)(2,1)}, u32[]{:S(2)}) copy-start(bf16[4,2,384,384]{3,2,1,0:T(8,128)(2,1)} %param.9) | copy-start | bytes 7077892
  7.8 16.9 %all-to-all-start = ((bf16[2,2,128,384]{3,1,0,2:T(2,128)(2,1)}), bf16[2,2,128,384]{3,1,0,2:T(2,128)(2,1)S(1)}, u32[]{:S(2)}, u32[]{:S(2)}) async-start(bf16[2,2,128,384]{3,1,0,2:T(2,128)(2,1)} %copy.109), calls=%async_computation | async-start | bytes 786432 | tf_op jit(solution)/shard_map/all_to_all | solution.py:54
  33.9 3.1 %copy-start.3 = (bf16[4,32,384]{2,1,0:T(8,128)(2,1)}, bf16[4,32,384]{2,1,0:T(8,128)(2,1)S(1)}, u32[]{:S(2)}) copy-start(bf16[4,32,384]{2,1,0:T(8,128)(2,1)S(1)} %fusion.64) | copy-start | bytes 294916
  38.8 2.0 %copy-start.1 = (bf16[1,32,4,16,24]{1,4,0,2,3:T(8,128)(2,1)S(1)}, bf16[1,32,4,16,24]{1,4,0,2,3:T(8,128)(2,1)}, u32[]{:S(2)}) copy-start(bf16[1,32,4,16,24]{1,4,0,2,3:T(8,128)(2,1)} %copy.124) | copy-start | bytes 294916
  38.8 2.0 %copy-start.2 = (bf16[1,32,4,16,24]{1,4,0,2,3:T(8,128)(2,1)S(1)}, bf16[1,32,4,16,24]{1,4,0,2,3:T(8,128)(2,1)}, u32[]{:S(2)}) copy-start(bf16[1,32,4,16,24]{1,4,0,2,3:T(8,128)(2,1)} %copy.123) | copy-start | bytes 294916
  40.9 1.1 copy-start.4
  48.2 38.8 %all-to-all-start.2 = ((bf16[16,9,384,24]{2,3,1,0:T(8,128)(2,1)}), bf16[16,9,384,24]{2,3,1,0:T(8,128)(2,1)S(1)}, u32[]{:S(2)}, u32[]{:S(2)}) async-start(bf16[16,9,384,24]{2,3,1,0:T(8,128)(2,1)} %copy.125), calls=%async_computation.2 | async-start | bytes 5308416 | tf_op jit(solution)/shard_map/all_to_all | solution.py:101
  104.6 12.4 %all-to-all-start.1 = ((bf16[32,8,384]{2,1,0:T(8,128)(2,1)}), bf16[32,8,384]{2,1,0:T(8,128)(2,1)S(1)}, u32[]{:S(2)}, u32[]{:S(2)}) async-start(bf16[32,8,384]{2,1,0:T(8,128)(2,1)} %copy.116), calls=%async_computation.1 | async-start | bytes 393216 | tf_op jit(solution)/shard_map/all_to_all | solution.py:77
  117.0 29.7 %all-to-all-start.4 = ((f32[16,1,2592]{2,1,0:T(1,128)}), f32[16,1,2592]{2,1,0:T(1,128)S(1)}, u32[]{:S(2)}, u32[]{:S(2)}) async-start(f32[16,1,2592]{2,1,0:T(1,128)} %reshape.465), calls=%async_computation.4 | async-start | bytes 344064 | tf_op jit(solution)/shard_map/all_to_all | solution.py:110

commit v7 on v6

--- a/solution.py
+++ b/solution.py
@@ -58,15 +58,18 @@
     grad_imag = parts[0, :, :, 1]
     input_real = parts[1, :, :, 0]
     input_imag = parts[1, :, :, 1]
-    factor_real = inverse_factor[:, 0]
-    factor_imag = inverse_factor[:, 1]
     f32 = jnp.float32
 
-    def mm(x, p, eq):
-        return jnp.einsum(eq, x, p, preferred_element_type=f32)
-
-    u_real = mm(grad_real, factor_real, "ibr,brc->ibc") + mm(grad_imag, factor_imag, "ibr,brc->ibc")
-    u_imag = mm(grad_imag, factor_real, "ibr,brc->ibc") - mm(grad_real, factor_imag, "ibr,brc->ibc")
+    u_lhs = jnp.stack(
+        [jnp.stack([grad_real, grad_imag], axis=2), jnp.stack([grad_imag, -grad_real], axis=2)]
+    )
+    v_lhs = jnp.stack(
+        [jnp.stack([input_real, -input_imag], axis=2), jnp.stack([input_imag, input_real], axis=2)]
+    )
+    u_both = jnp.einsum("eibpr,bprc->eibc", u_lhs, inverse_factor, preferred_element_type=f32)
+    v_both = jnp.einsum("eibpk,bpck->eibc", v_lhs, inverse_factor, preferred_element_type=f32)
+    u_real = u_both[0]
+    u_imag = u_both[1]
     back_real = 2.0 * u_real - grad_real.astype(f32)
     back_imag = 2.0 * u_imag - grad_imag.astype(f32)
     back_both = (
@@ -75,8 +78,6 @@
         .reshape(image_rows, 2 * bins_local, channels)
     )
     returned = lax.all_to_all(back_both, "freq", split_axis=0, concat_axis=1, tiled=True)
-    v_real = mm(input_real, factor_real, "ibk,bck->ibc") - mm(input_imag, factor_imag, "ibk,bck->ibc")
-    v_imag = mm(input_real, factor_imag, "ibk,bck->ibc") + mm(input_imag, factor_real, "ibk,bck->ibc")
     local_bins = lax.dynamic_slice_in_dim(
         bin_order, lax.axis_index("freq") * bins_local, bins_local
     )
@@ -87,7 +88,7 @@
     ui = u_imag[None]
     z_t = jnp.stack([cos_t * ur - sin_t * ui, cos_t * ui + sin_t * ur], axis=1).astype(jnp.bfloat16)
     w_t = jnp.stack([cos_t * ur + sin_t * ui, cos_t * ui - sin_t * ur], axis=1).astype(jnp.bfloat16)
-    y_all = jnp.stack([v_real, v_imag], axis=0).astype(jnp.bfloat16)
+    y_all = v_both.astype(jnp.bfloat16)
     taps = z_t.shape[0]
     col_share = channels // freq_devices
     row_share = channels // data_devices
@@ -99,16 +100,20 @@
     tap_scale = 2.0 * gram_scale / math.sqrt(total_bins)
     col_pieces = ((second - first) * tap_scale).astype(jnp.bfloat16)
     col_pieces = lax.all_to_all(col_pieces, "freq", split_axis=0, concat_axis=0, tiled=True)
-    col_sum = jnp.sum(col_pieces.astype(f32), axis=0)
     z_devices = lax.axis_size("z")
     core_devices = lax.axis_size("c")
-    row_pieces = jnp.transpose(
-        col_sum.reshape(taps, z_devices, core_devices, row_share, col_share), (2, 1, 0, 3, 4)
+    block = taps * row_share * col_share
+    col_sum = jnp.sum(
+        col_pieces.reshape(
+            freq_devices, taps, z_devices, core_devices, row_share, col_share
+        ).astype(f32),
+        axis=0,
     )
+    row_pieces = jnp.transpose(col_sum, (2, 1, 0, 3, 4)).reshape(core_devices, z_devices * block)
     row_pieces = lax.all_to_all(row_pieces, "c", split_axis=0, concat_axis=0, tiled=True)
-    row_pieces = jnp.sum(row_pieces, axis=0)
+    row_pieces = jnp.sum(row_pieces, axis=0).reshape(z_devices, block)
     row_pieces = lax.all_to_all(row_pieces, "z", split_axis=0, concat_axis=0, tiled=True)
-    tap_grad = jnp.sum(row_pieces, axis=0)
+    tap_grad = jnp.sum(row_pieces, axis=0).reshape(taps, row_share, col_share)
     return (returned, tap_grad)
 
 

time: 150 us -> 160 us (1.067)
  local copies, waits for them, and re-layouts: 30 us -> 35 us
  waiting for transfers between devices: 60.2 us -> 63.6 us
  other arithmetic: 9.8 us -> 11.8 us
    reduce_sum x1, local copies, waits for them, and re-layouts: 0.3 us -> 7.35 us  [local(): jnp.sum(col_pieces.reshape(freq_devices, taps, z_devices, core_devices, r...]
    another operation x5 -> x0, local copies, waits for them, and re-layouts: 5.69 us -> none  [the longest x4 5.67 us: local(): y_all = jnp.stack([v_real, v_imag], axis=0).astype(jnp.bfloat16)]
    unnamed x18, local copies, waits for them, and re-layouts: 5.72 us -> 0.76 us
    all_to_all x1, waiting for transfers between devices: 2.87 us -> 6.85 us  [local(): lax.all_to_all(back_both, 'freq', split_axis=0, concat_axis=1, tiled=True)]
    another operation x2 -> x5, other arithmetic: 2.74 us -> 6.13 us
    all_to_all x2 -> x0, other arithmetic: 2.71 us -> none  [the longest x1 1.67 us: local(): lax.all_to_all(row_pieces, 'c', split_axis=0, concat_axis=0, tiled=True)]
    dot_general x8 -> x2, matrix products: 4.61 us -> 2 us  [the longest x1 1.51 us: local(): jnp.einsum('eibpk,bpck->eibc', v_lhs, inverse_factor, preferred_element_t...]
    transpose x1, local copies, waits for them, and re-layouts: 3.88 us -> 6.13 us  [local(): jnp.transpose(col_sum, (2, 1, 0, 3, 4))]
  transfers between devices with their start and end apart: 4 -> 4, of which waited for: 4 -> 4; matrix products, arithmetic and copies ran while one was open for 5% -> 1% of each run, Pallas kernels for 0% -> 0%
where the time goes in v7:
time: 160 us; the launch traced here: 159 us
  waiting for transfers between devices  63.6 us (40%)
  local copies, waits for them, and re-layouts  35 us (22%)
  starting transfers between devices  31.2 us (20%)
  other arithmetic  11.8 us (7%)
  matrix products  11.8 us (7%)
  blocking collectives  4 us (2%)
  between operations  1.76 us (1%)
    all_to_all x1, waiting for transfers between devices, local(): lax.all_to_all(col_pieces, 'freq', split_axis=0, concat_axis=0, tiled=True)  33.5 us
    all_to_all x1, starting transfers between devices, local(): lax.all_to_all(row_pieces, 'z', split_axis=0, concat_axis=0, tiled=True)  15.2 us
    all_to_all x1, waiting for transfers between devices, local(): lax.all_to_all(row_pieces, 'z', split_axis=0, concat_axis=0, tiled=True)  13.8 us
    all_to_all x1, waiting for transfers between devices, local(): lax.all_to_all(both_spec, 'freq', split_axis=2, concat_axis=1, tiled=True)  9.56 us
    reduce_sum x1, local copies, waits for them, and re-layouts, local(): jnp.sum(col_pieces.reshape(freq_devices, taps, z_devices, core_devices, r...  7.35 us
    all_to_all x1, starting transfers between devices, local(): lax.all_to_all(both_spec, 'freq', split_axis=2, concat_axis=1, tiled=True)  7.05 us
    all_to_all x1, waiting for transfers between devices, local(): lax.all_to_all(back_both, 'freq', split_axis=0, concat_axis=1, tiled=True)  6.85 us
    transpose x1, local copies, waits for them, and re-layouts, local(): jnp.transpose(col_sum, (2, 1, 0, 3, 4))  6.13 us
  transfers between devices with their start and end apart: 4, of which 4 were waited for; matrix products, arithmetic and copies ran while one was open for 1% of the time, Pallas kernels for 0%

profile of v7, /device:TPU:32, one launch (start us, length us, event | category | flops | bytes accessed | tf_op | source)
XLA Modules:
  0.0 159.2 jit_solution(10928933710449577855)
XLA Ops:
  3.7 2.1 %fusion.34 = bf16[1,2,128,384]{3,2,1,0:T(8,128)(2,1)S(1)} fusion(bf16[1024,128,1]{0,1,2:T(8,128)(2,1)S(1)} %reshape.523, bf16[2,384,1024]{2,1,0:T(8,128)(2,1)} %param.6, bf16[2]{0:T(256)(128)(2,1)S(1)} %compare_convert_fusion), kind=kOutput, calls=%fused_computation.29 | convolution fusion | flops 204570624 | bytes 2031620 | tf_op jit(solution)/shard_map/scp,pk->skc/dot_general | solution.py:49
  5.8 2.1 %fusion.37 = bf16[1,2,128,384]{3,2,1,0:T(8,128)(2,1)S(1)} fusion(bf16[1024,128,1]{0,1,2:T(8,128)(2,1)S(1)} %reshape.523, bf16[2,384,1024]{2,1,0:T(8,128)(2,1)} %param.5, bf16[2]{0:T(256)(128)(2,1)S(1)} %compare_convert_fusion), kind=kOutput, calls=%fused_computation.30 | convolution fusion | flops 204570624 | bytes 2031620 | tf_op jit(solution)/shard_map/scp,pk->skc/dot_general | solution.py:49
  9.2 7.0 %all-to-all-start = ((bf16[2,2,128,384]{3,1,0,2:T(2,128)(2,1)}), bf16[2,2,128,384]{3,1,0,2:T(2,128)(2,1)S(1)}, u32[]{:S(2)}, u32[]{:S(2)}) async-start(bf16[2,2,128,384]{3,1,0,2:T(2,128)(2,1)} %copy.111), calls=%async_computation | async-start | bytes 786432 | tf_op jit(solution)/shard_map/all_to_all | solution.py:54
  16.5 9.6 %all-to-all-done = bf16[2,2,128,384]{3,1,0,2:T(2,128)(2,1)S(1)} async-done(((bf16[2,2,128,384]{3,1,0,2:T(2,128)(2,1)}), bf16[2,2,128,384]{3,1,0,2:T(2,128)(2,1)S(1)}, u32[]{:S(2)}, u32[]{:S(2)}) %all-to-all-start) | async-done | bytes 393248 | tf_op jit(solution)/shard_map/all_to_all | solution.py:54
  30.0 1.6 mul.350
  32.9 1.6 mul.354
  37.0 1.5 fusion.25
  38.5 2.4 %reshape.533 = bf16[2,32,4,16,24]{4,3,1,0,2:T(8,128)(2,1)S(1)} reshape(bf16[2,32,4,384]{3,1,0,2:T(8,128)(2,1)} %bitcast.136) | data formatting | bytes 393216 | tf_op jit(solution)/shard_map/reshape | solution.py:95
  40.9 1.6 %copy.126 = bf16[2,32,4,16,24]{1,4,0,2,3:T(8,128)(2,1)} copy(bf16[2,32,4,16,24]{4,3,1,0,2:T(8,128)(2,1)S(1)} %reshape.533) | data formatting | bytes 393216 | tf_op jit(solution)/shard_map/reshape | solution.py:95
  42.5 1.7 %subtract_convert_fusion.1 = (bf16[9,1,32,4,384]{4,2,1,3,0:T(8,128)(2,1)S(1)}, bf16[9,1,32,4,384]{4,2,1,3,0:T(8,128)(2,1)S(1)}) fusion(f32[32,4,384]{2,0,1:T(8,128)} %get-tuple-element.14, f32[9,4]{1,0:T(8,128)S(1)} %get-tuple-element.29, f32[32,4,384]{2,0,1:T(8,128)} %get-tuple-element.13, f32[9,4]{1,0:T(8,128)S(1)} %get-tuple-element.28), kind=kLoop, calls=%fused_computation.19 | loop fusion | flops 3538944 | bytes 2162976 | tf_op jit(solution)/shard_map/convert
  44.3 3.2 %add_convert_fusion = (bf16[9,1,32,4,16,24]{2,5,1,3,4,0:T(8,128)(2,1)S(1)}, bf16[9,1,32,4,16,24]{2,5,1,3,4,0:T(8,128)(2,1)S(1)}) fusion(f32[32,4,16,24]{0,3,1,2:T(8,128)} %copy.121, f32[9,4]{1,0:T(8,128)S(1)} %get-tuple-element.29, f32[32,4,16,24]{0,3,1,2:T(8,128)} %copy.120, f32[9,4]{1,0:T(8,128)S(1)} %get-tuple-element.28), kind=kLoop, calls=%fused_computation.5 | loop fusion | flops 3538944 | bytes 2162976 | tf_op jit(solution)/shard_map/convert.2
  48.6 4.4 %fusion.5 = bf16[16,9,384,24]{2,3,0,1:T(8,128)(2,1)S(1)} fusion(f32[16,24,9,384,1,1]{3,1,5,4,0,2:T(8,128)S(1)} %fusion.12, bf16[9,1,32,4,16,24]{2,5,1,3,4,0:T(8,128)(2,1)S(1)} %get-tuple-element.9, bf16[9,1,32,4,16,24]{2,5,1,3,4,0:T(8,128)(2,1)S(1)} %get-tuple-element.8, bf16[4,2,32,384]{3,2,1,0:T(8,128)(2,1)S(1)} %copy-done.6), kind=kOutput, calls=%fused_computation.8 | convolution fusion | flops 684343296 | bytes 9928704 | tf_op jit(solution)/shard_map/eibr,teibfc->ftrc/dot_general | solution.py:98
  53.1 1.8 %copy.127 = bf16[16,9,384,24]{2,3,1,0:T(8,128)(2,1)} copy(bf16[16,9,384,24]{2,3,0,1:T(8,128)(2,1)S(1)} %fusion.5) | data formatting | bytes 5308416 | tf_op jit(solution)/shard_map/convert_element_type | solution.py:101
  54.9 4.8 %all-to-all-start.2 = ((bf16[16,9,384,24]{2,3,1,0:T(8,128)(2,1)}), bf16[16,9,384,24]{2,3,1,0:T(8,128)(2,1)}, u32[]{:S(2)}, u32[]{:S(2)}) async-start(bf16[16,9,384,24]{2,3,1,0:T(8,128)(2,1)} %copy.127), calls=%async_computation.2 | async-start | bytes 5308416 | tf_op jit(solution)/shard_map/all_to_all | solution.py:102
  60.6 33.5 %all-to-all-done.2 = bf16[16,9,384,24]{2,3,1,0:T(8,128)(2,1)} async-done(((bf16[16,9,384,24]{2,3,1,0:T(8,128)(2,1)}), bf16[16,9,384,24]{2,3,1,0:T(8,128)(2,1)}, u32[]{:S(2)}, u32[]{:S(2)}) %all-to-all-start.2) | async-done | bytes 2654240 | tf_op jit(solution)/shard_map/all_to_all | solution.py:102
  94.0 2.2 %convert_reduce_fusion = f32[9,384,24]{1,2,0:T(8,128)S(1)} fusion(bf16[16,9,384,24]{2,3,1,0:T(8,128)(2,1)} %all-to-all-done.2), kind=kLoop, calls=%fused_computation.9 | loop fusion | flops 2571264 | bytes 2985984 | tf_op jit(solution)/shard_map/reduce_sum | solution.py:106
  96.2 7.4 %reduce_sum.30 = f32[9,16,2,12,24]{3,2,1,4,0:T(2,128)} reshape(f32[9,384,24]{1,2,0:T(8,128)S(1)} %convert_reduce_fusion) | data formatting | bytes 663552 | tf_op jit(solution)/shard_map/reduce_sum | solution.py:106
  103.6 6.1 %copy.128 = f32[2,16,9,12,24]{4,3,2,1,0:T(8,128)} copy(f32[2,16,9,12,24]{3,0,1,4,2:T(2,128)} %bitcast.133) | data formatting | bytes 663552 | tf_op jit(solution)/shard_map/transpose | solution.py:112
  109.7 2.6 %all_to_all.51 = f32[2,1,41472]{2,1,0:T(1,128)S(1)} reshape(f32[2,16,9,12,24]{4,3,2,1,0:T(8,128)} %copy.128) | data formatting | bytes 663552 | tf_op jit(solution)/shard_map/all_to_all | solution.py:113
  112.3 4.0 %all_to_all.57 = f32[2,1,41472]{2,1,0:T(1,128)S(1)} all-to-all(f32[2,1,41472]{2,1,0:T(1,128)S(1)} %all_to_all.51), channel_id=1, replica_groups=mesh['z'=16,'c'=2,'freq'=16] {'c'}, dimensions={0} | all-to-all | bytes 663552 | tf_op jit(solution)/shard_map/all_to_all | solution.py:113
  116.3 4.1 %all-to-all-start.1 = ((bf16[32,8,384]{2,1,0:T(8,128)(2,1)}), bf16[32,8,384]{2,1,0:T(8,128)(2,1)S(1)}, u32[]{:S(2)}, u32[]{:S(2)}) async-start(bf16[32,8,384]{2,1,0:T(8,128)(2,1)} %copy.118), calls=%async_computation.1 | async-start | bytes 393216 | tf_op jit(solution)/shard_map/all_to_all | solution.py:80
  121.8 6.8 %all-to-all-done.1 = bf16[32,8,384]{2,1,0:T(8,128)(2,1)S(1)} async-done(((bf16[32,8,384]{2,1,0:T(8,128)(2,1)}), bf16[32,8,384]{2,1,0:T(8,128)(2,1)S(1)}, u32[]{:S(2)}, u32[]{:S(2)}) %all-to-all-start.1) | async-done | bytes 196640 | tf_op jit(solution)/shard_map/all_to_all | solution.py:80
  128.7 15.2 %all-to-all-start.4 = ((f32[16,1,2592]{2,1,0:T(1,128)}), f32[16,1,2592]{2,1,0:T(1,128)S(1)}, u32[]{:S(2)}, u32[]{:S(2)}) async-start(f32[16,1,2592]{2,1,0:T(1,128)} %all_to_all.49), calls=%async_computation.4 | async-start | bytes 344064 | tf_op jit(solution)/shard_map/all_to_all | solution.py:115
  144.6 13.8 %all-to-all-done.4 = f32[16,1,2592]{2,1,0:T(1,128)S(1)} async-done(((f32[16,1,2592]{2,1,0:T(1,128)}), f32[16,1,2592]{2,1,0:T(1,128)S(1)}, u32[]{:S(2)}, u32[]{:S(2)}) %all-to-all-start.4) | async-done | bytes 165920 | tf_op jit(solution)/shard_map/all_to_all | solution.py:115
  (50 shorter events, 16.2 us)
Async XLA Ops:
  0.6 27.8 %copy-start = (bf16[4,2,384,384]{3,2,1,0:T(8,128)(2,1)S(1)}, bf16[4,2,384,384]{3,2,1,0:T(8,128)(2,1)}, u32[]{:S(2)}) copy-start(bf16[4,2,384,384]{3,2,1,0:T(8,128)(2,1)} %param.9) | copy-start | bytes 7077892
  3.7 12.6 %copy-start.7 = (s32[64]{0:T(128)S(1)}, s32[64]{0:T(128)}, u32[]{:S(2)}) copy-start(s32[64]{0:T(128)} %param.8) | copy-start | bytes 772
  9.2 16.9 %all-to-all-start = ((bf16[2,2,128,384]{3,1,0,2:T(2,128)(2,1)}), bf16[2,2,128,384]{3,1,0,2:T(2,128)(2,1)S(1)}, u32[]{:S(2)}, u32[]{:S(2)}) async-start(bf16[2,2,128,384]{3,1,0,2:T(2,128)(2,1)} %copy.111), calls=%async_computation | async-start | bytes 786432 | tf_op jit(solution)/shard_map/all_to_all | solution.py:54
  26.9 3.0 %copy-start.3 = (bf16[1,32,4,1,384]{4,0,3,2,1:T(2,128)(2,1)}, bf16[1,32,4,1,384]{4,0,3,2,1:T(2,128)(2,1)S(1)}, u32[]{:S(2)}) copy-start(bf16[1,32,4,1,384]{4,0,3,2,1:T(2,128)(2,1)S(1)} %get-tuple-element.18) | copy-start | bytes 294916
  29.0 1.1 copy-start.1
  44.3 3.2 %copy-start.5 = (bf16[2,32,4,16,24]{1,4,0,2,3:T(8,128)(2,1)S(1)}, bf16[2,32,4,16,24]{1,4,0,2,3:T(8,128)(2,1)}, u32[]{:S(2)}) copy-start(bf16[2,32,4,16,24]{1,4,0,2,3:T(8,128)(2,1)} %copy.126) | copy-start | bytes 589828
  47.5 1.1 copy-start.6
  54.9 4.8 %copy-start.2 = (f32[2,32,4,384]{3,1,2,0:T(8,128)S(1)}, f32[2,32,4,384]{3,1,2,0:T(8,128)}, u32[]{:S(2)}) copy-start(f32[2,32,4,384]{3,1,2,0:T(8,128)} %copy-done.1) | copy-start | bytes 1179652
  54.9 4.8 %copy-start.4 = (bf16[1,32,4,1,384]{4,0,3,2,1:T(2,128)(2,1)S(1)}, bf16[1,32,4,1,384]{4,0,3,2,1:T(2,128)(2,1)}, u32[]{:S(2)}) copy-start(bf16[1,32,4,1,384]{4,0,3,2,1:T(2,128)(2,1)} %copy-done.3) | copy-start | bytes 294916
  54.9 39.1 %all-to-all-start.2 = ((bf16[16,9,384,24]{2,3,1,0:T(8,128)(2,1)}), bf16[16,9,384,24]{2,3,1,0:T(8,128)(2,1)}, u32[]{:S(2)}, u32[]{:S(2)}) async-start(bf16[16,9,384,24]{2,3,1,0:T(8,128)(2,1)} %copy.127), calls=%async_computation.2 | async-start | bytes 5308416 | tf_op jit(solution)/shard_map/all_to_all | solution.py:102
  116.3 12.4 %all-to-all-start.1 = ((bf16[32,8,384]{2,1,0:T(8,128)(2,1)}), bf16[32,8,384]{2,1,0:T(8,128)(2,1)S(1)}, u32[]{:S(2)}, u32[]{:S(2)}) async-start(bf16[32,8,384]{2,1,0:T(8,128)(2,1)} %copy.118), calls=%async_computation.1 | async-start | bytes 393216 | tf_op jit(solution)/shard_map/all_to_all | solution.py:80
  128.7 29.7 %all-to-all-start.4 = ((f32[16,1,2592]{2,1,0:T(1,128)}), f32[16,1,2592]{2,1,0:T(1,128)S(1)}, u32[]{:S(2)}, u32[]{:S(2)}) async-start(f32[16,1,2592]{2,1,0:T(1,128)} %all_to_all.49), calls=%async_computation.4 | async-start | bytes 344064 | tf_op jit(solution)/shard_map/all_to_all | solution.py:115

commit v8 on v6

--- a/solution.py
+++ b/solution.py
@@ -88,6 +88,7 @@
     z_t = jnp.stack([cos_t * ur - sin_t * ui, cos_t * ui + sin_t * ur], axis=1).astype(jnp.bfloat16)
     w_t = jnp.stack([cos_t * ur + sin_t * ui, cos_t * ui - sin_t * ur], axis=1).astype(jnp.bfloat16)
     y_all = jnp.stack([v_real, v_imag], axis=0).astype(jnp.bfloat16)
+    returned, z_t, w_t, y_all = lax.optimization_barrier((returned, z_t, w_t, y_all))
     taps = z_t.shape[0]
     col_share = channels // freq_devices
     row_share = channels // data_devices
@@ -106,9 +107,9 @@
         col_sum.reshape(taps, z_devices, core_devices, row_share, col_share), (2, 1, 0, 3, 4)
     )
     row_pieces = lax.all_to_all(row_pieces, "c", split_axis=0, concat_axis=0, tiled=True)
-    row_pieces = jnp.sum(row_pieces, axis=0)
+    row_pieces = jnp.sum(row_pieces, axis=0).astype(jnp.bfloat16)
     row_pieces = lax.all_to_all(row_pieces, "z", split_axis=0, concat_axis=0, tiled=True)
-    tap_grad = jnp.sum(row_pieces, axis=0)
+    tap_grad = jnp.sum(row_pieces.astype(f32), axis=0)
     return (returned, tap_grad)
 
 

time: 150 us -> 154 us (1.027)
  the two profiles are of different devices: /device:TPU:32 before, /device:TPU:1 now
where the time goes in v8:
time: 154 us; the launch traced here: 153 us
  blocking collectives  70.6 us (46%)
  local copies, waits for them, and re-layouts  37.4 us (24%)
  matrix products  13 us (8%)
  starting transfers between devices  11.5 us (7%)
  waiting for transfers between devices  9.9 us (6%)
  other arithmetic  8.96 us (6%)
  between operations  1.74 us (1%)
    all_to_all x1, blocking collectives, local(): lax.all_to_all(col_pieces, 'freq', split_axis=0, concat_axis=0, tiled=True)  34.1 us
    all_to_all x1, blocking collectives, local(): lax.all_to_all(row_pieces, 'z', split_axis=0, concat_axis=0, tiled=True)  27.3 us
    reshape x1, local copies, waits for them, and re-layouts, local(): w_t.reshape(taps, 2, image_rows, bins_local, freq_devices, col_share)  13.2 us
    all_to_all x1, blocking collectives, local(): lax.all_to_all(row_pieces, 'c', split_axis=0, concat_axis=0, tiled=True)  9.2 us
    all_to_all x1, waiting for transfers between devices, local(): lax.all_to_all(both_spec, 'freq', split_axis=2, concat_axis=1, tiled=True)  7.75 us
    all_to_all x1, starting transfers between devices, local(): lax.all_to_all(both_spec, 'freq', split_axis=2, concat_axis=1, tiled=True)  7.72 us
    unnamed x16, local copies, waits for them, and re-layouts  6.54 us
    reshape x1, local copies, waits for them, and re-layouts, local(): col_sum.reshape(taps, z_devices, core_devices, row_share, col_share)  6.03 us
  transfers between devices with their start and end apart: 2, of which 2 were waited for; matrix products, arithmetic and copies ran while one was open for 3% of the time, Pallas kernels for 0%

profile of v8, /device:TPU:1, one launch (start us, length us, event | category | flops | bytes accessed | tf_op | source)
XLA Modules:
  0.0 153.0 jit_solution(4243792238735054329)
XLA Ops:
  1.4 1.1 fusion.90
  5.3 1.2 copy.104
  6.5 7.7 %all-to-all-start = ((bf16[2,2,128,384]{3,1,0,2:T(2,128)(2,1)}), bf16[2,2,128,384]{3,1,0,2:T(2,128)(2,1)S(1)}, u32[]{:S(2)}, u32[]{:S(2)}) async-start(bf16[2,2,128,384]{3,1,0,2:T(2,128)(2,1)} %copy.104), calls=%async_computation | async-start | bytes 786432 | tf_op jit(solution)/shard_map/all_to_all | solution.py:54
  14.5 7.8 %all-to-all-done = bf16[2,2,128,384]{3,1,0,2:T(2,128)(2,1)S(1)} async-done(((bf16[2,2,128,384]{3,1,0,2:T(2,128)(2,1)}), bf16[2,2,128,384]{3,1,0,2:T(2,128)(2,1)S(1)}, u32[]{:S(2)}, u32[]{:S(2)}) %all-to-all-start) | async-done | bytes 393248 | tf_op jit(solution)/shard_map/all_to_all | solution.py:54
  25.1 3.7 %all-to-all-start.1 = ((bf16[32,8,384]{2,1,0:T(8,128)(2,1)}), bf16[32,8,384]{2,1,0:T(8,128)(2,1)S(1)}, u32[]{:S(2)}, u32[]{:S(2)}) async-start(bf16[32,8,384]{2,1,0:T(8,128)(2,1)} %copy.111), calls=%async_computation.1 | async-start | bytes 393216 | tf_op jit(solution)/shard_map/all_to_all | solution.py:77
  30.8 1.2 fusion.7
  32.0 1.4 pad_maximum_fusion
  33.6 2.1 %all-to-all-done.1 = bf16[32,8,384]{2,1,0:T(8,128)(2,1)S(1)} async-done(((bf16[32,8,384]{2,1,0:T(8,128)(2,1)}), bf16[32,8,384]{2,1,0:T(8,128)(2,1)S(1)}, u32[]{:S(2)}, u32[]{:S(2)}) %all-to-all-start.1) | async-done | bytes 196640 | tf_op jit(solution)/shard_map/all_to_all | solution.py:77
  36.5 1.3 reshape.440
  37.8 1.6 %copy.117 = bf16[2,32,4,16,24]{1,4,0,2,3:T(8,128)(2,1)} copy(bf16[2,32,4,16,24]{4,3,1,2,0:T(8,128)(2,1)S(1)} %reshape.440) | data formatting | bytes 393216 | tf_op jit(solution)/shard_map/reshape | solution.py:95
  39.5 13.2 %reshape.439 = bf16[9,2,32,4,16,24]{5,4,2,3,1,0:T(8,128)(2,1)} reshape(bf16[9,2,32,4,384]{4,2,3,1,0:T(8,128)(2,1)S(1)} %pad_maximum_fusion.1) | data formatting | bytes 3538944 | tf_op jit(solution)/shard_map/reshape | solution.py:96
  52.7 2.7 %fusion.10 = f32[16,24,9,384,1,1]{3,1,5,4,0,2:T(8,128)S(1)} fusion(bf16[2,32,4,16,24]{1,4,0,2,3:T(8,128)(2,1)S(1)} %copy-done.2, bf16[9,2,32,4,384]{4,2,3,1,0:T(8,128)(2,1)} %pad_maximum_fusion), kind=kOutput, calls=%fused_computation.16 | convolution fusion | flops 679477248 | bytes 7274496 | tf_op jit(solution)/shard_map/teibr,eibfc->ftrc/dot_general | solution.py:97
  55.4 1.5 copy-done
  56.9 5.9 %fusion.3 = bf16[16,9,384,24]{2,3,0,1:T(8,128)(2,1)S(1)} fusion(f32[16,24,9,384,1,1]{3,1,5,4,0,2:T(8,128)S(1)} %fusion.10, bf16[9,2,32,4,16,24]{5,4,2,3,1,0:T(8,128)(2,1)S(1)} %copy-done, bf16[2,32,4,384]{3,1,2,0:T(8,128)(2,1)S(1)} %pad_maximum_fusion.4), kind=kOutput, calls=%fused_computation.4 | convolution fusion | flops 683458560 | bytes 9928704 | tf_op jit(solution)/shard_map/eibr,teibfc->ftrc/dot_general | solution.py:98
  63.0 34.1 %all_to_all.48 = bf16[16,9,384,24]{2,3,1,0:T(8,128)(2,1)S(1)} all-to-all(bf16[16,9,384,24]{2,3,1,0:T(8,128)(2,1)S(1)} %copy.119), channel_id=1, replica_groups=mesh['z'=16,'c'=2,'freq'=16] {'freq'}, dimensions={0} | all-to-all | bytes 5308416 | tf_op jit(solution)/shard_map/all_to_all | solution.py:102
  97.2 1.1 convert_reduce_fusion
  98.3 6.0 %reshape.441 = f32[9,16,2,12,24]{3,2,1,4,0:T(2,128)S(1)} reshape(f32[9,384,24]{1,2,0:T(8,128)} %convert_reduce_fusion) | data formatting | bytes 663552 | tf_op jit(solution)/shard_map/reshape | solution.py:107
  104.4 3.9 %copy.120 = f32[2,16,9,12,24]{4,1,3,2,0:T(8,128)} copy(f32[2,16,9,12,24]{3,0,1,4,2:T(2,128)S(1)} %bitcast.144) | data formatting | bytes 663552 | tf_op jit(solution)/shard_map/transpose | solution.py:106
  108.2 2.5 %reshape.449 = f32[2,1,41472]{2,1,0:T(1,128)S(1)} reshape(f32[2,9,12,16,24]{4,3,2,1,0:T(8,128)} %bitcast.145) | data formatting | bytes 663552
  110.7 9.2 %all_to_all.49 = f32[2,1,41472]{2,1,0:T(1,128)S(1)} all-to-all(f32[2,1,41472]{2,1,0:T(1,128)S(1)} %reshape.449), channel_id=1, replica_groups=mesh['z'=16,'c'=2,'freq'=16] {'c'}, dimensions={0} | all-to-all | bytes 663552 | tf_op jit(solution)/shard_map/all_to_all | solution.py:109
  120.5 1.7 %reduce = f32[2,41472]{1,0:T(2,128)S(1)} reduce(f32[2,1,41472]{2,1,0:T(1,128)S(1)} %all_to_all.49, f32[]{:T(128)} %broadcast.612), dimensions={1}, to_apply=%all_to_all.41.reduce_sub_computation | reduce | bytes 663556 | tf_op jit(solution)/shard_map/all_to_all | solution.py:109
  122.1 1.3 reshape.450
  124.3 27.3 %all_to_all.50 = bf16[16,2,1296]{2,1,0:T(2,128)(2,1)S(1)} all-to-all(bf16[16,2,1296]{2,1,0:T(2,128)(2,1)S(1)} %reshape.451), channel_id=1, replica_groups=mesh['z'=16,'c'=2,'freq'=16] {'z'}, dimensions={0} | all-to-all | bytes 165888 | tf_op jit(solution)/shard_map/all_to_all | solution.py:111
  152.2 0.9 convert_reduce_fusion.1
  (48 shorter events, 10.8 us)
Async XLA Ops:
  0.6 3.2 %copy-start.4 = (bf16[2,384,1024]{2,1,0:T(8,128)(2,1)S(1)}, bf16[2,384,1024]{2,1,0:T(8,128)(2,1)}, u32[]{:S(2)}) copy-start(bf16[2,384,1024]{2,1,0:T(8,128)(2,1)} %param.6) | copy-start | bytes 4718596
  3.0 1.5 %copy-start.5 = (bf16[2,384,1024]{2,1,0:T(8,128)(2,1)S(1)}, bf16[2,384,1024]{2,1,0:T(8,128)(2,1)}, u32[]{:S(2)}) copy-start(bf16[2,384,1024]{2,1,0:T(8,128)(2,1)} %param.5) | copy-start | bytes 4718596
  5.3 9.0 %copy-start.3 = (s32[64]{0:T(128)S(1)}, s32[64]{0:T(128)}, u32[]{:S(2)}) copy-start(s32[64]{0:T(128)} %param.8) | copy-start | bytes 772
  6.5 16.6 %copy-start.1 = (bf16[4,2,384,384]{3,2,1,0:T(8,128)(2,1)S(1)}, bf16[4,2,384,384]{3,2,1,0:T(8,128)(2,1)}, u32[]{:S(2)}) copy-start(bf16[4,2,384,384]{3,2,1,0:T(8,128)(2,1)} %param.9) | copy-start | bytes 7077892
  6.5 15.7 %all-to-all-start = ((bf16[2,2,128,384]{3,1,0,2:T(2,128)(2,1)}), bf16[2,2,128,384]{3,1,0,2:T(2,128)(2,1)S(1)}, u32[]{:S(2)}, u32[]{:S(2)}) async-start(bf16[2,2,128,384]{3,1,0,2:T(2,128)(2,1)} %copy.104), calls=%async_computation | async-start | bytes 786432 | tf_op jit(solution)/shard_map/all_to_all | solution.py:54
  25.1 10.6 %all-to-all-start.1 = ((bf16[32,8,384]{2,1,0:T(8,128)(2,1)}), bf16[32,8,384]{2,1,0:T(8,128)(2,1)S(1)}, u32[]{:S(2)}, u32[]{:S(2)}) async-start(bf16[32,8,384]{2,1,0:T(8,128)(2,1)} %copy.111), calls=%async_computation.1 | async-start | bytes 393216 | tf_op jit(solution)/shard_map/all_to_all | solution.py:77
  39.5 13.2 %copy-start.2 = (bf16[2,32,4,16,24]{1,4,0,2,3:T(8,128)(2,1)S(1)}, bf16[2,32,4,16,24]{1,4,0,2,3:T(8,128)(2,1)}, u32[]{:S(2)}) copy-start(bf16[2,32,4,16,24]{1,4,0,2,3:T(8,128)(2,1)} %copy.117) | copy-start | bytes 589828
  52.7 4.2 %copy-start = (bf16[9,2,32,4,16,24]{5,4,2,3,1,0:T(8,128)(2,1)S(1)}, bf16[9,2,32,4,16,24]{5,4,2,3,1,0:T(8,128)(2,1)}, u32[]{:S(2)}) copy-start(bf16[9,2,32,4,16,24]{5,4,2,3,1,0:T(8,128)(2,1)} %reshape.439) | copy-start | bytes 5308420

commit v9 on v6

--- a/solution.py
+++ b/solution.py
@@ -81,6 +81,7 @@
         bin_order, lax.axis_index("freq") * bins_local, bins_local
     )
     cos_local, sin_local = tap_phases(local_bins, GRID)
+    returned, cos_local, sin_local = lax.optimization_barrier((returned, cos_local, sin_local))
     cos_t = cos_local.T[:, None, :, None]
     sin_t = sin_local.T[:, None, :, None]
     ur = u_real[None]

time: 150 us -> 163 us (1.087)
  the two profiles are of different devices: /device:TPU:32 before, /device:TPU:1 now
where the time goes in v9:
time: 163 us; the launch traced here: 160 us
  blocking collectives  72.6 us (45%)
  local copies, waits for them, and re-layouts  33.3 us (20%)
  matrix products  18.7 us (11%)
  other arithmetic  14.3 us (9%)
  starting transfers between devices  11.9 us (7%)
  waiting for transfers between devices  7.75 us (5%)
  between operations  1.64 us (1%)
    all_to_all x1, blocking collectives, local(): lax.all_to_all(col_pieces, 'freq', split_axis=0, concat_axis=0, tiled=True)  36.1 us
    all_to_all x1, blocking collectives, local(): lax.all_to_all(row_pieces, 'z', split_axis=0, concat_axis=0, tiled=True)  27.4 us
    dot_general x8, matrix products, mm(): return jnp.einsum(eq, x, p, preferred_element_type=f32)  10.4 us
    all_to_all x1, blocking collectives, local(): lax.all_to_all(row_pieces, 'c', split_axis=0, concat_axis=0, tiled=True)  9.16 us
    all_to_all x1, waiting for transfers between devices, local(): lax.all_to_all(both_spec, 'freq', split_axis=2, concat_axis=1, tiled=True)  7.75 us
    all_to_all x1, starting transfers between devices, local(): lax.all_to_all(both_spec, 'freq', split_axis=2, concat_axis=1, tiled=True)  7.58 us
    another operation x4, local copies, waits for them, and re-layouts, local(): y_all = jnp.stack([v_real, v_imag], axis=0).astype(jnp.bfloat16)  6.71 us
    reshape x1, local copies, waits for them, and re-layouts, local(): col_sum.reshape(taps, z_devices, core_devices, row_share, col_share)  6.03 us
  transfers between devices with their start and end apart: 2, of which 1 were waited for; matrix products, arithmetic and copies ran while one was open for 9% of the time, Pallas kernels for 0%

profile of v9, /device:TPU:1, one launch (start us, length us, event | category | flops | bytes accessed | tf_op | source)
XLA Modules:
  0.0 160.2 jit_solution(7030672267800244808)
XLA Ops:
  4.4 2.1 %fusion.40 = bf16[1,2,128,384]{3,2,1,0:T(8,128)(2,1)S(1)} fusion(bf16[1024,128,1]{0,1,2:T(8,128)(2,1)S(1)} %reshape.362, bf16[2,384,1024]{2,1,0:T(8,128)(2,1)} %param.5, bf16[2]{0:T(256)(128)(2,1)S(1)} %compare_convert_fusion), kind=kOutput, calls=%fused_computation.39 | convolution fusion | flops 204570624 | bytes 2031620 | tf_op jit(solution)/shard_map/scp,pk->skc/dot_general | solution.py:49
  7.8 7.6 %all-to-all-start = ((bf16[2,2,128,384]{3,1,0,2:T(2,128)(2,1)}), bf16[2,2,128,384]{3,1,0,2:T(2,128)(2,1)S(1)}, u32[]{:S(2)}, u32[]{:S(2)}) async-start(bf16[2,2,128,384]{3,1,0,2:T(2,128)(2,1)} %copy.109), calls=%async_computation | async-start | bytes 786432 | tf_op jit(solution)/shard_map/all_to_all | solution.py:54
  15.6 7.8 %all-to-all-done = bf16[2,2,128,384]{3,1,0,2:T(2,128)(2,1)S(1)} async-done(((bf16[2,2,128,384]{3,1,0,2:T(2,128)(2,1)}), bf16[2,2,128,384]{3,1,0,2:T(2,128)(2,1)S(1)}, u32[]{:S(2)}, u32[]{:S(2)}) %all-to-all-start) | async-done | bytes 393248 | tf_op jit(solution)/shard_map/all_to_all | solution.py:54
  28.2 1.6 mul.301
  29.8 2.0 %fusion.46 = f32[32,4,384]{2,0,1:T(8,128)} fusion(f32[4,32,384]{2,1,0:T(8,128)} %fusion.21, bf16[4,2,384,384]{3,2,1,0:T(8,128)(2,1)S(1)} %copy-done, bf16[1,32,4,1,384]{4,0,3,2,1:T(2,128)(2,1)} %copy-done.2), kind=kOutput, calls=%fused_computation.41 | convolution fusion | flops 37797888 | bytes 1671168 | tf_op jit(solution)/shard_map/ibr,brc->ibc/dot_general | solution.py:66
  31.8 1.7 %fusion.85 = bf16[32,4,1,384]{3,0,1,2:T(8,128)(2,1)} fusion(f32[32,4,384]{2,0,1:T(8,128)} %fusion.46, bf16[1,32,4,1,384]{4,0,3,2,1:T(2,128)(2,1)} %copy-done.2), kind=kLoop, calls=%fused_computation.78 | loop fusion | flops 196608 | bytes 393216 | tf_op jit(solution)/shard_map/stack | solution.py:73
  33.4 2.5 %mul.297 = f32[32,4,16,24]{3,2,0,1:T(8,128)} reshape(f32[32,4,384]{2,0,1:T(8,128)} %fusion.46) | data formatting | bytes 393216 | tf_op jit(solution)/shard_map/mul | solution.py:90
  37.7 4.4 %all-to-all-start.1 = ((bf16[32,8,384]{2,1,0:T(8,128)(2,1)}), bf16[32,8,384]{2,1,0:T(8,128)(2,1)}, u32[]{:S(2)}, u32[]{:S(2)}) async-start(bf16[32,8,384]{2,1,0:T(8,128)(2,1)} %copy.116), calls=%async_computation.1 | async-start | bytes 393216 | tf_op jit(solution)/shard_map/all_to_all | solution.py:77
  43.5 2.1 %fusion.17 = f32[4,32,384]{2,1,0:T(8,128)} fusion(bf16[4,2,384,384]{3,2,1,0:T(8,128)(2,1)S(1)} %copy-done, bf16[1,32,4,1,384]{4,0,3,2,1:T(2,128)(2,1)} %get-tuple-element.20), kind=kOutput, calls=%fused_computation.22 | convolution fusion | flops 37748736 | bytes 1474560 | tf_op jit(solution)/shard_map/ibk,bck->ibc/dot_general | solution.py:66
  46.0 1.5 stack.67
  47.6 2.2 %copy.124 = bf16[1,32,4,16,24]{1,4,0,2,3:T(8,128)(2,1)} copy(bf16[1,32,4,16,24]{4,3,1,2,0:T(8,128)(2,1)} %stack.67) | data formatting | bytes 196608 | tf_op jit(solution)/shard_map/stack | solution.py:91
  49.8 2.1 %fusion.64 = bf16[4,32,384]{2,1,0:T(8,128)(2,1)} fusion(f32[4,32,384]{2,1,0:T(8,128)} %fusion.17, bf16[4,2,384,384]{3,2,1,0:T(8,128)(2,1)S(1)} %copy-done, bf16[1,32,4,1,384]{4,0,3,2,1:T(2,128)(2,1)} %get-tuple-element.21), kind=kOutput, calls=%fused_computation.47 | convolution fusion | flops 37847040 | bytes 1572864 | tf_op jit(solution)/shard_map/ibk,bck->ibc/dot_general | solution.py:66
  51.9 1.7 %stack.66 = bf16[1,32,4,16,24]{4,3,1,2,0:T(8,128)(2,1)S(1)} reshape(bf16[32,4,384]{2,0,1:T(8,128)(2,1)} %bitcast.148) | data formatting | bytes 196608 | tf_op jit(solution)/shard_map/stack | solution.py:91
  55.8 1.6 %copy.165 = bf16[2,16,8,384]{3,2,1,0:T(8,128)(2,1)} copy(bf16[2,16,8,384]{3,2,0,1:T(8,128)(2,1)} %bitcast.19) | data formatting | bytes 393216 | tf_op jit(solution)/shard_map/all_to_all | solution.py:77
  57.5 1.7 %subtract_convert_fusion.1 = (bf16[9,1,32,4,384]{4,2,1,3,0:T(8,128)(2,1)S(1)}, bf16[9,1,32,4,384]{4,2,1,3,0:T(8,128)(2,1)S(1)}) fusion(f32[32,4,384]{2,0,1:T(8,128)} %fusion.52, f32[9,4]{1,0:T(8,128)S(1)} %bitcast.151, f32[32,4,384]{2,0,1:T(8,128)} %fusion.46, f32[9,4]{1,0:T(8,128)S(1)} %bitcast.153), kind=kLoop, calls=%fused_computation.15 | loop fusion | flops 3538944 | bytes 2162976 | tf_op jit(solution)/shard_map/convert
  59.2 2.0 %add_convert_fusion = (bf16[9,1,32,4,16,24]{2,5,1,3,4,0:T(8,128)(2,1)S(1)}, bf16[9,1,32,4,16,24]{2,5,1,3,4,0:T(8,128)(2,1)S(1)}) fusion(f32[32,4,16,24]{0,3,1,2:T(8,128)S(1)} %copy.119, f32[9,4]{1,0:T(8,128)S(1)} %bitcast.152, f32[32,4,16,24]{0,3,1,2:T(8,128)S(1)} %copy.118, f32[9,4]{1,0:T(8,128)S(1)} %bitcast.154), kind=kLoop, calls=%fused_computation.5 | loop fusion | flops 3538944 | bytes 2162976 | tf_op jit(solution)/shard_map/convert.10
  62.4 4.4 %fusion.5 = bf16[16,9,384,24]{2,3,0,1:T(8,128)(2,1)S(1)} fusion(f32[16,24,9,384,1,1]{3,1,5,4,0,2:T(8,128)S(1)} %fusion.8, bf16[9,1,32,4,16,24]{2,5,1,3,4,0:T(8,128)(2,1)S(1)} %get-tuple-element.17, bf16[9,1,32,4,16,24]{2,5,1,3,4,0:T(8,128)(2,1)S(1)} %get-tuple-element.16, bf16[1,32,4,384]{3,1,2,0:T(8,128)(2,1)S(1)} %bitcast.147, ...), kind=kOutput, calls=%fused_computation.8 | convolution fusion | flops 684441600 | bytes 9928704 | tf_op jit(solution)/shard_map/eibr,teibfc->ftrc/dot_general | solution.py:98
  67.1 36.1 %all_to_all.48 = bf16[16,9,384,24]{2,3,1,0:T(8,128)(2,1)S(1)} all-to-all(bf16[16,9,384,24]{2,3,1,0:T(8,128)(2,1)S(1)} %copy.125), channel_id=1, replica_groups=mesh['z'=16,'c'=2,'freq'=16] {'freq'}, dimensions={0} | all-to-all | bytes 5308416 | tf_op jit(solution)/shard_map/all_to_all | solution.py:102
  104.3 6.0 %reshape.361 = f32[9,16,2,12,24]{3,2,1,4,0:T(2,128)S(1)} reshape(f32[9,384,24]{1,2,0:T(8,128)} %convert_reduce_fusion) | data formatting | bytes 663552 | tf_op jit(solution)/shard_map/reshape | solution.py:107
  110.3 3.9 %copy.126 = f32[2,16,9,12,24]{4,1,3,2,0:T(8,128)} copy(f32[2,16,9,12,24]{3,0,1,4,2:T(2,128)S(1)} %bitcast.141) | data formatting | bytes 663552 | tf_op jit(solution)/shard_map/transpose | solution.py:106
  114.2 2.5 %reshape.369 = f32[2,1,41472]{2,1,0:T(1,128)S(1)} reshape(f32[2,9,12,16,24]{4,3,2,1,0:T(8,128)} %bitcast.142) | data formatting | bytes 663552
  116.7 9.2 %all_to_all.49 = f32[2,1,41472]{2,1,0:T(1,128)S(1)} all-to-all(f32[2,1,41472]{2,1,0:T(1,128)S(1)} %reshape.369), channel_id=1, replica_groups=mesh['z'=16,'c'=2,'freq'=16] {'c'}, dimensions={0} | all-to-all | bytes 663552 | tf_op jit(solution)/shard_map/all_to_all | solution.py:109
  126.3 1.7 %reduce = f32[2,41472]{1,0:T(2,128)S(1)} reduce(f32[2,1,41472]{2,1,0:T(1,128)S(1)} %all_to_all.49, f32[]{:T(128)} %broadcast.518), dimensions={1}, to_apply=%all_to_all.41.reduce_sub_computation | reduce | bytes 663556 | tf_op jit(solution)/shard_map/all_to_all | solution.py:109
  130.5 27.4 %all_to_all.50 = f32[16,1,2592]{2,1,0:T(1,128)S(1)} all-to-all(f32[16,1,2592]{2,1,0:T(1,128)S(1)} %reshape.371), channel_id=1, replica_groups=mesh['z'=16,'c'=2,'freq'=16] {'z'}, dimensions={0} | all-to-all | bytes 331776 | tf_op jit(solution)/shard_map/all_to_all | solution.py:111
  (58 shorter events, 22.8 us)
Async XLA Ops:
  0.6 3.0 %copy-start.8 = (bf16[2,384,1024]{2,1,0:T(8,128)(2,1)S(1)}, bf16[2,384,1024]{2,1,0:T(8,128)(2,1)}, u32[]{:S(2)}) copy-start(bf16[2,384,1024]{2,1,0:T(8,128)(2,1)} %param.6) | copy-start | bytes 4718596
  4.4 11.0 %copy-start.7 = (s32[64]{0:T(128)S(1)}, s32[64]{0:T(128)}, u32[]{:S(2)}) copy-start(s32[64]{0:T(128)} %param.8) | copy-start | bytes 772
  6.6 18.4 %copy-start = (bf16[4,2,384,384]{3,2,1,0:T(8,128)(2,1)S(1)}, bf16[4,2,384,384]{3,2,1,0:T(8,128)(2,1)}, u32[]{:S(2)}) copy-start(bf16[4,2,384,384]{3,2,1,0:T(8,128)(2,1)} %param.9) | copy-start | bytes 7077892
  7.8 15.6 %all-to-all-start = ((bf16[2,2,128,384]{3,1,0,2:T(2,128)(2,1)}), bf16[2,2,128,384]{3,1,0,2:T(2,128)(2,1)S(1)}, u32[]{:S(2)}, u32[]{:S(2)}) async-start(bf16[2,2,128,384]{3,1,0,2:T(2,128)(2,1)} %copy.109), calls=%async_computation | async-start | bytes 786432 | tf_op jit(solution)/shard_map/all_to_all | solution.py:54
  25.0 2.3 %copy-start.2 = (bf16[1,32,4,1,384]{4,0,3,2,1:T(2,128)(2,1)}, bf16[1,32,4,1,384]{4,0,3,2,1:T(2,128)(2,1)S(1)}, u32[]{:S(2)}) copy-start(bf16[1,32,4,1,384]{4,0,3,2,1:T(2,128)(2,1)S(1)} %get-tuple-element.23) | copy-start | bytes 294916
  37.7 18.2 %all-to-all-start.1 = ((bf16[32,8,384]{2,1,0:T(8,128)(2,1)}), bf16[32,8,384]{2,1,0:T(8,128)(2,1)}, u32[]{:S(2)}, u32[]{:S(2)}) async-start(bf16[32,8,384]{2,1,0:T(8,128)(2,1)} %copy.116), calls=%async_computation.1 | async-start | bytes 393216 | tf_op jit(solution)/shard_map/all_to_all | solution.py:77
  42.0 3.6 %copy-start.3 = (bf16[1,32,4,1,384]{4,0,3,2,1:T(2,128)(2,1)S(1)}, bf16[1,32,4,1,384]{4,0,3,2,1:T(2,128)(2,1)}, u32[]{:S(2)}) copy-start(bf16[1,32,4,1,384]{4,0,3,2,1:T(2,128)(2,1)} %get-tuple-element.20) | copy-start | bytes 294916
  51.9 3.4 %copy-start.1 = (f32[32,4,16,24]{3,2,0,1:T(8,128)S(1)}, f32[32,4,16,24]{3,2,0,1:T(8,128)}, u32[]{:S(2)}) copy-start(f32[32,4,16,24]{3,2,0,1:T(8,128)} %mul.297) | copy-start | bytes 589828
  59.2 2.0 %copy-start.4 = (bf16[1,32,4,16,24]{1,4,0,2,3:T(8,128)(2,1)S(1)}, bf16[1,32,4,16,24]{1,4,0,2,3:T(8,128)(2,1)}, u32[]{:S(2)}) copy-start(bf16[1,32,4,16,24]{1,4,0,2,3:T(8,128)(2,1)} %copy.124) | copy-start | bytes 294916
  59.2 2.0 %copy-start.5 = (bf16[1,32,4,16,24]{1,4,0,2,3:T(8,128)(2,1)S(1)}, bf16[1,32,4,16,24]{1,4,0,2,3:T(8,128)(2,1)}, u32[]{:S(2)}) copy-start(bf16[1,32,4,16,24]{1,4,0,2,3:T(8,128)(2,1)} %copy.123) | copy-start | bytes 294916
  61.3 1.1 copy-start.6

commit v10 on v6

--- a/solution.py
+++ b/solution.py
@@ -97,18 +97,21 @@
     second = jnp.einsum("eibr,teibfc->ftrc", y_all, w_cols, preferred_element_type=f32)
     gram_scale = 1.0 / math.sqrt(data_devices * freq_devices * slot_count)
     tap_scale = 2.0 * gram_scale / math.sqrt(total_bins)
-    col_pieces = ((second - first) * tap_scale).astype(jnp.bfloat16)
-    col_pieces = lax.all_to_all(col_pieces, "freq", split_axis=0, concat_axis=0, tiled=True)
-    col_sum = jnp.sum(col_pieces.astype(f32), axis=0)
     z_devices = lax.axis_size("z")
     core_devices = lax.axis_size("c")
-    row_pieces = jnp.transpose(
-        col_sum.reshape(taps, z_devices, core_devices, row_share, col_share), (2, 1, 0, 3, 4)
+    block = taps * row_share * col_share
+    col_pieces = ((second - first) * tap_scale).reshape(
+        freq_devices, taps, z_devices, core_devices, row_share, col_share
     )
+    col_pieces = jnp.transpose(col_pieces, (0, 3, 2, 1, 4, 5)).reshape(
+        freq_devices, core_devices * z_devices * block
+    ).astype(jnp.bfloat16)
+    col_pieces = lax.all_to_all(col_pieces, "freq", split_axis=0, concat_axis=0, tiled=True)
+    row_pieces = jnp.sum(col_pieces.astype(f32), axis=0).reshape(core_devices, z_devices * block)
     row_pieces = lax.all_to_all(row_pieces, "c", split_axis=0, concat_axis=0, tiled=True)
-    row_pieces = jnp.sum(row_pieces, axis=0)
+    row_pieces = jnp.sum(row_pieces, axis=0).reshape(z_devices, block)
     row_pieces = lax.all_to_all(row_pieces, "z", split_axis=0, concat_axis=0, tiled=True)
-    tap_grad = jnp.sum(row_pieces, axis=0)
+    tap_grad = jnp.sum(row_pieces, axis=0).reshape(taps, row_share, col_share)
     return (returned, tap_grad)
 
 

time: 150 us -> 257 us (1.71)
  the two profiles are of different devices: /device:TPU:32 before, /device:TPU:1 now
where the time goes in v10:
time: 257 us; the launch traced here: 253 us
  local copies, waits for them, and re-layouts  71.3 us (28%)
  other arithmetic  71.3 us (28%)
  waiting for transfers between devices  54.3 us (21%)
  starting transfers between devices  30.8 us (12%)
  matrix products  13 us (5%)
  blocking collectives  10.5 us (4%)
    convert_element_type x1, other arithmetic, local(): col_pieces = jnp.transpose(col_pieces, (0, 3, 2, 1, 4, 5)).reshape(freq_d...  56.9 us
    convert_element_type x4, local copies, waits for them, and re-layouts, local(): col_pieces = jnp.transpose(col_pieces, (0, 3, 2, 1, 4, 5)).reshape(freq_d...  47.5 us
    all_to_all x1, waiting for transfers between devices, local(): lax.all_to_all(col_pieces, 'freq', split_axis=0, concat_axis=0, tiled=True)  29.4 us
    all_to_all x1, starting transfers between devices, local(): lax.all_to_all(row_pieces, 'z', split_axis=0, concat_axis=0, tiled=True)  14.9 us
    all_to_all x1, waiting for transfers between devices, local(): lax.all_to_all(row_pieces, 'z', split_axis=0, concat_axis=0, tiled=True)  11.5 us
    all_to_all x1, blocking collectives, local(): lax.all_to_all(row_pieces, 'c', split_axis=0, concat_axis=0, tiled=True)  10.5 us
    unnamed x16, local copies, waits for them, and re-layouts  10.4 us
    reduce_sum x1, other arithmetic, local(): jnp.sum(col_pieces.astype(f32), axis=0)  8.72 us
  transfers between devices with their start and end apart: 4, of which 4 were waited for; matrix products, arithmetic and copies ran while one was open for 1% of the time, Pallas kernels for 0%

profile of v10, /device:TPU:1, one launch (start us, length us, event | category | flops | bytes accessed | tf_op | source)
XLA Modules:
  0.0 252.9 jit_solution(13069580866234575111)
XLA Ops:
  4.4 2.1 fusion.40
  7.8 7.6 %all-to-all-start = ((bf16[2,2,128,384]{3,1,0,2:T(2,128)(2,1)}), bf16[2,2,128,384]{3,1,0,2:T(2,128)(2,1)S(1)}, u32[]{:S(2)}, u32[]{:S(2)}) async-start(bf16[2,2,128,384]{3,1,0,2:T(2,128)(2,1)} %copy.130), calls=%async_computation | async-start | bytes 786432 | tf_op jit(solution)/shard_map/all_to_all | solution.py:54
  15.6 7.7 %all-to-all-done = bf16[2,2,128,384]{3,1,0,2:T(2,128)(2,1)S(1)} async-done(((bf16[2,2,128,384]{3,1,0,2:T(2,128)(2,1)}), bf16[2,2,128,384]{3,1,0,2:T(2,128)(2,1)S(1)}, u32[]{:S(2)}, u32[]{:S(2)}) %all-to-all-start) | async-done | bytes 393248 | tf_op jit(solution)/shard_map/all_to_all | solution.py:54
  25.9 1.2 fusion.17
  27.5 1.5 stack.67
  29.0 2.2 copy.145
  31.2 1.4 fusion.64
  33.3 1.3 copy.144
  37.6 2.0 add_convert_fusion
  40.7 4.4 %fusion.5 = bf16[16,9,384,24]{2,3,0,1:T(8,128)(2,1)S(1)} fusion(f32[16,24,9,384,1,1]{3,1,5,4,0,2:T(8,128)S(1)} %fusion.8, bf16[9,1,32,4,16,24]{2,5,1,3,4,0:T(8,128)(2,1)S(1)} %get-tuple-element.5, bf16[9,1,32,4,16,24]{2,5,1,3,4,0:T(8,128)(2,1)S(1)} %get-tuple-element.4, bf16[1,32,4,384]{3,1,2,0:T(8,128)(2,1)S(1)} %bitcast.144, ...), kind=kOutput, calls=%fused_computation.8 | convolution fusion | flops 684441600 | bytes 9928704 | tf_op jit(solution)/shard_map/eibr,teibfc->ftrc/dot_general | solution.py:97
  45.2 10.8 %copy.146 = bf16[16,9,384,24]{3,0,2,1:T(8,128)(2,1)} copy(bf16[16,9,384,24]{2,3,0,1:T(8,128)(2,1)S(1)} %fusion.5) | data formatting | bytes 5308416 | tf_op jit(solution)/shard_map/convert_element_type | solution.py:108
  56.0 13.5 %copy.147 = bf16[16,2,16,9,12,24]{5,4,3,2,1,0:T(8,128)(2,1)} copy(bf16[16,2,16,9,12,24]{5,0,4,1,2,3:T(8,128)(2,1)} %bitcast.137) | data formatting | bytes 5308416 | tf_op jit(solution)/shard_map/convert_element_type | solution.py:108
  69.5 22.7 %convert_element_type.107 = bf16[16,1,82944]{2,1,0:T(2,128)(2,1)} reshape(bf16[16,2,16,9,12,24]{5,4,3,2,1,0:T(8,128)(2,1)} %copy.147) | data formatting | bytes 5308416 | tf_op jit(solution)/shard_map/convert_element_type | solution.py:108
  92.7 56.9 %reduce.3 = bf16[16,82944]{1,0:T(8,128)(2,1)S(1)} reduce(bf16[16,1,82944]{2,1,0:T(2,128)(2,1)} %convert_element_type.107, bf16[]{:T(256)} %broadcast.636), dimensions={1}, to_apply=%convert_element_type.107.reduce_sub_computation | reduce | bytes 5308418 | tf_op jit(solution)/shard_map/convert_element_type | solution.py:108
  149.7 3.3 %reshape.488 = bf16[16,2,41472]{2,1,0:T(2,128)(2,1)} reshape(bf16[16,82944]{1,0:T(8,128)(2,1)S(1)} %reduce.3) | data formatting | bytes 5308416
  153.0 4.0 %all-to-all-start.2 = ((bf16[16,2,41472]{2,1,0:T(2,128)(2,1)}), bf16[16,2,41472]{2,1,0:T(2,128)(2,1)S(1)}, u32[]{:S(2)}, u32[]{:S(2)}) async-start(bf16[16,2,41472]{2,1,0:T(2,128)(2,1)} %reshape.488), calls=%async_computation.2 | async-start | bytes 5308416 | tf_op jit(solution)/shard_map/all_to_all | solution.py:109
  157.9 29.4 %all-to-all-done.2 = bf16[16,2,41472]{2,1,0:T(2,128)(2,1)S(1)} async-done(((bf16[16,2,41472]{2,1,0:T(2,128)(2,1)}), bf16[16,2,41472]{2,1,0:T(2,128)(2,1)S(1)}, u32[]{:S(2)}, u32[]{:S(2)}) %all-to-all-start.2) | async-done | bytes 2654240 | tf_op jit(solution)/shard_map/all_to_all | solution.py:109
  187.3 7.0 %reshape.489 = bf16[16,1,82944]{2,1,0:T(2,128)(2,1)} reshape(bf16[16,2,41472]{2,1,0:T(2,128)(2,1)S(1)} %all-to-all-done.2) | data formatting | bytes 5308416
  194.3 8.7 %convert_reduce_fusion = f32[82944]{0:T(1024)S(1)} fusion(bf16[16,1,82944]{2,1,0:T(2,128)(2,1)} %reshape.489), kind=kLoop, calls=%fused_computation.9 | loop fusion | flops 2571264 | bytes 2985984 | tf_op jit(solution)/shard_map/reduce_sum | solution.py:110
  203.0 10.5 %all_to_all.57 = f32[2,1,41472]{2,1,0:T(1,128)S(1)} all-to-all(f32[2,1,41472]{2,1,0:T(1,128)S(1)} %bitcast.140), channel_id=1, replica_groups=mesh['z'=16,'c'=2,'freq'=16] {'c'}, dimensions={0} | all-to-all | bytes 663552 | tf_op jit(solution)/shard_map/all_to_all | solution.py:111
  213.5 4.4 %all-to-all-start.1 = ((bf16[32,8,384]{2,1,0:T(8,128)(2,1)}), bf16[32,8,384]{2,1,0:T(8,128)(2,1)S(1)}, u32[]{:S(2)}, u32[]{:S(2)}) async-start(bf16[32,8,384]{2,1,0:T(8,128)(2,1)} %copy.137), calls=%async_computation.1 | async-start | bytes 393216 | tf_op jit(solution)/shard_map/all_to_all | solution.py:77
  219.2 5.7 %all-to-all-done.1 = bf16[32,8,384]{2,1,0:T(8,128)(2,1)S(1)} async-done(((bf16[32,8,384]{2,1,0:T(8,128)(2,1)}), bf16[32,8,384]{2,1,0:T(8,128)(2,1)S(1)}, u32[]{:S(2)}, u32[]{:S(2)}) %all-to-all-start.1) | async-done | bytes 196640 | tf_op jit(solution)/shard_map/all_to_all | solution.py:77
  224.9 14.9 %all-to-all-start.4 = ((f32[16,1,2592]{2,1,0:T(1,128)}), f32[16,1,2592]{2,1,0:T(1,128)S(1)}, u32[]{:S(2)}, u32[]{:S(2)}) async-start(f32[16,1,2592]{2,1,0:T(1,128)} %all_to_all.50), calls=%async_computation.4 | async-start | bytes 344064 | tf_op jit(solution)/shard_map/all_to_all | solution.py:113
  240.5 11.5 %all-to-all-done.4 = f32[16,1,2592]{2,1,0:T(1,128)S(1)} async-done(((f32[16,1,2592]{2,1,0:T(1,128)}), f32[16,1,2592]{2,1,0:T(1,128)S(1)}, u32[]{:S(2)}, u32[]{:S(2)}) %all-to-all-start.4) | async-done | bytes 165920 | tf_op jit(solution)/shard_map/all_to_all | solution.py:113
  (54 shorter events, 16.4 us)
Async XLA Ops:
  0.6 3.0 %copy-start.6 = (bf16[2,384,1024]{2,1,0:T(8,128)(2,1)S(1)}, bf16[2,384,1024]{2,1,0:T(8,128)(2,1)}, u32[]{:S(2)}) copy-start(bf16[2,384,1024]{2,1,0:T(8,128)(2,1)} %param.6) | copy-start | bytes 4718596
  4.4 11.0 %copy-start.5 = (s32[64]{0:T(128)S(1)}, s32[64]{0:T(128)}, u32[]{:S(2)}) copy-start(s32[64]{0:T(128)} %param.8) | copy-start | bytes 772
  6.6 17.7 %copy-start = (bf16[4,2,384,384]{3,2,1,0:T(8,128)(2,1)S(1)}, bf16[4,2,384,384]{3,2,1,0:T(8,128)(2,1)}, u32[]{:S(2)}) copy-start(bf16[4,2,384,384]{3,2,1,0:T(8,128)(2,1)} %param.9) | copy-start | bytes 7077892
  7.8 15.6 %all-to-all-start = ((bf16[2,2,128,384]{3,1,0,2:T(2,128)(2,1)}), bf16[2,2,128,384]{3,1,0,2:T(2,128)(2,1)S(1)}, u32[]{:S(2)}, u32[]{:S(2)}) async-start(bf16[2,2,128,384]{3,1,0,2:T(2,128)(2,1)} %copy.130), calls=%async_computation | async-start | bytes 786432 | tf_op jit(solution)/shard_map/all_to_all | solution.py:54
  32.6 3.1 %copy-start.3 = (bf16[4,32,384]{2,1,0:T(8,128)(2,1)}, bf16[4,32,384]{2,1,0:T(8,128)(2,1)S(1)}, u32[]{:S(2)}) copy-start(bf16[4,32,384]{2,1,0:T(8,128)(2,1)S(1)} %fusion.64) | copy-start | bytes 294916
  37.6 2.0 copy-start.1
  37.6 2.0 copy-start.2
  39.7 1.1 copy-start.4
  153.0 34.3 %all-to-all-start.2 = ((bf16[16,2,41472]{2,1,0:T(2,128)(2,1)}), bf16[16,2,41472]{2,1,0:T(2,128)(2,1)S(1)}, u32[]{:S(2)}, u32[]{:S(2)}) async-start(bf16[16,2,41472]{2,1,0:T(2,128)(2,1)} %reshape.488), calls=%async_computation.2 | async-start | bytes 5308416 | tf_op jit(solution)/shard_map/all_to_all | solution.py:109
  213.5 11.4 %all-to-all-start.1 = ((bf16[32,8,384]{2,1,0:T(8,128)(2,1)}), bf16[32,8,384]{2,1,0:T(8,128)(2,1)S(1)}, u32[]{:S(2)}, u32[]{:S(2)}) async-start(bf16[32,8,384]{2,1,0:T(8,128)(2,1)} %copy.137), calls=%async_computation.1 | async-start | bytes 393216 | tf_op jit(solution)/shard_map/all_to_all | solution.py:77
  224.9 27.1 %all-to-all-start.4 = ((f32[16,1,2592]{2,1,0:T(1,128)}), f32[16,1,2592]{2,1,0:T(1,128)S(1)}, u32[]{:S(2)}, u32[]{:S(2)}) async-start(f32[16,1,2592]{2,1,0:T(1,128)} %all_to_all.50), calls=%async_computation.4 | async-start | bytes 344064 | tf_op jit(solution)/shard_map/all_to_all | solution.py:113

commit v11 on v8

--- a/solution.py
+++ b/solution.py
@@ -88,7 +88,6 @@
     z_t = jnp.stack([cos_t * ur - sin_t * ui, cos_t * ui + sin_t * ur], axis=1).astype(jnp.bfloat16)
     w_t = jnp.stack([cos_t * ur + sin_t * ui, cos_t * ui - sin_t * ur], axis=1).astype(jnp.bfloat16)
     y_all = jnp.stack([v_real, v_imag], axis=0).astype(jnp.bfloat16)
-    returned, z_t, w_t, y_all = lax.optimization_barrier((returned, z_t, w_t, y_all))
     taps = z_t.shape[0]
     col_share = channels // freq_devices
     row_share = channels // data_devices
@@ -104,10 +103,11 @@
     z_devices = lax.axis_size("z")
     core_devices = lax.axis_size("c")
     row_pieces = jnp.transpose(
-        col_sum.reshape(taps, z_devices, core_devices, row_share, col_share), (2, 1, 0, 3, 4)
+        col_sum.astype(jnp.bfloat16).reshape(taps, z_devices, core_devices, row_share, col_share),
+        (2, 1, 0, 3, 4),
     )
     row_pieces = lax.all_to_all(row_pieces, "c", split_axis=0, concat_axis=0, tiled=True)
-    row_pieces = jnp.sum(row_pieces, axis=0).astype(jnp.bfloat16)
+    row_pieces = jnp.sum(row_pieces.astype(f32), axis=0).astype(jnp.bfloat16)
     row_pieces = lax.all_to_all(row_pieces, "z", split_axis=0, concat_axis=0, tiled=True)
     tap_grad = jnp.sum(row_pieces.astype(f32), axis=0)
     return (returned, tap_grad)

time: 154 us -> 137 us (0.89)
  blocking collectives: 70.6 us -> 10.3 us
  waiting for transfers between devices: 9.9 us -> 52.5 us
  starting transfers between devices: 11.5 us -> 30.8 us
  local copies, waits for them, and re-layouts: 37.4 us -> 22.8 us
  other arithmetic: 8.96 us -> 6.38 us
  matrix products: 13 us -> 11.4 us
    all_to_all x2 -> x0, blocking collectives: 61.4 us -> none  [the longest x1 34.1 us: local(): lax.all_to_all(col_pieces, 'freq', split_axis=0, concat_axis=0, tiled=True)]
    all_to_all x0 -> x2, waiting for transfers between devices: none -> 40.5 us  [the longest x1 29.4 us: local(): lax.all_to_all(col_pieces, 'freq', split_axis=0, concat_axis=0, tiled=True)]
    all_to_all x0 -> x2, starting transfers between devices: none -> 18.9 us  [the longest x1 14.9 us: local(): lax.all_to_all(row_pieces, 'z', split_axis=0, concat_axis=0, tiled=True)]
    reshape x4 -> x1, local copies, waits for them, and re-layouts: 22.2 us -> 3.99 us  [local(): col_sum.astype(jnp.bfloat16)]
    another operation x0 -> x4, local copies, waits for them, and re-layouts: none -> 3.89 us  [local(): y_all = jnp.stack([v_real, v_imag], axis=0).astype(jnp.bfloat16)]
    unnamed x16 -> x18, local copies, waits for them, and re-layouts: 6.54 us -> 4.26 us
    mul x0 -> x4, local copies, waits for them, and re-layouts: none -> 2.24 us  [the longest x2 1.12 us: local(): cos_t * ur + sin_t * ui]
    all_to_all x1, waiting for transfers between devices: 2.15 us -> 4.25 us  [local(): lax.all_to_all(back_both, 'freq', split_axis=0, concat_axis=1, tiled=True)]
  transfers between devices with their start and end apart: 2 -> 4, of which waited for: 2 -> 4; matrix products, arithmetic and copies ran while one was open for 3% -> 3% of each run, Pallas kernels for 0% -> 0%
where the time goes in v11:
time: 137 us; the launch traced here: 136 us
  waiting for transfers between devices  52.5 us (38%)
  starting transfers between devices  30.8 us (22%)
  local copies, waits for them, and re-layouts  22.8 us (17%)
  matrix products  11.4 us (8%)
  blocking collectives  10.3 us (8%)
  other arithmetic  6.38 us (5%)
  between operations  1.81 us (1%)
    all_to_all x1, waiting for transfers between devices, local(): lax.all_to_all(col_pieces, 'freq', split_axis=0, concat_axis=0, tiled=True)  29.4 us
    all_to_all x1, starting transfers between devices, local(): lax.all_to_all(row_pieces, 'z', split_axis=0, concat_axis=0, tiled=True)  14.9 us
    all_to_all x1, waiting for transfers between devices, local(): lax.all_to_all(row_pieces, 'z', split_axis=0, concat_axis=0, tiled=True)  11.1 us
    all_to_all x1, blocking collectives, local(): lax.all_to_all(row_pieces, 'c', split_axis=0, concat_axis=0, tiled=True)  10.3 us
    all_to_all x1, waiting for transfers between devices, local(): lax.all_to_all(both_spec, 'freq', split_axis=2, concat_axis=1, tiled=True)  7.74 us
    all_to_all x1, starting transfers between devices, local(): lax.all_to_all(both_spec, 'freq', split_axis=2, concat_axis=1, tiled=True)  7.59 us
    dot_general x1, matrix products, local(): jnp.einsum('eibr,teibfc->ftrc', y_all, w_cols, preferred_element_type=f32)  4.44 us
    all_to_all x1, starting transfers between devices, local(): lax.all_to_all(back_both, 'freq', split_axis=0, concat_axis=1, tiled=True)  4.36 us
  transfers between devices with their start and end apart: 4, of which 4 were waited for; matrix products, arithmetic and copies ran while one was open for 3% of the time, Pallas kernels for 0%

profile of v11, /device:TPU:1, one launch (start us, length us, event | category | flops | bytes accessed | tf_op | source)
XLA Modules:
  0.0 136.0 jit_solution(17668139572337699015)
XLA Ops:
  2.1 1.1 fusion.84
  4.4 2.1 %fusion.40 = bf16[1,2,128,384]{3,2,1,0:T(8,128)(2,1)S(1)} fusion(bf16[1024,128,1]{0,1,2:T(8,128)(2,1)S(1)} %reshape.456, bf16[2,384,1024]{2,1,0:T(8,128)(2,1)} %param.5, bf16[2]{0:T(256)(128)(2,1)S(1)} %compare_convert_fusion), kind=kOutput, calls=%fused_computation.38 | convolution fusion | flops 204570624 | bytes 2031620 | tf_op jit(solution)/shard_map/scp,pk->skc/dot_general | solution.py:49
  6.6 1.2 copy.110
  7.8 7.6 %all-to-all-start = ((bf16[2,2,128,384]{3,1,0,2:T(2,128)(2,1)}), bf16[2,2,128,384]{3,1,0,2:T(2,128)(2,1)S(1)}, u32[]{:S(2)}, u32[]{:S(2)}) async-start(bf16[2,2,128,384]{3,1,0,2:T(2,128)(2,1)} %copy.110), calls=%async_computation | async-start | bytes 786432 | tf_op jit(solution)/shard_map/all_to_all | solution.py:54
  15.6 7.7 %all-to-all-done = bf16[2,2,128,384]{3,1,0,2:T(2,128)(2,1)S(1)} async-done(((bf16[2,2,128,384]{3,1,0,2:T(2,128)(2,1)}), bf16[2,2,128,384]{3,1,0,2:T(2,128)(2,1)S(1)}, u32[]{:S(2)}, u32[]{:S(2)}) %all-to-all-start) | async-done | bytes 393248 | tf_op jit(solution)/shard_map/all_to_all | solution.py:54
  28.0 1.3 copy.124
  30.0 1.3 copy.125
  34.3 2.0 %add_convert_fusion = (bf16[9,1,32,4,16,24]{2,5,1,3,4,0:T(8,128)(2,1)S(1)}, bf16[9,1,32,4,16,24]{2,5,1,3,4,0:T(8,128)(2,1)S(1)}) fusion(f32[32,4,16,24]{0,3,1,2:T(8,128)S(1)} %copy.120, f32[9,4]{1,0:T(8,128)S(1)} %get-tuple-element.21, f32[32,4,16,24]{0,3,1,2:T(8,128)S(1)} %copy.119, f32[9,4]{1,0:T(8,128)S(1)} %get-tuple-element.20), kind=kLoop, calls=%fused_computation.5 | loop fusion | flops 3538944 | bytes 2162976 | tf_op jit(solution)/shard_map/convert.12
  36.3 1.1 fusion.8
  37.4 4.4 %fusion.5 = bf16[16,9,384,24]{2,3,0,1:T(8,128)(2,1)S(1)} fusion(f32[16,24,9,384,1,1]{3,1,5,4,0,2:T(8,128)S(1)} %fusion.8, bf16[9,1,32,4,16,24]{2,5,1,3,4,0:T(8,128)(2,1)S(1)} %get-tuple-element.11, bf16[9,1,32,4,16,24]{2,5,1,3,4,0:T(8,128)(2,1)S(1)} %get-tuple-element.10, bf16[1,32,4,384]{3,1,2,0:T(8,128)(2,1)S(1)} %bitcast.148, ...), kind=kOutput, calls=%fused_computation.8 | convolution fusion | flops 684441600 | bytes 9928704 | tf_op jit(solution)/shard_map/eibr,teibfc->ftrc/dot_general | solution.py:97
  41.9 1.8 %copy.126 = bf16[16,9,384,24]{2,3,1,0:T(8,128)(2,1)} copy(bf16[16,9,384,24]{2,3,0,1:T(8,128)(2,1)S(1)} %fusion.5) | data formatting | bytes 5308416 | tf_op jit(solution)/shard_map/convert_element_type | solution.py:100
  43.6 4.0 %all-to-all-start.2 = ((bf16[16,9,384,24]{2,3,1,0:T(8,128)(2,1)}), bf16[16,9,384,24]{2,3,1,0:T(8,128)(2,1)S(1)}, u32[]{:S(2)}, u32[]{:S(2)}) async-start(bf16[16,9,384,24]{2,3,1,0:T(8,128)(2,1)} %copy.126), calls=%async_computation.2 | async-start | bytes 5308416 | tf_op jit(solution)/shard_map/all_to_all | solution.py:101
  48.5 29.4 %all-to-all-done.2 = bf16[16,9,384,24]{2,3,1,0:T(8,128)(2,1)S(1)} async-done(((bf16[16,9,384,24]{2,3,1,0:T(8,128)(2,1)}), bf16[16,9,384,24]{2,3,1,0:T(8,128)(2,1)S(1)}, u32[]{:S(2)}, u32[]{:S(2)}) %all-to-all-start.2) | async-done | bytes 2654240 | tf_op jit(solution)/shard_map/all_to_all | solution.py:101
  78.3 4.0 %reshape.455 = bf16[9,16,2,12,24]{3,2,1,4,0:T(2,128)(2,1)S(1)} reshape(bf16[9,384,24]{1,2,0:T(8,128)(2,1)S(1)} %reduce_sum.33) | data formatting | bytes 331776 | tf_op jit(solution)/shard_map/reshape | solution.py:106
  82.3 2.6 %copy.127 = bf16[2,16,9,12,24]{4,1,3,2,0:T(8,128)(2,1)S(1)} copy(bf16[2,16,9,12,24]{3,0,1,4,2:T(2,128)(2,1)S(1)} %bitcast.139) | data formatting | bytes 331776 | tf_op jit(solution)/shard_map/transpose | solution.py:105
  84.9 1.2 reshape.463
  86.1 10.3 %all_to_all.48 = bf16[2,2,20736]{2,1,0:T(2,128)(2,1)S(1)} all-to-all(bf16[2,2,20736]{2,1,0:T(2,128)(2,1)S(1)} %reshape.463), channel_id=1, replica_groups=mesh['z'=16,'c'=2,'freq'=16] {'c'}, dimensions={0} | all-to-all | bytes 331776 | tf_op jit(solution)/shard_map/all_to_all | solution.py:109
  96.4 4.4 %all-to-all-start.1 = ((bf16[32,8,384]{2,1,0:T(8,128)(2,1)}), bf16[32,8,384]{2,1,0:T(8,128)(2,1)S(1)}, u32[]{:S(2)}, u32[]{:S(2)}) async-start(bf16[32,8,384]{2,1,0:T(8,128)(2,1)} %copy.117), calls=%async_computation.1 | async-start | bytes 393216 | tf_op jit(solution)/shard_map/all_to_all | solution.py:77
  100.8 1.3 reshape.464
  102.4 1.2 reshape.465
  103.6 4.2 %all-to-all-done.1 = bf16[32,8,384]{2,1,0:T(8,128)(2,1)S(1)} async-done(((bf16[32,8,384]{2,1,0:T(8,128)(2,1)}), bf16[32,8,384]{2,1,0:T(8,128)(2,1)S(1)}, u32[]{:S(2)}, u32[]{:S(2)}) %all-to-all-start.1) | async-done | bytes 196640 | tf_op jit(solution)/shard_map/all_to_all | solution.py:77
  107.8 14.9 %all-to-all-start.4 = ((bf16[16,2,1296]{2,1,0:T(2,128)(2,1)}), bf16[16,2,1296]{2,1,0:T(2,128)(2,1)S(1)}, u32[]{:S(2)}, u32[]{:S(2)}) async-start(bf16[16,2,1296]{2,1,0:T(2,128)(2,1)} %reshape.465), calls=%async_computation.4 | async-start | bytes 180224 | tf_op jit(solution)/shard_map/all_to_all | solution.py:111
  123.5 11.1 %all-to-all-done.4 = bf16[16,2,1296]{2,1,0:T(2,128)(2,1)S(1)} async-done(((bf16[16,2,1296]{2,1,0:T(2,128)(2,1)}), bf16[16,2,1296]{2,1,0:T(2,128)(2,1)S(1)}, u32[]{:S(2)}, u32[]{:S(2)}) %all-to-all-start.4) | async-done | bytes 82976 | tf_op jit(solution)/shard_map/all_to_all | solution.py:111
  135.2 0.9 convert_reduce_fusion
  (53 shorter events, 13.2 us)
Async XLA Ops:
  0.6 3.0 %copy-start.6 = (bf16[2,384,1024]{2,1,0:T(8,128)(2,1)S(1)}, bf16[2,384,1024]{2,1,0:T(8,128)(2,1)}, u32[]{:S(2)}) copy-start(bf16[2,384,1024]{2,1,0:T(8,128)(2,1)} %param.6) | copy-start | bytes 4718596
  4.4 11.0 %copy-start.5 = (s32[64]{0:T(128)S(1)}, s32[64]{0:T(128)}, u32[]{:S(2)}) copy-start(s32[64]{0:T(128)} %param.8) | copy-start | bytes 772
  6.6 17.7 %copy-start = (bf16[4,2,384,384]{3,2,1,0:T(8,128)(2,1)S(1)}, bf16[4,2,384,384]{3,2,1,0:T(8,128)(2,1)}, u32[]{:S(2)}) copy-start(bf16[4,2,384,384]{3,2,1,0:T(8,128)(2,1)} %param.9) | copy-start | bytes 7077892
  7.8 15.6 %all-to-all-start = ((bf16[2,2,128,384]{3,1,0,2:T(2,128)(2,1)}), bf16[2,2,128,384]{3,1,0,2:T(2,128)(2,1)S(1)}, u32[]{:S(2)}, u32[]{:S(2)}) async-start(bf16[2,2,128,384]{3,1,0,2:T(2,128)(2,1)} %copy.110), calls=%async_computation | async-start | bytes 786432 | tf_op jit(solution)/shard_map/all_to_all | solution.py:54
  26.1 3.2 %copy-start.3 = (bf16[4,32,384]{2,1,0:T(8,128)(2,1)}, bf16[4,32,384]{2,1,0:T(8,128)(2,1)S(1)}, u32[]{:S(2)}) copy-start(bf16[4,32,384]{2,1,0:T(8,128)(2,1)S(1)} %fusion.61) | copy-start | bytes 294916
  34.2 2.0 %copy-start.1 = (bf16[1,32,4,16,24]{1,4,0,2,3:T(8,128)(2,1)S(1)}, bf16[1,32,4,16,24]{1,4,0,2,3:T(8,128)(2,1)}, u32[]{:S(2)}) copy-start(bf16[1,32,4,16,24]{1,4,0,2,3:T(8,128)(2,1)} %copy.124) | copy-start | bytes 294916
  34.3 2.0 %copy-start.2 = (bf16[1,32,4,16,24]{1,4,0,2,3:T(8,128)(2,1)S(1)}, bf16[1,32,4,16,24]{1,4,0,2,3:T(8,128)(2,1)}, u32[]{:S(2)}) copy-start(bf16[1,32,4,16,24]{1,4,0,2,3:T(8,128)(2,1)} %copy.125) | copy-start | bytes 294916
  36.3 1.1 copy-start.4
  43.6 34.3 %all-to-all-start.2 = ((bf16[16,9,384,24]{2,3,1,0:T(8,128)(2,1)}), bf16[16,9,384,24]{2,3,1,0:T(8,128)(2,1)S(1)}, u32[]{:S(2)}, u32[]{:S(2)}) async-start(bf16[16,9,384,24]{2,3,1,0:T(8,128)(2,1)} %copy.126), calls=%async_computation.2 | async-start | bytes 5308416 | tf_op jit(solution)/shard_map/all_to_all | solution.py:101
  96.4 11.4 %all-to-all-start.1 = ((bf16[32,8,384]{2,1,0:T(8,128)(2,1)}), bf16[32,8,384]{2,1,0:T(8,128)(2,1)S(1)}, u32[]{:S(2)}, u32[]{:S(2)}) async-start(bf16[32,8,384]{2,1,0:T(8,128)(2,1)} %copy.117), calls=%async_computation.1 | async-start | bytes 393216 | tf_op jit(solution)/shard_map/all_to_all | solution.py:77
  107.8 26.7 %all-to-all-start.4 = ((bf16[16,2,1296]{2,1,0:T(2,128)(2,1)}), bf16[16,2,1296]{2,1,0:T(2,128)(2,1)S(1)}, u32[]{:S(2)}, u32[]{:S(2)}) async-start(bf16[16,2,1296]{2,1,0:T(2,128)(2,1)} %reshape.465), calls=%async_computation.4 | async-start | bytes 180224 | tf_op jit(solution)/shard_map/all_to_all | solution.py:111

commit v12 on v11

--- a/solution.py
+++ b/solution.py
@@ -45,10 +45,8 @@
     bins_table = dft_table(bin_order, GRID)
 
     def spectrum(images):
-        masked = images * live_mask[:, None, None]
-        return jnp.einsum(
-            "scp,pk->skc", masked, bins_table, preferred_element_type=jnp.float32
-        ).astype(jnp.bfloat16)
+        full = jnp.einsum("scp,pk->skc", images, bins_table, preferred_element_type=jnp.float32)
+        return (full * live_mask.astype(jnp.float32)[:, None, None]).astype(jnp.bfloat16)
 
     both_spec = jnp.stack([spectrum(output_grad), spectrum(layer_input)], axis=0)
     both_recv = lax.all_to_all(both_spec, "freq", split_axis=2, concat_axis=1, tiled=True)

time: 137 us -> 146 us (1.066)
  local copies, waits for them, and re-layouts: 22.8 us -> 29.3 us
  other arithmetic: 6.38 us -> 9.34 us
    unnamed x18 -> x36, local copies, waits for them, and re-layouts: 4.26 us -> 6.19 us
    mul x2, local copies, waits for them, and re-layouts: 1.12 us -> 2.92 us  [local(): cos_t * ur + sin_t * ui]
    reduce_sum x1, other arithmetic: 0.4 us -> 2.15 us  [local(): col_sum = jnp.sum(col_pieces.astype(f32), axis=0)]
    convert_element_type x2, local copies, waits for them, and re-layouts: 0.37 us -> 2.03 us  [dft_table(): return both_parts.reshape(grid_side * grid_side, -1).astype(jnp.bfloat16)]
    dot_general x2, matrix products: 2.86 us -> 1.3 us  [spectrum(): jnp.einsum('scp,pk->skc', images, bins_table, preferred_element_type=jnp....]
where the time goes in v12:
time: 146 us; the launch traced here: 145 us
  waiting for transfers between devices  52.7 us (36%)
  starting transfers between devices  31.1 us (21%)
  local copies, waits for them, and re-layouts  29.3 us (20%)
  matrix products  10.5 us (7%)
  blocking collectives  10.2 us (7%)
  other arithmetic  9.34 us (6%)
  between operations  1.9 us (1%)
    all_to_all x1, waiting for transfers between devices, local(): lax.all_to_all(col_pieces, 'freq', split_axis=0, concat_axis=0, tiled=True)  29.6 us
    all_to_all x1, starting transfers between devices, local(): lax.all_to_all(row_pieces, 'z', split_axis=0, concat_axis=0, tiled=True)  14.3 us
    all_to_all x1, waiting for transfers between devices, local(): lax.all_to_all(row_pieces, 'z', split_axis=0, concat_axis=0, tiled=True)  11.1 us
    all_to_all x1, blocking collectives, local(): lax.all_to_all(row_pieces, 'c', split_axis=0, concat_axis=0, tiled=True)  10.2 us
    all_to_all x1, waiting for transfers between devices, local(): lax.all_to_all(both_spec, 'freq', split_axis=2, concat_axis=1, tiled=True)  7.74 us
    all_to_all x1, starting transfers between devices, local(): lax.all_to_all(both_spec, 'freq', split_axis=2, concat_axis=1, tiled=True)  7.59 us
    unnamed x36, local copies, waits for them, and re-layouts  6.19 us
    all_to_all x1, starting transfers between devices, local(): lax.all_to_all(col_pieces, 'freq', split_axis=0, concat_axis=0, tiled=True)  4.82 us
  transfers between devices with their start and end apart: 4, of which 4 were waited for; matrix products, arithmetic and copies ran while one was open for 3% of the time, Pallas kernels for 0%

profile of v12, /device:TPU:1, one launch (start us, length us, event | category | flops | bytes accessed | tf_op | source)
XLA Modules:
  0.0 145.0 jit_solution(11108768097180880537)
XLA Ops:
  6.9 1.2 copy.110
  8.0 7.6 %all-to-all-start = ((bf16[2,2,128,384]{3,1,0,2:T(2,128)(2,1)}), bf16[2,2,128,384]{3,1,0,2:T(2,128)(2,1)S(1)}, u32[]{:S(2)}, u32[]{:S(2)}) async-start(bf16[2,2,128,384]{3,1,0,2:T(2,128)(2,1)} %copy.110), calls=%async_computation | async-start | bytes 786432 | tf_op jit(solution)/shard_map/all_to_all | solution.py:52
  15.9 7.7 %all-to-all-done = bf16[2,2,128,384]{3,1,0,2:T(2,128)(2,1)S(1)} async-done(((bf16[2,2,128,384]{3,1,0,2:T(2,128)(2,1)}), bf16[2,2,128,384]{3,1,0,2:T(2,128)(2,1)S(1)}, u32[]{:S(2)}, u32[]{:S(2)}) %all-to-all-start) | async-done | bytes 393248 | tf_op jit(solution)/shard_map/all_to_all | solution.py:52
  29.8 1.3 copy.124
  31.7 1.3 copy.125
  34.1 1.6 %mul.326 = f32[32,4,16,24]{3,2,0,1:T(8,128)S(1)} reshape(f32[32,4,384]{2,0,1:T(8,128)} %fusion.34) | data formatting | bytes 393216 | tf_op jit(solution)/shard_map/mul | solution.py:87
  35.7 1.3 copy.119
  37.1 1.8 %subtract_convert_fusion.1 = (bf16[9,1,32,4,384]{4,2,1,3,0:T(8,128)(2,1)S(1)}, bf16[9,1,32,4,384]{4,2,1,3,0:T(8,128)(2,1)S(1)}) fusion(f32[32,4,384]{2,0,1:T(8,128)} %copy-done.3, f32[9,4]{1,0:T(8,128)S(1)} %get-tuple-element.21, f32[32,4,384]{2,0,1:T(8,128)} %fusion.34, f32[9,4]{1,0:T(8,128)S(1)} %get-tuple-element.20), kind=kLoop, calls=%fused_computation.14 | loop fusion | flops 3538944 | bytes 2162976 | tf_op jit(solution)/shard_map/convert.2
  38.9 2.0 %add_convert_fusion = (bf16[9,1,32,4,16,24]{2,5,1,3,4,0:T(8,128)(2,1)S(1)}, bf16[9,1,32,4,16,24]{2,5,1,3,4,0:T(8,128)(2,1)S(1)}) fusion(f32[32,4,16,24]{0,3,1,2:T(8,128)S(1)} %copy.120, f32[9,4]{1,0:T(8,128)S(1)} %get-tuple-element.21, f32[32,4,16,24]{0,3,1,2:T(8,128)S(1)} %copy-done.2, f32[9,4]{1,0:T(8,128)S(1)} %get-tuple-element.20), kind=kLoop, calls=%fused_computation.5 | loop fusion | flops 3538944 | bytes 2162976 | tf_op jit(solution)/shard_map/convert.12
  42.1 4.4 %fusion.5 = bf16[16,9,384,24]{2,3,0,1:T(8,128)(2,1)S(1)} fusion(f32[16,24,9,384,1,1]{3,1,5,4,0,2:T(8,128)S(1)} %fusion.8, bf16[9,1,32,4,16,24]{2,5,1,3,4,0:T(8,128)(2,1)S(1)} %get-tuple-element.11, bf16[9,1,32,4,16,24]{2,5,1,3,4,0:T(8,128)(2,1)S(1)} %get-tuple-element.10, bf16[1,32,4,384]{3,1,2,0:T(8,128)(2,1)S(1)} %bitcast.150, ...), kind=kOutput, calls=%fused_computation.8 | convolution fusion | flops 684441600 | bytes 9928704 | tf_op jit(solution)/shard_map/eibr,teibfc->ftrc/dot_general | solution.py:95
  46.5 1.8 %copy.126 = bf16[16,9,384,24]{2,3,1,0:T(8,128)(2,1)} copy(bf16[16,9,384,24]{2,3,0,1:T(8,128)(2,1)S(1)} %fusion.5) | data formatting | bytes 5308416 | tf_op jit(solution)/shard_map/convert_element_type | solution.py:98
  48.3 4.8 %all-to-all-start.2 = ((bf16[16,9,384,24]{2,3,1,0:T(8,128)(2,1)}), bf16[16,9,384,24]{2,3,1,0:T(8,128)(2,1)}, u32[]{:S(2)}, u32[]{:S(2)}) async-start(bf16[16,9,384,24]{2,3,1,0:T(8,128)(2,1)} %copy.126), calls=%async_computation.2 | async-start | bytes 5308416 | tf_op jit(solution)/shard_map/all_to_all | solution.py:99
  54.1 29.6 %all-to-all-done.2 = bf16[16,9,384,24]{2,3,1,0:T(8,128)(2,1)} async-done(((bf16[16,9,384,24]{2,3,1,0:T(8,128)(2,1)}), bf16[16,9,384,24]{2,3,1,0:T(8,128)(2,1)}, u32[]{:S(2)}, u32[]{:S(2)}) %all-to-all-start.2) | async-done | bytes 2654240 | tf_op jit(solution)/shard_map/all_to_all | solution.py:99
  83.7 2.2 %reduce_sum.33 = bf16[9,384,24]{1,2,0:T(8,128)(2,1)S(1)} reduce(bf16[16,9,384,24]{2,3,1,0:T(8,128)(2,1)} %all-to-all-done.2, bf16[]{:T(256)} %constant.123.clone.1), dimensions={0}, to_apply=%region_0.1 | reduce | flops 1244160 | bytes 2820098 | tf_op jit(solution)/shard_map/reduce_sum | solution.py:100
  85.8 4.0 %reshape.456 = bf16[9,16,2,12,24]{3,2,1,4,0:T(2,128)(2,1)S(1)} reshape(bf16[9,384,24]{1,2,0:T(8,128)(2,1)S(1)} %reduce_sum.33) | data formatting | bytes 331776 | tf_op jit(solution)/shard_map/reshape | solution.py:104
  89.8 3.7 %copy.127 = bf16[2,16,9,12,24]{4,1,3,2,0:T(8,128)(2,1)} copy(bf16[2,16,9,12,24]{3,0,1,4,2:T(2,128)(2,1)S(1)} %bitcast.141) | data formatting | bytes 331776 | tf_op jit(solution)/shard_map/transpose | solution.py:103
  93.6 2.3 %reshape.464 = bf16[2,2,20736]{2,1,0:T(2,128)(2,1)S(1)} reshape(bf16[2,9,12,16,24]{4,3,2,1,0:T(8,128)(2,1)} %bitcast.143) | data formatting | bytes 331776
  95.8 10.2 %all_to_all.48 = bf16[2,2,20736]{2,1,0:T(2,128)(2,1)S(1)} all-to-all(bf16[2,2,20736]{2,1,0:T(2,128)(2,1)S(1)} %reshape.464), channel_id=1, replica_groups=mesh['z'=16,'c'=2,'freq'=16] {'c'}, dimensions={0} | all-to-all | bytes 331776 | tf_op jit(solution)/shard_map/all_to_all | solution.py:107
  106.0 4.4 %all-to-all-start.1 = ((bf16[32,8,384]{2,1,0:T(8,128)(2,1)}), bf16[32,8,384]{2,1,0:T(8,128)(2,1)S(1)}, u32[]{:S(2)}, u32[]{:S(2)}) async-start(bf16[32,8,384]{2,1,0:T(8,128)(2,1)} %copy.117), calls=%async_computation.1 | async-start | bytes 393216 | tf_op jit(solution)/shard_map/all_to_all | solution.py:75
  110.4 1.3 reshape.465
  112.0 1.2 reshape.466
  113.2 4.2 %all-to-all-done.1 = bf16[32,8,384]{2,1,0:T(8,128)(2,1)S(1)} async-done(((bf16[32,8,384]{2,1,0:T(8,128)(2,1)}), bf16[32,8,384]{2,1,0:T(8,128)(2,1)S(1)}, u32[]{:S(2)}, u32[]{:S(2)}) %all-to-all-start.1) | async-done | bytes 196640 | tf_op jit(solution)/shard_map/all_to_all | solution.py:75
  117.4 14.3 %all-to-all-start.4 = ((bf16[16,2,1296]{2,1,0:T(2,128)(2,1)}), bf16[16,2,1296]{2,1,0:T(2,128)(2,1)S(1)}, u32[]{:S(2)}, u32[]{:S(2)}) async-start(bf16[16,2,1296]{2,1,0:T(2,128)(2,1)} %reshape.466), calls=%async_computation.4 | async-start | bytes 180224 | tf_op jit(solution)/shard_map/all_to_all | solution.py:109
  132.4 11.1 %all-to-all-done.4 = bf16[16,2,1296]{2,1,0:T(2,128)(2,1)S(1)} async-done(((bf16[16,2,1296]{2,1,0:T(2,128)(2,1)}), bf16[16,2,1296]{2,1,0:T(2,128)(2,1)S(1)}, u32[]{:S(2)}, u32[]{:S(2)}) %all-to-all-start.4) | async-done | bytes 82976 | tf_op jit(solution)/shard_map/all_to_all | solution.py:109
  (71 shorter events, 17.9 us)
Async XLA Ops:
  0.6 4.8 %copy-start = (bf16[2,384,1024]{2,1,0:T(8,128)(2,1)S(1)}, bf16[2,384,1024]{2,1,0:T(8,128)(2,1)}, u32[]{:S(2)}) copy-start(bf16[2,384,1024]{2,1,0:T(8,128)(2,1)} %param.6) | copy-start | bytes 4718596
  0.6 5.5 %copy-start.10 = (bf16[2,384,1024]{2,1,0:T(8,128)(2,1)S(1)}, bf16[2,384,1024]{2,1,0:T(8,128)(2,1)}, u32[]{:S(2)}) copy-start(bf16[2,384,1024]{2,1,0:T(8,128)(2,1)} %param.5) | copy-start | bytes 4718596
  6.1 9.5 %copy-start.15 = (s32[64]{0:T(128)S(1)}, s32[64]{0:T(128)}, u32[]{:S(2)}) copy-start(s32[64]{0:T(128)} %param.8) | copy-start | bytes 772
  8.0 15.6 %all-to-all-start = ((bf16[2,2,128,384]{3,1,0,2:T(2,128)(2,1)}), bf16[2,2,128,384]{3,1,0,2:T(2,128)(2,1)S(1)}, u32[]{:S(2)}, u32[]{:S(2)}) async-start(bf16[2,2,128,384]{3,1,0,2:T(2,128)(2,1)} %copy.110), calls=%async_computation | async-start | bytes 786432 | tf_op jit(solution)/shard_map/all_to_all | solution.py:52
  23.6 1.7 %copy-start.1 = (bf16[4,2,384,384]{3,2,1,0:T(8,128)(2,1)S(1)}, bf16[4,2,384,384]{3,2,1,0:T(8,128)(2,1)}, u32[]{:S(2)}) copy-start(bf16[4,2,384,384]{3,2,1,0:T(8,128)(2,1)} %param.9) | copy-start | bytes 7077892
  24.5 3.3 %copy-start.8 = (bf16[1,32,4,1,384]{4,0,3,2,1:T(2,128)(2,1)}, bf16[1,32,4,1,384]{4,0,3,2,1:T(2,128)(2,1)S(1)}, u32[]{:S(2)}) copy-start(bf16[1,32,4,1,384]{4,0,3,2,1:T(2,128)(2,1)S(1)} %get-tuple-element.17) | copy-start | bytes 294916
  24.5 4.3 %copy-start.6 = (bf16[1,32,4,1,384]{4,0,3,2,1:T(2,128)(2,1)}, bf16[1,32,4,1,384]{4,0,3,2,1:T(2,128)(2,1)S(1)}, u32[]{:S(2)}) copy-start(bf16[1,32,4,1,384]{4,0,3,2,1:T(2,128)(2,1)S(1)} %get-tuple-element.16) | copy-start | bytes 294916
  27.2 3.9 %copy-start.13 = (bf16[4,32,384]{2,1,0:T(8,128)(2,1)}, bf16[4,32,384]{2,1,0:T(8,128)(2,1)S(1)}, u32[]{:S(2)}) copy-start(bf16[4,32,384]{2,1,0:T(8,128)(2,1)S(1)} %fusion.49) | copy-start | bytes 294916
  29.1 3.9 %copy-start.3 = (f32[32,4,384]{2,0,1:T(8,128)}, f32[32,4,384]{2,0,1:T(8,128)S(1)}, u32[]{:S(2)}) copy-start(f32[32,4,384]{2,0,1:T(8,128)S(1)} %fusion.40) | copy-start | bytes 589828
  37.1 1.8 %copy-start.2 = (f32[32,4,16,24]{0,3,1,2:T(8,128)S(1)}, f32[32,4,16,24]{0,3,1,2:T(8,128)}, u32[]{:S(2)}) copy-start(f32[32,4,16,24]{0,3,1,2:T(8,128)} %copy.119) | copy-start | bytes 589828
  38.9 2.0 %copy-start.11 = (bf16[1,32,4,16,24]{1,4,0,2,3:T(8,128)(2,1)S(1)}, bf16[1,32,4,16,24]{1,4,0,2,3:T(8,128)(2,1)}, u32[]{:S(2)}) copy-start(bf16[1,32,4,16,24]{1,4,0,2,3:T(8,128)(2,1)} %copy.124) | copy-start | bytes 294916
  38.9 2.0 %copy-start.12 = (bf16[1,32,4,16,24]{1,4,0,2,3:T(8,128)(2,1)S(1)}, bf16[1,32,4,16,24]{1,4,0,2,3:T(8,128)(2,1)}, u32[]{:S(2)}) copy-start(bf16[1,32,4,16,24]{1,4,0,2,3:T(8,128)(2,1)} %copy.125) | copy-start | bytes 294916
  41.0 1.1 copy-start.14
  48.3 4.8 %copy-start.5 = (f32[32,4,384]{2,0,1:T(8,128)S(1)}, f32[32,4,384]{2,0,1:T(8,128)}, u32[]{:S(2)}) copy-start(f32[32,4,384]{2,0,1:T(8,128)} %fusion.34) | copy-start | bytes 589828
  48.3 4.9 %copy-start.9 = (bf16[1,32,4,1,384]{4,0,3,2,1:T(2,128)(2,1)S(1)}, bf16[1,32,4,1,384]{4,0,3,2,1:T(2,128)(2,1)}, u32[]{:S(2)}) copy-start(bf16[1,32,4,1,384]{4,0,3,2,1:T(2,128)(2,1)} %copy-done.8) | copy-start | bytes 294916
  48.3 4.9 %copy-start.4 = (f32[32,4,384]{2,0,1:T(8,128)S(1)}, f32[32,4,384]{2,0,1:T(8,128)}, u32[]{:S(2)}) copy-start(f32[32,4,384]{2,0,1:T(8,128)} %copy-done.3) | copy-start | bytes 589828
  48.3 4.9 %copy-start.7 = (bf16[1,32,4,1,384]{4,0,3,2,1:T(2,128)(2,1)S(1)}, bf16[1,32,4,1,384]{4,0,3,2,1:T(2,128)(2,1)}, u32[]{:S(2)}) copy-start(bf16[1,32,4,1,384]{4,0,3,2,1:T(2,128)(2,1)} %copy-done.6) | copy-start | bytes 294916
  48.3 35.3 %all-to-all-start.2 = ((bf16[16,9,384,24]{2,3,1,0:T(8,128)(2,1)}), bf16[16,9,384,24]{2,3,1,0:T(8,128)(2,1)}, u32[]{:S(2)}, u32[]{:S(2)}) async-start(bf16[16,9,384,24]{2,3,1,0:T(8,128)(2,1)} %copy.126), calls=%async_computation.2 | async-start | bytes 5308416 | tf_op jit(solution)/shard_map/all_to_all | solution.py:99
  106.0 11.4 %all-to-all-start.1 = ((bf16[32,8,384]{2,1,0:T(8,128)(2,1)}), bf16[32,8,384]{2,1,0:T(8,128)(2,1)S(1)}, u32[]{:S(2)}, u32[]{:S(2)}) async-start(bf16[32,8,384]{2,1,0:T(8,128)(2,1)} %copy.117), calls=%async_computation.1 | async-start | bytes 393216 | tf_op jit(solution)/shard_map/all_to_all | solution.py:75
  117.4 26.1 %all-to-all-start.4 = ((bf16[16,2,1296]{2,1,0:T(2,128)(2,1)}), bf16[16,2,1296]{2,1,0:T(2,128)(2,1)S(1)}, u32[]{:S(2)}, u32[]{:S(2)}) async-start(bf16[16,2,1296]{2,1,0:T(2,128)(2,1)} %reshape.466), calls=%async_computation.4 | async-start | bytes 180224 | tf_op jit(solution)/shard_map/all_to_all | solution.py:109
